TPU v7x, 256 devices: a whole 4x4x8 slice. The times are simulated.
256 devices in a mesh: pos: 16 (over x_hi, z), exp: 16 (over y, x_lo, core).
Axes of the slice: x: 4 (x_hi: 2, x_lo: 2; x = x_hi * 2 + x_lo), y: 4, z: 8, core: 2. Of those that a mesh axis runs over, the one named last changes fastest.
Arguments:
- patches: bfloat16 [65536, 4, 256], P(('pos', 'exp')), may hold values from -6 to 6
- conv_weight: bfloat16 [3, 256, 2048], replicated, may hold values from -0.21875 to 0.21875
- phi: bfloat16 [2048, 128], replicated, may hold values from -40 to 40, as said below
- w_in: bfloat16 [16, 2048, 8192], P('exp', None, 'pos'), may hold values from -0.125 to 0.125
- w_out: bfloat16 [16, 8192, 2048], P('exp', 'pos'), may hold values from -0.0625 to 0.0625
Outputs:
- mixed: bfloat16 [65536, 4, 2048], P(('pos', 'exp'))
Inputs may be any that keep to these rules, and one draw needn't show every extreme that they name: phi is real-valued.
All inputs are finite; a program needn't handle non-finite values.
Results may differ from a plain program's by a relative error of at most 0.019.
The roundings to bfloat16 on the way count: a program that leaves them out, or rounds other values in their place, can miss the bound.
Values may be sent and summed in bfloat16 or wider, within the bound.
No kernel may reach another device: no remote copies, remote signals or barrier semaphores. Data moves between devices by JAX's collectives and lax.ppermute only.
A program may use at most 128 MiB of HBM per device.

v0:
```python
import jax
import jax.numpy as jnp
from jax import lax
from jax.sharding import PartitionSpec as P

D = 2048
SLOTS_PER = 8


def with_halo(array, sides, width):
    for axis, dim in sides:
        count, length = (lax.axis_size(axis), array.shape[dim])
        up = [(i, (i + 1) % count) for i in range(count - 1)]
        down = [(j, i) for i, j in up]
        last = lax.slice_in_dim(array, length - width, length, axis=dim)
        initial = lax.slice_in_dim(array, 0, width, axis=dim)
        before = lax.ppermute(last, axis, up)
        after = lax.ppermute(initial, axis, down)
        array = jnp.concatenate([before, array, after], axis=dim)
    return array


def per_device(patches, conv_weight, phi, w_in, w_out):
    channels, periods, samples = patches.shape
    padded = with_halo(patches, ((("pos", "exp"), 0),), 1)
    running = jnp.zeros((channels * periods, D), jnp.float32)
    for offset in range(3):
        window = padded[offset : offset + channels].reshape(channels * periods, samples)
        running = running + jnp.dot(window, conv_weight[offset], preferred_element_type=jnp.float32)
    flat = running.astype(jnp.bfloat16)
    logits = jnp.dot(flat, phi, preferred_element_type=jnp.float32)
    local_peak = jnp.max(logits, axis=0)
    column_peak = lax.pmax(local_peak, ("pos", "exp"))
    raw_weights = jnp.exp(logits - column_peak)
    column_total = lax.psum(jnp.sum(raw_weights, axis=0), ("pos", "exp"))
    dispatch = (raw_weights / column_total).astype(jnp.bfloat16)
    group = lax.axis_index("exp")
    every_slot = lax.dot_general(
        dispatch, flat, (((0,), (0,)), ((), ())), preferred_element_type=jnp.float32
    )
    summed = lax.psum(every_slot, ("pos", "exp"))
    owned = lax.dynamic_slice_in_dim(summed, group * SLOTS_PER, SLOTS_PER, 0)
    slot_in = owned.astype(jnp.bfloat16)
    hidden = jax.nn.gelu(
        jnp.dot(slot_in, w_in[0], preferred_element_type=jnp.float32), approximate=True
    ).astype(jnp.bfloat16)
    expert_term = jnp.dot(hidden, w_out[0], preferred_element_type=jnp.float32)
    slot_out = lax.psum(expert_term, "pos").astype(jnp.bfloat16)
    row_peak = jnp.max(logits, axis=1, keepdims=True)
    row_weights = jnp.exp(logits - row_peak)
    combine = (row_weights / jnp.sum(row_weights, axis=1, keepdims=True)).astype(jnp.bfloat16)
    mixed = jnp.dot(
        combine,
        lax.all_gather(slot_out, "exp", axis=0, tiled=True),
        preferred_element_type=jnp.float32,
    )
    return mixed.astype(jnp.bfloat16).reshape(channels, periods, D)


def solution(mesh):
    in_specs = (
        P(("pos", "exp"), None, None),
        P(),
        P(),
        P("exp", None, "pos"),
        P("exp", "pos", None),
    )
    out_specs = P(("pos", "exp"), None, None)
    return jax.shard_map(
        per_device, mesh=mesh, in_specs=in_specs, out_specs=out_specs, check_vma=False
    )
```

profile of v0, /device:TPU:1, one launch (start us, length us, event | category | flops | bytes accessed | tf_op | source)
XLA Modules:
  0.0 376.0 jit_solution(2195007920341952127)
XLA Ops:
  0.0 0.0 copy-start
  0.0 0.9 fusion.47
  0.9 4.5 %collective-permute-start = (bf16[1,4,256]{2,1,0:T(4,128)(2,1)S(1)}, bf16[1,4,256]{2,1,0:T(4,128)(2,1)S(1)}, u32[]{:S(2)}, u32[]{:S(2)}) collective-permute-start(bf16[1,4,256]{2,1,0:T(4,128)(2,1)S(1)} %get-tuple-element.12), channel_id=1, source_target_pairs={{0,1},{1,2},{2,3},{3,4},{4,5},{5,6},{6,7},{7,8},{8,9},{9,10},{10,1... | collective-permute-start | bytes 6152 | tf_op jit(solution)/shard_map/ppermute | solution.py:17
  5.3 1.9 collective-permute-start.1
  7.3 1.2 reshape.17
  8.4 0.0 copy-start.2
  8.5 5.8 %fusion.8 = f32[1024,2048]{1,0:T(8,128)} fusion(bf16[1024,256]{1,0:T(8,128)(2,1)S(1)} %reshape.17, bf16[3,256,2048]{2,1,0:T(8,128)(2,1)} %param.6), kind=kOutput, calls=%fused_computation.8 | convolution fusion | flops 1073741824 | bytes 9961472 | tf_op jit(solution)/shard_map/dot_general | solution.py:29
  14.2 0.0 collective-permute-done
  14.2 0.0 collective-permute-done.1
  14.2 0.0 copy-done.2
  14.2 1.3 pad_maximum_fusion
  15.6 1.2 reshape.16
  16.7 0.0 copy-start.3
  16.8 5.8 %fusion.10 = f32[1024,2048]{1,0:T(8,128)} fusion(bf16[1024,256]{1,0:T(8,128)(2,1)S(1)} %reshape.16, bf16[3,256,2048]{2,1,0:T(8,128)(2,1)} %param.6), kind=kOutput, calls=%fused_computation.10 | convolution fusion | flops 1073741824 | bytes 9961472 | tf_op jit(solution)/shard_map/dot_general | solution.py:29
  22.5 0.0 copy-done.3
  22.5 0.1 reshape.18
  22.6 0.0 copy-start.4
  22.7 7.4 %add_convert_fusion = bf16[1024,2048]{1,0:T(8,128)(2,1)S(1)} fusion(f32[1024,2048]{1,0:T(8,128)} %fusion.10, f32[1024,2048]{1,0:T(8,128)} %fusion.8, bf16[1024,256]{1,0:T(8,128)(2,1)S(1)} %reshape.18, bf16[3,256,2048]{2,1,0:T(8,128)(2,1)} %param.6), kind=kOutput, calls=%fused_computation | convolution fusion | flops 1080033280 | bytes 22544384 | tf_op jit(solution)/shard_map/dot_general | solution.py:29
  30.0 0.0 copy-start.1
  30.1 2.0 copy-done.1
  32.1 0.0 copy-done.4
  32.1 1.3 fusion.46
  33.4 80.7 %pmax.7 = f32[128]{0:T(128)S(1)} all-reduce(f32[128]{0:T(128)S(1)} %get-tuple-element.8), channel_id=1, replica_groups=mesh['pos'=16,'exp'=16] {'pos','exp'}, use_global_device_ids=true, to_apply=%region_3.0 | all-reduce | flops 128 | bytes 1024 | tf_op jit(solution)/shard_map/pmax | solution.py:33
  114.1 0.4 fusion.15
  114.5 72.9 %psum.21 = f32[128]{0:T(128)S(1)} all-reduce(f32[128]{0:T(128)S(1)} %get-tuple-element.6), channel_id=1, replica_groups=mesh['pos'=16,'exp'=16] {'pos','exp'}, use_global_device_ids=true, to_apply=%region_5.0 | all-reduce | flops 128 | bytes 1024 | tf_op jit(solution)/shard_map/psum | solution.py:35
  187.4 3.9 %fusion.17 = f32[128,2048]{1,0:T(8,128)} fusion(bf16[1024,2048]{1,0:T(8,128)(2,1)} %copy-done.1, f32[1024,128]{1,0:T(8,128)S(1)} %get-tuple-element.13, f32[128]{0:T(128)S(1)} %psum.21, f32[128]{0:T(128)S(1)} %pmax.7), kind=kOutput, calls=%fused_computation.23 | convolution fusion | flops 537264128 | bytes 5768192 | tf_op jit(solution)/shard_map/dot_general | solution.py:38
  191.3 78.0 %all-reduce.1 = bf16[128,2048]{1,0:T(8,128)(2,1)S(1)} all-reduce(f32[128,2048]{1,0:T(8,128)} %fusion.17), channel_id=1, replica_groups=mesh['pos'=16,'exp'=16] {'pos','exp'}, use_global_device_ids=true, to_apply=%region_6.0 | all-reduce | flops 262144 | bytes 1572864 | tf_op jit(solution)/shard_map/psum | solution.py:41
  269.4 0.0 copy-done
  269.4 2.3 fusion
  271.7 62.1 %psum.23 = bf16[8,2048]{1,0:T(8,128)(2,1)S(1)} all-reduce(f32[8,2048]{1,0:T(8,128)S(1)} %fusion), channel_id=1, replica_groups=mesh['pos'=16,'exp'=16] {'pos'}, use_global_device_ids=true, to_apply=%region_7.0 | all-reduce | flops 16384 | bytes 98304 | tf_op jit(solution)/shard_map/psum | solution.py:48
  333.8 31.7 %all_gather.3 = bf16[128,2048]{1,0:T(8,128)(2,1)S(1)} all-gather(bf16[8,2048]{1,0:T(8,128)(2,1)S(1)} %psum.23), channel_id=1, replica_groups=mesh['pos'=16,'exp'=16] {'exp'}, dimensions={0}, use_global_device_ids=true | all-gather | bytes 557056 | tf_op jit(solution)/shard_map/all_gather | solution.py:54
  365.6 3.3 convolution_convert_fusion
  368.8 7.2 %reshape.19 = bf16[256,4,2048]{2,1,0:T(4,128)(2,1)} reshape(bf16[1024,2048]{1,0:T(8,128)(2,1)} %convolution_convert_fusion) | data formatting | bytes 8388608 | tf_op jit(solution)/shard_map/reshape | solution.py:57
Async XLA Ops:
  0.0 269.4 %copy-start = (bf16[1,512,2048]{2,1,0:T(8,128)(2,1)S(1)}, bf16[1,512,2048]{2,1,0:T(8,128)(2,1)}, u32[]{:S(2)}) copy-start(bf16[1,512,2048]{2,1,0:T(8,128)(2,1)} %param.9) | copy-start | bytes 6291460
  0.9 13.4 %collective-permute-start = (bf16[1,4,256]{2,1,0:T(4,128)(2,1)S(1)}, bf16[1,4,256]{2,1,0:T(4,128)(2,1)S(1)}, u32[]{:S(2)}, u32[]{:S(2)}) collective-permute-start(bf16[1,4,256]{2,1,0:T(4,128)(2,1)S(1)} %get-tuple-element.12), channel_id=1, source_target_pairs={{0,1},{1,2},{2,3},{3,4},{4,5},{5,6},{6,7},{7,8},{8,9},{9,10},{10,1... | collective-permute-start | bytes 6152 | tf_op jit(solution)/shard_map/ppermute | solution.py:17
  5.3 8.9 %collective-permute-start.1 = (bf16[1,4,256]{2,1,0:T(4,128)(2,1)S(1)}, bf16[1,4,256]{2,1,0:T(4,128)(2,1)S(1)}, u32[]{:S(2)}, u32[]{:S(2)}) collective-permute-start(bf16[1,4,256]{2,1,0:T(4,128)(2,1)S(1)} %get-tuple-element.11), channel_id=1, source_target_pairs={{1,0},{2,1},{3,2},{4,3},{5,4},{6,5},{7,6},{8,7},{9,8},{10,9},{11,1... | collective-permute-start | bytes 6152 | tf_op jit(solution)/shard_map/ppermute | solution.py:18
  8.4 5.8 %copy-start.2 = (bf16[256,4,256]{2,1,0:T(4,128)(2,1)S(1)}, bf16[256,4,256]{2,1,0:T(4,128)(2,1)}, u32[]{:S(2)}) copy-start(bf16[256,4,256]{2,1,0:T(4,128)(2,1)} %param.5) | copy-start | bytes 1572868
  16.7 5.8 %copy-start.3 = (bf16[256,4,256]{2,1,0:T(4,128)(2,1)S(1)}, bf16[256,4,256]{2,1,0:T(4,128)(2,1)}, u32[]{:S(2)}) copy-start(bf16[256,4,256]{2,1,0:T(4,128)(2,1)} %get-tuple-element.9) | copy-start | bytes 1572868
  22.6 9.4 %copy-start.4 = (bf16[2048,128]{1,0:T(8,128)(2,1)S(1)}, bf16[2048,128]{1,0:T(8,128)(2,1)}, u32[]{:S(2)}) copy-start(bf16[2048,128]{1,0:T(8,128)(2,1)} %param.7) | copy-start | bytes 1572868
  30.0 2.0 copy-start.1
where the time goes:
time: 377 us; the launch traced here: 376 us
  blocking collectives  326 us (86%)
  matrix products  29.8 us (8%)
  local copies, waits for them, and re-layouts  12.5 us (3%)
  starting transfers between devices  6.41 us (2%)
    pmax x1, blocking collectives, per_device(): column_peak = lax.pmax(local_peak, ('pos', 'exp'))  80.7 us
    psum x1, blocking collectives, per_device(): summed = lax.psum(every_slot, ('pos', 'exp'))  78 us
    psum x1, blocking collectives, per_device(): column_total = lax.psum(jnp.sum(raw_weights, axis=0), ('pos', 'exp'))  72.9 us
    psum x1, blocking collectives, per_device(): slot_out = lax.psum(expert_term, 'pos').astype(jnp.bfloat16)  62.1 us
    all_gather x1, blocking collectives, per_device(): lax.all_gather(slot_out, 'exp', axis=0, tiled=True)  31.7 us
    dot_general x3, matrix products, per_device(): jnp.dot(window, conv_weight[offset], preferred_element_type=jnp.float32)  18.9 us
  transfers between devices with their start and end apart: 2, of which 0 were waited for; matrix products, arithmetic and copies ran while one was open for 2% of the time, Pallas kernels for 0%

commit v1 on v0

--- a/solution.py
+++ b/solution.py
@@ -20,32 +20,55 @@
     return array
 
 
+def butterfly_sum(value, axis):
+    count = lax.axis_size(axis)
+    step = 1
+    while step < count:
+        pairs = [(i, i ^ step) for i in range(count)]
+        value = value + lax.ppermute(value, axis, pairs)
+        step *= 2
+    return value
+
+
+def gather_rows(row, axes):
+    count = lax.axis_size(axes)
+    tiled = jnp.broadcast_to(row[None, :], (count, row.shape[0]))
+    return lax.all_to_all(tiled, axes, 0, 0, tiled=True)
+
+
 def per_device(patches, conv_weight, phi, w_in, w_out):
     channels, periods, samples = patches.shape
-    padded = with_halo(patches, ((("pos", "exp"), 0),), 1)
+    every = ("pos", "exp")
+    padded = with_halo(patches, ((every, 0),), 1)
     running = jnp.zeros((channels * periods, D), jnp.float32)
     for offset in range(3):
         window = padded[offset : offset + channels].reshape(channels * periods, samples)
         running = running + jnp.dot(window, conv_weight[offset], preferred_element_type=jnp.float32)
     flat = running.astype(jnp.bfloat16)
     logits = jnp.dot(flat, phi, preferred_element_type=jnp.float32)
+    slots = logits.shape[1]
+
     local_peak = jnp.max(logits, axis=0)
-    column_peak = lax.pmax(local_peak, ("pos", "exp"))
+    local_total = jnp.sum(jnp.exp(logits - local_peak), axis=0)
+    stats = gather_rows(jnp.concatenate([local_peak, local_total]), every)
+    peaks, totals = stats[:, :slots], stats[:, slots:]
+    column_peak = jnp.max(peaks, axis=0)
+    column_total = jnp.sum(totals * jnp.exp(peaks - column_peak), axis=0)
+
     raw_weights = jnp.exp(logits - column_peak)
-    column_total = lax.psum(jnp.sum(raw_weights, axis=0), ("pos", "exp"))
     dispatch = (raw_weights / column_total).astype(jnp.bfloat16)
-    group = lax.axis_index("exp")
     every_slot = lax.dot_general(
         dispatch, flat, (((0,), (0,)), ((), ())), preferred_element_type=jnp.float32
     )
-    summed = lax.psum(every_slot, ("pos", "exp"))
-    owned = lax.dynamic_slice_in_dim(summed, group * SLOTS_PER, SLOTS_PER, 0)
-    slot_in = owned.astype(jnp.bfloat16)
+    groups = lax.axis_size("exp")
+    mine = lax.all_to_all(every_slot, "exp", 0, 0, tiled=True)
+    owned = jnp.sum(mine.reshape(groups, SLOTS_PER, D), axis=0)
+    slot_in = butterfly_sum(owned, "pos").astype(jnp.bfloat16)
     hidden = jax.nn.gelu(
         jnp.dot(slot_in, w_in[0], preferred_element_type=jnp.float32), approximate=True
     ).astype(jnp.bfloat16)
     expert_term = jnp.dot(hidden, w_out[0], preferred_element_type=jnp.float32)
-    slot_out = lax.psum(expert_term, "pos").astype(jnp.bfloat16)
+    slot_out = butterfly_sum(expert_term, "pos").astype(jnp.bfloat16)
     row_peak = jnp.max(logits, axis=1, keepdims=True)
     row_weights = jnp.exp(logits - row_peak)
     combine = (row_weights / jnp.sum(row_weights, axis=1, keepdims=True)).astype(jnp.bfloat16)

time: 377 us -> 162 us (0.43)
  blocking collectives: 326 us -> 80.7 us
  waiting for transfers between devices: 0.01 us -> 33.8 us
  matrix products: 29.8 us -> 18.8 us
  starting transfers between devices: 6.41 us -> 13.4 us
    psum x3 -> x0, blocking collectives: 213 us -> none  [the longest x1 78 us: per_device(): summed = lax.psum(every_slot, ('pos', 'exp'))]
    pmax x1 -> x0, blocking collectives: 80.7 us -> none  [per_device(): column_peak = lax.pmax(local_peak, ('pos', 'exp'))]
    all_to_all x0 -> x2, blocking collectives: none -> 50.6 us  [the longest x1 31.6 us: gather_rows(): return lax.all_to_all(tiled, axes, 0, 0, tiled=True)]
    ppermute x0 -> x8, waiting for transfers between devices: none -> 33.8 us  [butterfly_sum(): value = value + lax.ppermute(value, axis, pairs)]
    dot_general x3, matrix products: 18.9 us -> 11.1 us  [per_device(): jnp.dot(window, conv_weight[offset], preferred_element_type=jnp.float32)]
    ppermute x0 -> x8, starting transfers between devices: none -> 6.42 us  [butterfly_sum(): value = value + lax.ppermute(value, axis, pairs)]
  transfers between devices with their start and end apart: 2 -> 10, of which waited for: 0 -> 8; matrix products, arithmetic and copies ran while one was open for 2% -> 4% of each run, Pallas kernels for 0% -> 0%
where the time goes in v1:
time: 162 us
  blocking collectives  80.7 us (50%)
  waiting for transfers between devices  33.8 us (21%)
  matrix products  18.8 us (12%)
  starting transfers between devices  13.4 us (8%)
  local copies, waits for them, and re-layouts  11.7 us (7%)
  other arithmetic  3 us (2%)
    ppermute x8, waiting for transfers between devices, butterfly_sum(): value = value + lax.ppermute(value, axis, pairs)  33.8 us
    all_to_all x1, blocking collectives, gather_rows(): return lax.all_to_all(tiled, axes, 0, 0, tiled=True)  31.6 us
    all_gather x1, blocking collectives, per_device(): lax.all_gather(slot_out, 'exp', axis=0, tiled=True)  30.1 us
    all_to_all x1, blocking collectives, per_device(): mine = lax.all_to_all(every_slot, 'exp', 0, 0, tiled=True)  18.9 us
    dot_general x3, matrix products, per_device(): jnp.dot(window, conv_weight[offset], preferred_element_type=jnp.float32)  11.1 us
    reshape x1, local copies, waits for them, and re-layouts, per_device(): return mixed.astype(jnp.bfloat16).reshape(channels, periods, D)  7.16 us
    ppermute x8, starting transfers between devices, butterfly_sum(): value = value + lax.ppermute(value, axis, pairs)  6.42 us
    ppermute x1, starting transfers between devices, with_halo(): after = lax.ppermute(initial, axis, down)  5.1 us
  transfers between devices with their start and end apart: 10, of which 8 were waited for; matrix products, arithmetic and copies ran while one was open for 4% of the time, Pallas kernels for 0%

profile of v1, /device:TPU:1, one launch (start us, length us, event | category | flops | bytes accessed | tf_op | source)
XLA Modules:
  0.0 161.6 jit_solution(5333478168599324480)
XLA Ops:
  0.0 0.0 copy-start
  0.0 0.9 fusion.44
  0.9 5.1 %collective-permute-start.1 = (bf16[1,4,256]{2,1,0:T(4,128)(2,1)S(1)}, bf16[1,4,256]{2,1,0:T(4,128)(2,1)S(1)}, u32[]{:S(2)}, u32[]{:S(2)}) collective-permute-start(bf16[1,4,256]{2,1,0:T(4,128)(2,1)S(1)} %get-tuple-element.11), channel_id=1, source_target_pairs={{1,0},{2,1},{3,2},{4,3},{5,4},{6,5},{7,6},{8,7},{9,8},{10,9},{11,1... | collective-permute-start | bytes 6152 | tf_op jit(solution)/shard_map/ppermute | solution.py:18
  6.0 1.9 %collective-permute-start = (bf16[1,4,256]{2,1,0:T(4,128)(2,1)S(1)}, bf16[1,4,256]{2,1,0:T(4,128)(2,1)S(1)}, u32[]{:S(2)}, u32[]{:S(2)}) collective-permute-start(bf16[1,4,256]{2,1,0:T(4,128)(2,1)S(1)} %get-tuple-element.12), channel_id=1, source_target_pairs={{0,1},{1,2},{2,3},{3,4},{4,5},{5,6},{6,7},{7,8},{8,9},{9,10},{10,1... | collective-permute-start | bytes 6152 | tf_op jit(solution)/shard_map/ppermute | solution.py:17
  7.9 1.2 reshape.28
  9.1 0.0 copy-start.2
  9.1 5.8 %fusion.8 = f32[1024,2048]{1,0:T(8,128)} fusion(bf16[1024,256]{1,0:T(8,128)(2,1)S(1)} %reshape.28, bf16[3,256,2048]{2,1,0:T(8,128)(2,1)} %param.6), kind=kOutput, calls=%fused_computation.9 | convolution fusion | flops 1073741824 | bytes 9961472 | tf_op jit(solution)/shard_map/dot_general | solution.py:46
  14.8 0.0 collective-permute-done.1
  14.8 0.0 collective-permute-done
  14.8 0.0 copy-done.2
  14.8 1.2 pad_maximum_fusion
  16.0 0.1 reshape.29
  16.1 1.2 reshape.27
  17.3 0.0 copy-start.1
  17.3 2.6 %fusion.10 = f32[1024,2048]{1,0:T(8,128)S(1)} fusion(bf16[1024,256]{1,0:T(8,128)(2,1)S(1)} %reshape.27, bf16[3,256,2048]{2,1,0:T(8,128)(2,1)} %param.6), kind=kOutput, calls=%fused_computation.11 | convolution fusion | flops 1073741824 | bytes 9961472 | tf_op jit(solution)/shard_map/dot_general | solution.py:46
  20.0 1.0 copy-done.1
  21.0 0.0 copy-start.3
  21.0 2.7 %add_convert_fusion = bf16[1024,2048]{1,0:T(8,128)(2,1)S(1)} fusion(f32[1024,2048]{1,0:T(8,128)S(1)} %fusion.10, f32[1024,2048]{1,0:T(8,128)S(1)} %copy-done.1, bf16[1024,256]{1,0:T(8,128)(2,1)S(1)} %reshape.29, bf16[3,256,2048]{2,1,0:T(8,128)(2,1)} %param.6), kind=kOutput, calls=%fused_computation | convolution fusion | flops 1080033280 | bytes 22544384 | tf_op jit(solution)/shard_map/dot_general | solution.py:46
  23.7 0.0 copy-done.3
  23.8 1.3 fusion.43
  25.1 0.4 fusion.15
  25.5 0.1 broadcast_in_dim.2
  25.6 31.6 %all_to_all.18 = f32[256,1,256]{2,1,0:T(1,128)S(1)} all-to-all(f32[256,1,256]{2,1,0:T(1,128)S(1)} %broadcast_in_dim.2), channel_id=1, replica_groups=mesh['pos'=16,'exp'=16] {'pos','exp'}, dimensions={0} | all-to-all | bytes 524288 | tf_op jit(solution)/shard_map/all_to_all | solution.py:36
  57.3 0.1 fusion.20
  57.4 0.8 convolution_bitcast_fusion
  58.2 18.9 %all_to_all.19 = f32[16,8,2048]{2,1,0:T(8,128)} all-to-all(f32[16,8,2048]{2,1,0:T(8,128)S(1)} %convolution_bitcast_fusion), channel_id=1, replica_groups=mesh['pos'=16,'exp'=16] {'exp'}, dimensions={0} | all-to-all | bytes 2097152 | tf_op jit(solution)/shard_map/all_to_all | solution.py:64
  77.1 1.3 reduce_sum.39
  78.4 0.9 collective-permute-start.2
  79.2 2.3 %collective-permute-done.2 = f32[8,2048]{1,0:T(8,128)S(1)} collective-permute-done((f32[8,2048]{1,0:T(8,128)S(1)}, f32[8,2048]{1,0:T(8,128)S(1)}, u32[]{:S(2)}, u32[]{:S(2)}) %collective-permute-start.2) | collective-permute-done | bytes 65568 | tf_op jit(solution)/shard_map/ppermute | solution.py:28
  81.6 0.6 collective-permute-start.3
  82.2 4.2 %collective-permute-done.3 = f32[8,2048]{1,0:T(8,128)S(1)} collective-permute-done((f32[8,2048]{1,0:T(8,128)S(1)}, f32[8,2048]{1,0:T(8,128)S(1)}, u32[]{:S(2)}, u32[]{:S(2)}) %collective-permute-start.3) | collective-permute-done | bytes 65568 | tf_op jit(solution)/shard_map/ppermute | solution.py:28
  86.4 1.1 collective-permute-start.4
  87.5 6.3 %collective-permute-done.4 = f32[8,2048]{1,0:T(8,128)S(1)} collective-permute-done((f32[8,2048]{1,0:T(8,128)S(1)}, f32[8,2048]{1,0:T(8,128)S(1)}, u32[]{:S(2)}, u32[]{:S(2)}) %collective-permute-start.4) | collective-permute-done | bytes 65568 | tf_op jit(solution)/shard_map/ppermute | solution.py:28
  93.7 1.3 collective-permute-start.5
  95.0 3.4 %collective-permute-done.5 = f32[8,2048]{1,0:T(8,128)S(1)} collective-permute-done((f32[8,2048]{1,0:T(8,128)S(1)}, f32[8,2048]{1,0:T(8,128)S(1)}, u32[]{:S(2)}, u32[]{:S(2)}) %collective-permute-start.5) | collective-permute-done | bytes 65568 | tf_op jit(solution)/shard_map/ppermute | solution.py:28
  98.4 0.0 copy-done
  98.4 2.3 %fusion = f32[8,2048]{1,0:T(8,128)S(1)} fusion(bf16[1,512,2048]{2,1,0:T(8,128)(2,1)S(1)} %copy-done, bf16[1,2048,512]{2,1,0:T(8,128)(2,1)} %param.8, f32[8,2048]{1,0:T(8,128)S(1)} %add.43, f32[8,2048]{1,0:T(8,128)S(1)} %collective-permute-done.5), kind=kOutput, calls=%fused_computation.3 | convolution fusion | flops 33624064 | bytes 4390912 | tf_op jit(solution)/shard_map/dot_general | solution.py:70
  100.8 0.2 collective-permute-start.6
  101.0 3.1 %collective-permute-done.6 = f32[8,2048]{1,0:T(8,128)S(1)} collective-permute-done((f32[8,2048]{1,0:T(8,128)S(1)}, f32[8,2048]{1,0:T(8,128)S(1)}, u32[]{:S(2)}, u32[]{:S(2)}) %collective-permute-start.6) | collective-permute-done | bytes 65568 | tf_op jit(solution)/shard_map/ppermute | solution.py:28
  104.1 0.2 collective-permute-start.7
  104.2 4.4 %collective-permute-done.7 = f32[8,2048]{1,0:T(8,128)S(1)} collective-permute-done((f32[8,2048]{1,0:T(8,128)S(1)}, f32[8,2048]{1,0:T(8,128)S(1)}, u32[]{:S(2)}, u32[]{:S(2)}) %collective-permute-start.7) | collective-permute-done | bytes 65568 | tf_op jit(solution)/shard_map/ppermute | solution.py:28
  108.6 1.1 collective-permute-start.8
  109.7 6.6 %collective-permute-done.8 = f32[8,2048]{1,0:T(8,128)S(1)} collective-permute-done((f32[8,2048]{1,0:T(8,128)S(1)}, f32[8,2048]{1,0:T(8,128)S(1)}, u32[]{:S(2)}, u32[]{:S(2)}) %collective-permute-start.8) | collective-permute-done | bytes 65568 | tf_op jit(solution)/shard_map/ppermute | solution.py:28
  116.3 1.2 collective-permute-start.9
  117.5 3.6 %collective-permute-done.9 = f32[8,2048]{1,0:T(8,128)S(1)} collective-permute-done((f32[8,2048]{1,0:T(8,128)S(1)}, f32[8,2048]{1,0:T(8,128)S(1)}, u32[]{:S(2)}, u32[]{:S(2)}) %collective-permute-start.9) | collective-permute-done | bytes 65568 | tf_op jit(solution)/shard_map/ppermute | solution.py:28
  121.0 30.1 %all_gather.3 = bf16[128,2048]{1,0:T(8,128)(2,1)S(1)} all-gather(bf16[8,2048]{1,0:T(8,128)(2,1)S(1)} %add_convert_fusion.1), channel_id=1, replica_groups=mesh['pos'=16,'exp'=16] {'exp'}, dimensions={0}, use_global_device_ids=true | all-gather | bytes 557056 | tf_op jit(solution)/shard_map/all_gather | solution.py:77
  151.2 3.2 %convolution_convert_fusion = bf16[1024,2048]{1,0:T(8,128)(2,1)} fusion(bf16[128,2048]{1,0:T(8,128)(2,1)S(1)} %all_gather.3, f32[1024,128]{1,0:T(8,128)S(1)} %get-tuple-element.13, f32[1024]{0:T(1024)S(1)} %get-tuple-element.5, f32[1024]{0:T(1024)S(1)} %get-tuple-element.7), kind=kOutput, calls=%fused_computation.1 | convolution fusion | flops 539361280 | bytes 5251072 | tf_op jit(solution)/shard_map/dot_general | solution.py:75
  154.4 7.2 %reshape.30 = bf16[256,4,2048]{2,1,0:T(4,128)(2,1)} reshape(bf16[1024,2048]{1,0:T(8,128)(2,1)} %convolution_convert_fusion) | data formatting | bytes 8388608 | tf_op jit(solution)/shard_map/reshape | solution.py:80
  (10 shorter events, 0.1 us)
Async XLA Ops:
  0.0 98.4 %copy-start = (bf16[1,512,2048]{2,1,0:T(8,128)(2,1)S(1)}, bf16[1,512,2048]{2,1,0:T(8,128)(2,1)}, u32[]{:S(2)}) copy-start(bf16[1,512,2048]{2,1,0:T(8,128)(2,1)} %param.9) | copy-start | bytes 6291460
  0.9 14.0 %collective-permute-start.1 = (bf16[1,4,256]{2,1,0:T(4,128)(2,1)S(1)}, bf16[1,4,256]{2,1,0:T(4,128)(2,1)S(1)}, u32[]{:S(2)}, u32[]{:S(2)}) collective-permute-start(bf16[1,4,256]{2,1,0:T(4,128)(2,1)S(1)} %get-tuple-element.11), channel_id=1, source_target_pairs={{1,0},{2,1},{3,2},{4,3},{5,4},{6,5},{7,6},{8,7},{9,8},{10,9},{11,1... | collective-permute-start | bytes 6152 | tf_op jit(solution)/shard_map/ppermute | solution.py:18
  6.0 8.9 %collective-permute-start = (bf16[1,4,256]{2,1,0:T(4,128)(2,1)S(1)}, bf16[1,4,256]{2,1,0:T(4,128)(2,1)S(1)}, u32[]{:S(2)}, u32[]{:S(2)}) collective-permute-start(bf16[1,4,256]{2,1,0:T(4,128)(2,1)S(1)} %get-tuple-element.12), channel_id=1, source_target_pairs={{0,1},{1,2},{2,3},{3,4},{4,5},{5,6},{6,7},{7,8},{8,9},{9,10},{10,1... | collective-permute-start | bytes 6152 | tf_op jit(solution)/shard_map/ppermute | solution.py:17
  9.1 5.8 %copy-start.2 = (bf16[256,4,256]{2,1,0:T(4,128)(2,1)S(1)}, bf16[256,4,256]{2,1,0:T(4,128)(2,1)}, u32[]{:S(2)}) copy-start(bf16[256,4,256]{2,1,0:T(4,128)(2,1)} %param.5) | copy-start | bytes 1572868
  17.3 3.7 %copy-start.1 = (f32[1024,2048]{1,0:T(8,128)S(1)}, f32[1024,2048]{1,0:T(8,128)}, u32[]{:S(2)}) copy-start(f32[1024,2048]{1,0:T(8,128)} %fusion.8) | copy-start | bytes 25165828
  21.0 2.7 %copy-start.3 = (bf16[2048,128]{1,0:T(8,128)(2,1)S(1)}, bf16[2048,128]{1,0:T(8,128)(2,1)}, u32[]{:S(2)}) copy-start(bf16[2048,128]{1,0:T(8,128)(2,1)} %param.7) | copy-start | bytes 1572868
  78.4 3.2 %collective-permute-start.2 = (f32[8,2048]{1,0:T(8,128)S(1)}, f32[8,2048]{1,0:T(8,128)S(1)}, u32[]{:S(2)}, u32[]{:S(2)}) collective-permute-start(f32[8,2048]{1,0:T(8,128)S(1)} %reduce_sum.39), channel_id=1, source_target_pairs={{0,16},{16,0},{32,48},{48,32},{64,80},{80,64},{96,112},{112,96},{1... | collective-permute-start | bytes 196616 | tf_op jit(solution)/shard_map/ppermute | solution.py:28
  81.6 4.8 %collective-permute-start.3 = (f32[8,2048]{1,0:T(8,128)S(1)}, f32[8,2048]{1,0:T(8,128)S(1)}, u32[]{:S(2)}, u32[]{:S(2)}) collective-permute-start(f32[8,2048]{1,0:T(8,128)S(1)} %add.41), channel_id=1, source_target_pairs={{0,32},{16,48},{32,0},{48,16},{64,96},{80,112},{96,64},{112,80},{1... | collective-permute-start | bytes 196616 | tf_op jit(solution)/shard_map/ppermute | solution.py:28
  86.4 7.3 %collective-permute-start.4 = (f32[8,2048]{1,0:T(8,128)S(1)}, f32[8,2048]{1,0:T(8,128)S(1)}, u32[]{:S(2)}, u32[]{:S(2)}) collective-permute-start(f32[8,2048]{1,0:T(8,128)S(1)} %add.42), channel_id=1, source_target_pairs={{0,64},{16,80},{32,96},{48,112},{64,0},{80,16},{96,32},{112,48},{1... | collective-permute-start | bytes 196616 | tf_op jit(solution)/shard_map/ppermute | solution.py:28
  93.7 4.7 %collective-permute-start.5 = (f32[8,2048]{1,0:T(8,128)S(1)}, f32[8,2048]{1,0:T(8,128)S(1)}, u32[]{:S(2)}, u32[]{:S(2)}) collective-permute-start(f32[8,2048]{1,0:T(8,128)S(1)} %add.43), channel_id=1, source_target_pairs={{0,128},{16,144},{32,160},{48,176},{64,192},{80,208},{96,224},{112... | collective-permute-start | bytes 196616 | tf_op jit(solution)/shard_map/ppermute | solution.py:28
  100.8 3.3 %collective-permute-start.6 = (f32[8,2048]{1,0:T(8,128)S(1)}, f32[8,2048]{1,0:T(8,128)S(1)}, u32[]{:S(2)}, u32[]{:S(2)}) collective-permute-start(f32[8,2048]{1,0:T(8,128)S(1)} %fusion), channel_id=1, source_target_pairs={{0,16},{16,0},{32,48},{48,32},{64,80},{80,64},{96,112},{112,96},{1... | collective-permute-start | bytes 196616 | tf_op jit(solution)/shard_map/ppermute | solution.py:28
  104.1 4.5 %collective-permute-start.7 = (f32[8,2048]{1,0:T(8,128)S(1)}, f32[8,2048]{1,0:T(8,128)S(1)}, u32[]{:S(2)}, u32[]{:S(2)}) collective-permute-start(f32[8,2048]{1,0:T(8,128)S(1)} %add.48), channel_id=1, source_target_pairs={{0,32},{16,48},{32,0},{48,16},{64,96},{80,112},{96,64},{112,80},{1... | collective-permute-start | bytes 196616 | tf_op jit(solution)/shard_map/ppermute | solution.py:28
  108.6 7.7 %collective-permute-start.8 = (f32[8,2048]{1,0:T(8,128)S(1)}, f32[8,2048]{1,0:T(8,128)S(1)}, u32[]{:S(2)}, u32[]{:S(2)}) collective-permute-start(f32[8,2048]{1,0:T(8,128)S(1)} %add.49), channel_id=1, source_target_pairs={{0,64},{16,80},{32,96},{48,112},{64,0},{80,16},{96,32},{112,48},{1... | collective-permute-start | bytes 196616 | tf_op jit(solution)/shard_map/ppermute | solution.py:28
  116.3 4.7 %collective-permute-start.9 = (f32[8,2048]{1,0:T(8,128)S(1)}, f32[8,2048]{1,0:T(8,128)S(1)}, u32[]{:S(2)}, u32[]{:S(2)}) collective-permute-start(f32[8,2048]{1,0:T(8,128)S(1)} %add.50), channel_id=1, source_target_pairs={{0,128},{16,144},{32,160},{48,176},{64,192},{80,208},{96,224},{112... | collective-permute-start | bytes 196616 | tf_op jit(solution)/shard_map/ppermute | solution.py:28

commit v2 on v1

--- a/solution.py
+++ b/solution.py
@@ -30,10 +30,22 @@
     return value
 
 
-def gather_rows(row, axes):
-    count = lax.axis_size(axes)
-    tiled = jnp.broadcast_to(row[None, :], (count, row.shape[0]))
-    return lax.all_to_all(tiled, axes, 0, 0, tiled=True)
+def merge(mine, theirs):
+    peak = jnp.maximum(mine[:, D], theirs[:, D])
+    a = jnp.exp(mine[:, D] - peak)[:, None]
+    b = jnp.exp(theirs[:, D] - peak)[:, None]
+    merged = mine * a + theirs * b
+    return merged.at[:, D].set(peak)
+
+
+def butterfly_softmax_sum(value, axis):
+    count = lax.axis_size(axis)
+    step = 1
+    while step < count:
+        pairs = [(i, i ^ step) for i in range(count)]
+        value = merge(value, lax.ppermute(value, axis, pairs))
+        step *= 2
+    return value
 
 
 def per_device(patches, conv_weight, phi, w_in, w_out):
@@ -49,21 +61,27 @@
     slots = logits.shape[1]
 
     local_peak = jnp.max(logits, axis=0)
-    local_total = jnp.sum(jnp.exp(logits - local_peak), axis=0)
-    stats = gather_rows(jnp.concatenate([local_peak, local_total]), every)
-    peaks, totals = stats[:, :slots], stats[:, slots:]
-    column_peak = jnp.max(peaks, axis=0)
-    column_total = jnp.sum(totals * jnp.exp(peaks - column_peak), axis=0)
-
-    raw_weights = jnp.exp(logits - column_peak)
-    dispatch = (raw_weights / column_total).astype(jnp.bfloat16)
+    raw_weights = jnp.exp(logits - local_peak)
+    local_total = jnp.sum(raw_weights, axis=0)
     every_slot = lax.dot_general(
-        dispatch, flat, (((0,), (0,)), ((), ())), preferred_element_type=jnp.float32
+        raw_weights.astype(jnp.bfloat16), flat, (((0,), (0,)), ((), ())),
+        preferred_element_type=jnp.float32,
     )
+    extra = jnp.zeros((slots, 128), jnp.float32)
+    extra = extra.at[:, 0].set(local_peak).at[:, 1].set(local_total)
+    packed = jnp.concatenate([every_slot, extra], axis=1)
     groups = lax.axis_size("exp")
-    mine = lax.all_to_all(every_slot, "exp", 0, 0, tiled=True)
-    owned = jnp.sum(mine.reshape(groups, SLOTS_PER, D), axis=0)
-    slot_in = butterfly_sum(owned, "pos").astype(jnp.bfloat16)
+    mine = lax.all_to_all(packed, "exp", 0, 0, tiled=True).reshape(groups, SLOTS_PER, -1)
+    peaks = mine[:, :, D]
+    peak = jnp.max(peaks, axis=0)
+    scale = jnp.exp(peaks - peak)
+    sums = jnp.sum(mine[:, :, :D] * scale[:, :, None], axis=0)
+    total = jnp.sum(mine[:, :, D + 1] * scale, axis=0)
+    owned = jnp.concatenate(
+        [sums, jnp.zeros((SLOTS_PER, 128), jnp.float32).at[:, 0].set(peak).at[:, 1].set(total)], axis=1
+    )
+    owned = butterfly_softmax_sum(owned, "pos")
+    slot_in = (owned[:, :D] / owned[:, D + 1 : D + 2]).astype(jnp.bfloat16)
     hidden = jax.nn.gelu(
         jnp.dot(slot_in, w_in[0], preferred_element_type=jnp.float32), approximate=True
     ).astype(jnp.bfloat16)

time: 162 us -> 149 us (0.920)
  blocking collectives: 80.7 us -> 51.5 us
  starting transfers between devices: 13.4 us -> 31.8 us
  waiting for transfers between devices: 33.8 us -> 16.6 us
  matrix products: 18.8 us -> 26.6 us
  other arithmetic: 3 us -> 9.85 us
    all_to_all x2 -> x1, blocking collectives: 50.6 us -> 22.7 us  [per_device(): lax.all_to_all(packed, 'exp', 0, 0, tiled=True)]
    ppermute x8 -> x4, waiting for transfers between devices: 33.8 us -> 10.1 us  [butterfly_sum(): value = value + lax.ppermute(value, axis, pairs)]
    ppermute x0 -> x4, starting transfers between devices: none -> 15.9 us  [butterfly_softmax_sum(): value = merge(value, lax.ppermute(value, axis, pairs))]
    dot_general x3, matrix products: 11.1 us -> 18.8 us  [per_device(): jnp.dot(window, conv_weight[offset], preferred_element_type=jnp.float32)]
    ppermute x0 -> x4, waiting for transfers between devices: none -> 6.5 us  [butterfly_softmax_sum(): value = merge(value, lax.ppermute(value, axis, pairs))]
    another operation x0 -> x7, other arithmetic: none -> 4.6 us
    ppermute x1, starting transfers between devices: 5.1 us -> 1.92 us  [with_halo(): after = lax.ppermute(initial, axis, down)]
    ppermute x8 -> x4, starting transfers between devices: 6.42 us -> 9.52 us  [butterfly_sum(): value = value + lax.ppermute(value, axis, pairs)]
  transfers between devices with their start and end apart: 10 -> 10, of which waited for: 8 -> 8; matrix products, arithmetic and copies ran while one was open for 4% -> 6% of each run, Pallas kernels for 0% -> 0%
where the time goes in v2:
time: 149 us
  blocking collectives  51.5 us (35%)
  starting transfers between devices  31.8 us (21%)
  matrix products  26.6 us (18%)
  waiting for transfers between devices  16.6 us (11%)
  local copies, waits for them, and re-layouts  12.1 us (8%)
  other arithmetic  9.85 us (7%)
    all_gather x1, blocking collectives, per_device(): lax.all_gather(slot_out, 'exp', axis=0, tiled=True)  28.8 us
    all_to_all x1, blocking collectives, per_device(): lax.all_to_all(packed, 'exp', 0, 0, tiled=True)  22.7 us
    dot_general x3, matrix products, per_device(): jnp.dot(window, conv_weight[offset], preferred_element_type=jnp.float32)  18.8 us
    ppermute x4, starting transfers between devices, butterfly_softmax_sum(): value = merge(value, lax.ppermute(value, axis, pairs))  15.9 us
    ppermute x4, waiting for transfers between devices, butterfly_sum(): value = value + lax.ppermute(value, axis, pairs)  10.1 us
    ppermute x4, starting transfers between devices, butterfly_sum(): value = value + lax.ppermute(value, axis, pairs)  9.52 us
    reshape x1, local copies, waits for them, and re-layouts, per_device(): return mixed.astype(jnp.bfloat16).reshape(channels, periods, D)  7.16 us
    ppermute x4, waiting for transfers between devices, butterfly_softmax_sum(): value = merge(value, lax.ppermute(value, axis, pairs))  6.5 us
  transfers between devices with their start and end apart: 10, of which 8 were waited for; matrix products, arithmetic and copies ran while one was open for 6% of the time, Pallas kernels for 0%

profile of v2, /device:TPU:1, one launch (start us, length us, event | category | flops | bytes accessed | tf_op | source)
XLA Modules:
  0.0 148.6 jit_solution(7470590385884064457)
XLA Ops:
  0.0 0.9 fusion.68
  0.9 4.5 %collective-permute-start = (bf16[1,4,256]{2,1,0:T(4,128)(2,1)S(1)}, bf16[1,4,256]{2,1,0:T(4,128)(2,1)S(1)}, u32[]{:S(2)}, u32[]{:S(2)}) collective-permute-start(bf16[1,4,256]{2,1,0:T(4,128)(2,1)S(1)} %get-tuple-element.119), channel_id=1, source_target_pairs={{0,1},{1,2},{2,3},{3,4},{4,5},{5,6},{6,7},{7,8},{8,9},{9,10},{10,1... | collective-permute-start | bytes 6152 | tf_op jit(solution)/shard_map/ppermute | solution.py:17
  5.3 1.9 %collective-permute-start.1 = (bf16[1,4,256]{2,1,0:T(4,128)(2,1)S(1)}, bf16[1,4,256]{2,1,0:T(4,128)(2,1)S(1)}, u32[]{:S(2)}, u32[]{:S(2)}) collective-permute-start(bf16[1,4,256]{2,1,0:T(4,128)(2,1)S(1)} %get-tuple-element.118), channel_id=1, source_target_pairs={{1,0},{2,1},{3,2},{4,3},{5,4},{6,5},{7,6},{8,7},{9,8},{10,9},{11,1... | collective-permute-start | bytes 6152 | tf_op jit(solution)/shard_map/ppermute | solution.py:18
  7.3 1.2 reshape.245
  8.5 5.8 %fusion.9 = f32[1024,2048]{1,0:T(8,128)} fusion(bf16[1024,256]{1,0:T(8,128)(2,1)S(1)} %reshape.245, bf16[3,256,2048]{2,1,0:T(8,128)(2,1)} %param.22), kind=kOutput, calls=%fused_computation.11 | convolution fusion | flops 1073741824 | bytes 9961472 | tf_op jit(solution)/shard_map/dot_general | solution.py:58
  14.2 0.6 compare_reduce_fusion.1
  14.9 0.7 compare_reduce_fusion.2
  15.6 1.2 pad_maximum_fusion
  16.8 1.2 reshape.244
  17.9 5.7 %fusion.11 = f32[1024,2048]{1,0:T(8,128)} fusion(bf16[1024,256]{1,0:T(8,128)(2,1)S(1)} %reshape.244, bf16[3,256,2048]{2,1,0:T(8,128)(2,1)} %param.22), kind=kOutput, calls=%fused_computation.13 | convolution fusion | flops 1073741824 | bytes 9961472 | tf_op jit(solution)/shard_map/dot_general | solution.py:58
  23.8 7.4 %add_convert_fusion = bf16[1024,2048]{1,0:T(8,128)(2,1)S(1)} fusion(f32[1024,2048]{1,0:T(8,128)} %fusion.11, f32[1024,2048]{1,0:T(8,128)} %fusion.9, bf16[1024,256]{1,0:T(8,128)(2,1)S(1)} %reshape.246, bf16[3,256,2048]{2,1,0:T(8,128)(2,1)} %param.22), kind=kOutput, calls=%fused_computation | convolution fusion | flops 1080033280 | bytes 22544384 | tf_op jit(solution)/shard_map/dot_general | solution.py:58
  31.2 1.3 fusion.66
  32.5 0.8 fusion.19
  33.3 0.4 fusion.16
  33.6 0.6 fusion.59
  34.3 0.7 fusion.58
  35.1 0.4 scatter.25
  35.6 22.7 %all_to_all.9 = f32[16,8,2176]{2,1,0:T(8,128)S(1)} all-to-all(f32[16,8,2176]{2,1,0:T(8,128)S(1)} %maximum_bitcast_fusion), channel_id=1, replica_groups=mesh['pos'=16,'exp'=16] {'exp'}, dimensions={0} | all-to-all | bytes 2228224 | tf_op jit(solution)/shard_map/all_to_all | solution.py:74
  58.5 0.7 fusion.60
  59.5 0.2 fusion.57
  59.7 0.6 fusion.61
  60.7 2.0 %collective-permute-start.2 = (f32[8,2176]{1,0:T(8,128)S(1)}, f32[8,2176]{1,0:T(8,128)S(1)}, u32[]{:S(2)}, u32[]{:S(2)}) collective-permute-start(f32[8,2176]{1,0:T(8,128)S(1)} %pad_maximum_fusion.2), channel_id=1, source_target_pairs={{0,16},{16,0},{32,48},{48,32},{64,80},{80,64},{96,112},{112,96},{1... | collective-permute-start | bytes 208904 | tf_op jit(solution)/shard_map/ppermute | solution.py:46
  62.7 0.7 compare_reduce_fusion
  63.4 1.4 collective-permute-done.2
  64.8 0.2 exponential_reduce_fusion.5
  65.1 0.7 slice_select_fusion.2
  65.9 3.4 %collective-permute-start.3 = (f32[8,2176]{1,0:T(8,128)S(1)}, f32[8,2176]{1,0:T(8,128)S(1)}, u32[]{:S(2)}, u32[]{:S(2)}) collective-permute-start(f32[8,2176]{1,0:T(8,128)S(1)} %scatter.30), channel_id=1, source_target_pairs={{0,32},{16,48},{32,0},{48,16},{64,96},{80,112},{96,64},{112,80},{1... | collective-permute-start | bytes 208904 | tf_op jit(solution)/shard_map/ppermute | solution.py:46
  69.2 1.7 %collective-permute-done.3 = f32[8,2176]{1,0:T(8,128)S(1)} collective-permute-done((f32[8,2176]{1,0:T(8,128)S(1)}, f32[8,2176]{1,0:T(8,128)S(1)}, u32[]{:S(2)}, u32[]{:S(2)}) %collective-permute-start.3) | collective-permute-done | bytes 69664 | tf_op jit(solution)/shard_map/ppermute | solution.py:46
  70.9 0.2 exponential_reduce_fusion.3
  71.2 0.7 slice_select_fusion.1
  72.0 7.4 %collective-permute-start.4 = (f32[8,2176]{1,0:T(8,128)S(1)}, f32[8,2176]{1,0:T(8,128)S(1)}, u32[]{:S(2)}, u32[]{:S(2)}) collective-permute-start(f32[8,2176]{1,0:T(8,128)S(1)} %scatter.31), channel_id=1, source_target_pairs={{0,64},{16,80},{32,96},{48,112},{64,0},{80,16},{96,32},{112,48},{1... | collective-permute-start | bytes 208904 | tf_op jit(solution)/shard_map/ppermute | solution.py:46
  79.4 1.7 %collective-permute-done.4 = f32[8,2176]{1,0:T(8,128)S(1)} collective-permute-done((f32[8,2176]{1,0:T(8,128)S(1)}, f32[8,2176]{1,0:T(8,128)S(1)}, u32[]{:S(2)}, u32[]{:S(2)}) %collective-permute-start.4) | collective-permute-done | bytes 69664 | tf_op jit(solution)/shard_map/ppermute | solution.py:46
  81.4 0.7 slice_select_fusion
  82.2 3.1 %collective-permute-start.5 = (f32[8,2176]{1,0:T(8,128)S(1)}, f32[8,2176]{1,0:T(8,128)S(1)}, u32[]{:S(2)}, u32[]{:S(2)}) collective-permute-start(f32[8,2176]{1,0:T(8,128)S(1)} %scatter.34), channel_id=1, source_target_pairs={{0,128},{16,144},{32,160},{48,176},{64,192},{80,208},{96,224},{112... | collective-permute-start | bytes 208904 | tf_op jit(solution)/shard_map/ppermute | solution.py:46
  85.2 1.7 %collective-permute-done.5 = f32[8,2176]{1,0:T(8,128)S(1)} collective-permute-done((f32[8,2176]{1,0:T(8,128)S(1)}, f32[8,2176]{1,0:T(8,128)S(1)}, u32[]{:S(2)}, u32[]{:S(2)}) %collective-permute-start.5) | collective-permute-done | bytes 69664 | tf_op jit(solution)/shard_map/ppermute | solution.py:46
  87.2 0.2 slice_reduce_fusion
  87.3 2.4 %fusion = f32[8,2048]{1,0:T(8,128)S(1)} fusion(bf16[1,512,2048]{2,1,0:T(8,128)(2,1)S(1)} %copy-done, bf16[1,2048,512]{2,1,0:T(8,128)(2,1)} %param.24, f32[8,2176]{1,0:T(8,128)S(1)} %multiply_add_fusion, f32[8]{0:T(128)S(1)} %slice_reduce_fusion), kind=kOutput, calls=%fused_computation.2 | convolution fusion | flops 33624064 | bytes 4325888 | tf_op jit(solution)/shard_map/dot_general | solution.py:88
  89.7 0.2 collective-permute-start.6
  89.9 3.1 %collective-permute-done.6 = f32[8,2048]{1,0:T(8,128)S(1)} collective-permute-done((f32[8,2048]{1,0:T(8,128)S(1)}, f32[8,2048]{1,0:T(8,128)S(1)}, u32[]{:S(2)}, u32[]{:S(2)}) %collective-permute-start.6) | collective-permute-done | bytes 65568 | tf_op jit(solution)/shard_map/ppermute | solution.py:28
  93.0 0.8 collective-permute-start.7
  93.9 3.7 %collective-permute-done.7 = f32[8,2048]{1,0:T(8,128)S(1)} collective-permute-done((f32[8,2048]{1,0:T(8,128)S(1)}, f32[8,2048]{1,0:T(8,128)S(1)}, u32[]{:S(2)}, u32[]{:S(2)}) %collective-permute-start.7) | collective-permute-done | bytes 65568 | tf_op jit(solution)/shard_map/ppermute | solution.py:28
  97.6 5.5 %collective-permute-start.8 = (f32[8,2048]{1,0:T(8,128)S(1)}, f32[8,2048]{1,0:T(8,128)S(1)}, u32[]{:S(2)}, u32[]{:S(2)}) collective-permute-start(f32[8,2048]{1,0:T(8,128)S(1)} %add.69), channel_id=1, source_target_pairs={{0,64},{16,80},{32,96},{48,112},{64,0},{80,16},{96,32},{112,48},{1... | collective-permute-start | bytes 196616 | tf_op jit(solution)/shard_map/ppermute | solution.py:28
  103.0 1.7 %collective-permute-done.8 = f32[8,2048]{1,0:T(8,128)S(1)} collective-permute-done((f32[8,2048]{1,0:T(8,128)S(1)}, f32[8,2048]{1,0:T(8,128)S(1)}, u32[]{:S(2)}, u32[]{:S(2)}) %collective-permute-start.8) | collective-permute-done | bytes 65568 | tf_op jit(solution)/shard_map/ppermute | solution.py:28
  104.7 3.0 %collective-permute-start.9 = (f32[8,2048]{1,0:T(8,128)S(1)}, f32[8,2048]{1,0:T(8,128)S(1)}, u32[]{:S(2)}, u32[]{:S(2)}) collective-permute-start(f32[8,2048]{1,0:T(8,128)S(1)} %add.70), channel_id=1, source_target_pairs={{0,128},{16,144},{32,160},{48,176},{64,192},{80,208},{96,224},{112... | collective-permute-start | bytes 196616 | tf_op jit(solution)/shard_map/ppermute | solution.py:28
  107.7 1.7 %collective-permute-done.9 = f32[8,2048]{1,0:T(8,128)S(1)} collective-permute-done((f32[8,2048]{1,0:T(8,128)S(1)}, f32[8,2048]{1,0:T(8,128)S(1)}, u32[]{:S(2)}, u32[]{:S(2)}) %collective-permute-start.9) | collective-permute-done | bytes 65568 | tf_op jit(solution)/shard_map/ppermute | solution.py:28
  109.4 28.8 %all_gather.3 = bf16[128,2048]{1,0:T(8,128)(2,1)S(1)} all-gather(bf16[8,2048]{1,0:T(8,128)(2,1)S(1)} %add_convert_fusion.1), channel_id=1, replica_groups=mesh['pos'=16,'exp'=16] {'exp'}, dimensions={0}, use_global_device_ids=true | all-gather | bytes 557056 | tf_op jit(solution)/shard_map/all_gather | solution.py:95
  138.2 3.3 %convolution_convert_fusion = bf16[1024,2048]{1,0:T(8,128)(2,1)} fusion(bf16[128,2048]{1,0:T(8,128)(2,1)S(1)} %all_gather.3, f32[1024,128]{1,0:T(8,128)S(1)} %copy-done.2, f32[1024]{0:T(1024)S(1)} %get-tuple-element.101, f32[1024]{0:T(1024)S(1)} %get-tuple-element.103), kind=kOutput, calls=%fused_computation.1 | convolution fusion | flops 539361280 | bytes 5251072 | tf_op jit(solution)/shard_map/dot_general | solution.py:93
  141.5 7.2 %reshape.251 = bf16[256,4,2048]{2,1,0:T(4,128)(2,1)} reshape(bf16[1024,2048]{1,0:T(8,128)(2,1)} %convolution_convert_fusion) | data formatting | bytes 8388608 | tf_op jit(solution)/shard_map/reshape | solution.py:98
  (41 shorter events, 2.3 us)
Async XLA Ops:
  0.0 87.3 %copy-start = (bf16[1,512,2048]{2,1,0:T(8,128)(2,1)S(1)}, bf16[1,512,2048]{2,1,0:T(8,128)(2,1)}, u32[]{:S(2)}) copy-start(bf16[1,512,2048]{2,1,0:T(8,128)(2,1)} %param.25) | copy-start | bytes 6291460
  0.9 14.7 %collective-permute-start = (bf16[1,4,256]{2,1,0:T(4,128)(2,1)S(1)}, bf16[1,4,256]{2,1,0:T(4,128)(2,1)S(1)}, u32[]{:S(2)}, u32[]{:S(2)}) collective-permute-start(bf16[1,4,256]{2,1,0:T(4,128)(2,1)S(1)} %get-tuple-element.119), channel_id=1, source_target_pairs={{0,1},{1,2},{2,3},{3,4},{4,5},{5,6},{6,7},{7,8},{8,9},{9,10},{10,1... | collective-permute-start | bytes 6152 | tf_op jit(solution)/shard_map/ppermute | solution.py:17
  5.3 10.2 %collective-permute-start.1 = (bf16[1,4,256]{2,1,0:T(4,128)(2,1)S(1)}, bf16[1,4,256]{2,1,0:T(4,128)(2,1)S(1)}, u32[]{:S(2)}, u32[]{:S(2)}) collective-permute-start(bf16[1,4,256]{2,1,0:T(4,128)(2,1)S(1)} %get-tuple-element.118), channel_id=1, source_target_pairs={{1,0},{2,1},{3,2},{4,3},{5,4},{6,5},{7,6},{8,7},{9,8},{10,9},{11,1... | collective-permute-start | bytes 6152 | tf_op jit(solution)/shard_map/ppermute | solution.py:18
  8.4 7.1 %copy-start.3 = (bf16[256,4,256]{2,1,0:T(4,128)(2,1)S(1)}, bf16[256,4,256]{2,1,0:T(4,128)(2,1)}, u32[]{:S(2)}) copy-start(bf16[256,4,256]{2,1,0:T(4,128)(2,1)} %param.21) | copy-start | bytes 1572868
  23.8 7.4 %copy-start.4 = (bf16[2048,128]{1,0:T(8,128)(2,1)S(1)}, bf16[2048,128]{1,0:T(8,128)(2,1)}, u32[]{:S(2)}) copy-start(bf16[2048,128]{1,0:T(8,128)(2,1)} %param.23) | copy-start | bytes 1572868
  32.5 1.1 copy-start.1
  60.7 4.1 %collective-permute-start.2 = (f32[8,2176]{1,0:T(8,128)S(1)}, f32[8,2176]{1,0:T(8,128)S(1)}, u32[]{:S(2)}, u32[]{:S(2)}) collective-permute-start(f32[8,2176]{1,0:T(8,128)S(1)} %pad_maximum_fusion.2), channel_id=1, source_target_pairs={{0,16},{16,0},{32,48},{48,32},{64,80},{80,64},{96,112},{112,96},{1... | collective-permute-start | bytes 208904 | tf_op jit(solution)/shard_map/ppermute | solution.py:46
  65.9 5.1 %collective-permute-start.3 = (f32[8,2176]{1,0:T(8,128)S(1)}, f32[8,2176]{1,0:T(8,128)S(1)}, u32[]{:S(2)}, u32[]{:S(2)}) collective-permute-start(f32[8,2176]{1,0:T(8,128)S(1)} %scatter.30), channel_id=1, source_target_pairs={{0,32},{16,48},{32,0},{48,16},{64,96},{80,112},{96,64},{112,80},{1... | collective-permute-start | bytes 208904 | tf_op jit(solution)/shard_map/ppermute | solution.py:46
  71.1 67.1 %copy-start.2 = (f32[1024,128]{1,0:T(8,128)S(1)}, f32[1024,128]{1,0:T(8,128)}, u32[]{:S(2)}) copy-start(f32[1024,128]{1,0:T(8,128)} %copy-done.1) | copy-start | bytes 1572868
  72.0 9.1 %collective-permute-start.4 = (f32[8,2176]{1,0:T(8,128)S(1)}, f32[8,2176]{1,0:T(8,128)S(1)}, u32[]{:S(2)}, u32[]{:S(2)}) collective-permute-start(f32[8,2176]{1,0:T(8,128)S(1)} %scatter.31), channel_id=1, source_target_pairs={{0,64},{16,80},{32,96},{48,112},{64,0},{80,16},{96,32},{112,48},{1... | collective-permute-start | bytes 208904 | tf_op jit(solution)/shard_map/ppermute | solution.py:46
  82.2 4.8 %collective-permute-start.5 = (f32[8,2176]{1,0:T(8,128)S(1)}, f32[8,2176]{1,0:T(8,128)S(1)}, u32[]{:S(2)}, u32[]{:S(2)}) collective-permute-start(f32[8,2176]{1,0:T(8,128)S(1)} %scatter.34), channel_id=1, source_target_pairs={{0,128},{16,144},{32,160},{48,176},{64,192},{80,208},{96,224},{112... | collective-permute-start | bytes 208904 | tf_op jit(solution)/shard_map/ppermute | solution.py:46
  89.7 3.3 %collective-permute-start.6 = (f32[8,2048]{1,0:T(8,128)S(1)}, f32[8,2048]{1,0:T(8,128)S(1)}, u32[]{:S(2)}, u32[]{:S(2)}) collective-permute-start(f32[8,2048]{1,0:T(8,128)S(1)} %fusion), channel_id=1, source_target_pairs={{0,16},{16,0},{32,48},{48,32},{64,80},{80,64},{96,112},{112,96},{1... | collective-permute-start | bytes 196616 | tf_op jit(solution)/shard_map/ppermute | solution.py:28
  93.0 4.5 %collective-permute-start.7 = (f32[8,2048]{1,0:T(8,128)S(1)}, f32[8,2048]{1,0:T(8,128)S(1)}, u32[]{:S(2)}, u32[]{:S(2)}) collective-permute-start(f32[8,2048]{1,0:T(8,128)S(1)} %add.68), channel_id=1, source_target_pairs={{0,32},{16,48},{32,0},{48,16},{64,96},{80,112},{96,64},{112,80},{1... | collective-permute-start | bytes 196616 | tf_op jit(solution)/shard_map/ppermute | solution.py:28
  97.6 7.1 %collective-permute-start.8 = (f32[8,2048]{1,0:T(8,128)S(1)}, f32[8,2048]{1,0:T(8,128)S(1)}, u32[]{:S(2)}, u32[]{:S(2)}) collective-permute-start(f32[8,2048]{1,0:T(8,128)S(1)} %add.69), channel_id=1, source_target_pairs={{0,64},{16,80},{32,96},{48,112},{64,0},{80,16},{96,32},{112,48},{1... | collective-permute-start | bytes 196616 | tf_op jit(solution)/shard_map/ppermute | solution.py:28
  104.7 4.7 %collective-permute-start.9 = (f32[8,2048]{1,0:T(8,128)S(1)}, f32[8,2048]{1,0:T(8,128)S(1)}, u32[]{:S(2)}, u32[]{:S(2)}) collective-permute-start(f32[8,2048]{1,0:T(8,128)S(1)} %add.70), channel_id=1, source_target_pairs={{0,128},{16,144},{32,160},{48,176},{64,192},{80,208},{96,224},{112... | collective-permute-start | bytes 196616 | tf_op jit(solution)/shard_map/ppermute | solution.py:28

commit v3 on v2

--- a/solution.py
+++ b/solution.py
@@ -52,11 +52,10 @@
     channels, periods, samples = patches.shape
     every = ("pos", "exp")
     padded = with_halo(patches, ((every, 0),), 1)
-    running = jnp.zeros((channels * periods, D), jnp.float32)
-    for offset in range(3):
-        window = padded[offset : offset + channels].reshape(channels * periods, samples)
-        running = running + jnp.dot(window, conv_weight[offset], preferred_element_type=jnp.float32)
-    flat = running.astype(jnp.bfloat16)
+    window = jnp.concatenate([padded[offset : offset + channels] for offset in range(3)], axis=2)
+    taps = conv_weight.reshape(3 * samples, D)
+    window = window.reshape(channels * periods, 3 * samples)
+    flat = jnp.dot(window, taps, preferred_element_type=jnp.float32).astype(jnp.bfloat16)
     logits = jnp.dot(flat, phi, preferred_element_type=jnp.float32)
     slots = logits.shape[1]
 

time: 149 us -> 149 us (level)
  matrix products: 26.6 us -> 15.4 us
  other arithmetic: 9.85 us -> 15.1 us
  waiting for transfers between devices: 16.6 us -> 20.1 us
  local copies, waits for them, and re-layouts: 12.1 us -> 14.3 us
    dot_general x3 -> x1, matrix products: 18.8 us -> 5.08 us  [per_device(): jnp.dot(window, taps, preferred_element_type=jnp.float32)]
    concatenate x1, other arithmetic: 1.17 us -> 4.24 us  [per_device(): jnp.concatenate([padded[offset:offset + channels] for offset in range(3)]...]
    ppermute x4, starting transfers between devices: 15.9 us -> 13.4 us  [butterfly_softmax_sum(): value = merge(value, lax.ppermute(value, axis, pairs))]
    ppermute x4, waiting for transfers between devices: 6.5 us -> 8.99 us  [butterfly_softmax_sum(): value = merge(value, lax.ppermute(value, axis, pairs))]
    all_to_all x1, blocking collectives: 22.7 us -> 25 us  [per_device(): lax.all_to_all(packed, 'exp', 0, 0, tiled=True)]
    all_gather x1, blocking collectives: 28.8 us -> 27.2 us  [per_device(): lax.all_gather(slot_out, 'exp', axis=0, tiled=True)]
    ppermute x4, starting transfers between devices: 9.52 us -> 11.1 us  [butterfly_sum(): value = value + lax.ppermute(value, axis, pairs)]
    ppermute x1, waiting for transfers between devices: 0.01 us -> 1.6 us  [with_halo(): after = lax.ppermute(initial, axis, down)]
  transfers between devices with their start and end apart: 10 -> 10, of which waited for: 8 -> 9; matrix products, arithmetic and copies ran while one was open for 6% -> 1% of each run, Pallas kernels for 0% -> 0%
where the time goes in v3:
time: 149 us; the launch traced here: 148 us
  blocking collectives  52.2 us (35%)
  starting transfers between devices  31 us (21%)
  waiting for transfers between devices  20.1 us (13%)
  matrix products  15.4 us (10%)
  other arithmetic  15.1 us (10%)
  local copies, waits for them, and re-layouts  14.3 us (10%)
    all_gather x1, blocking collectives, per_device(): lax.all_gather(slot_out, 'exp', axis=0, tiled=True)  27.2 us
    all_to_all x1, blocking collectives, per_device(): lax.all_to_all(packed, 'exp', 0, 0, tiled=True)  25 us
    ppermute x4, starting transfers between devices, butterfly_softmax_sum(): value = merge(value, lax.ppermute(value, axis, pairs))  13.4 us
    ppermute x4, starting transfers between devices, butterfly_sum(): value = value + lax.ppermute(value, axis, pairs)  11.1 us
    ppermute x4, waiting for transfers between devices, butterfly_sum(): value = value + lax.ppermute(value, axis, pairs)  9.49 us
    ppermute x4, waiting for transfers between devices, butterfly_softmax_sum(): value = merge(value, lax.ppermute(value, axis, pairs))  8.99 us
    reshape x1, local copies, waits for them, and re-layouts, per_device(): return mixed.astype(jnp.bfloat16).reshape(channels, periods, D)  7.16 us
    dot_general x1, matrix products, per_device(): jnp.dot(window, taps, preferred_element_type=jnp.float32)  5.08 us
  transfers between devices with their start and end apart: 10, of which 9 were waited for; matrix products, arithmetic and copies ran while one was open for 1% of the time, Pallas kernels for 0%

profile of v3, /device:TPU:1, one launch (start us, length us, event | category | flops | bytes accessed | tf_op | source)
XLA Modules:
  0.0 148.4 jit_solution(1167179323000761752)
XLA Ops:
  0.0 0.9 fusion.59
  0.9 4.6 %collective-permute-start = (bf16[1,4,256]{2,1,0:T(4,128)(2,1)S(1)}, bf16[1,4,256]{2,1,0:T(4,128)(2,1)S(1)}, u32[]{:S(2)}, u32[]{:S(2)}) collective-permute-start(bf16[1,4,256]{2,1,0:T(4,128)(2,1)S(1)} %get-tuple-element.116), channel_id=1, source_target_pairs={{0,1},{1,2},{2,3},{3,4},{4,5},{5,6},{6,7},{7,8},{8,9},{9,10},{10,1... | collective-permute-start | bytes 6152 | tf_op jit(solution)/shard_map/ppermute | solution.py:17
  5.5 1.9 %collective-permute-start.1 = (bf16[1,4,256]{2,1,0:T(4,128)(2,1)S(1)}, bf16[1,4,256]{2,1,0:T(4,128)(2,1)S(1)}, u32[]{:S(2)}, u32[]{:S(2)}) collective-permute-start(bf16[1,4,256]{2,1,0:T(4,128)(2,1)S(1)} %get-tuple-element.117), channel_id=1, source_target_pairs={{1,0},{2,1},{3,2},{4,3},{5,4},{6,5},{7,6},{8,7},{9,8},{10,9},{11,1... | collective-permute-start | bytes 6152 | tf_op jit(solution)/shard_map/ppermute | solution.py:18
  7.4 0.7 compare_reduce_fusion.2
  8.1 0.7 compare_reduce_fusion.1
  8.8 1.6 %collective-permute-done.1 = bf16[1,4,256]{2,1,0:T(4,128)(2,1)S(1)} collective-permute-done((bf16[1,4,256]{2,1,0:T(4,128)(2,1)S(1)}, bf16[1,4,256]{2,1,0:T(4,128)(2,1)S(1)}, u32[]{:S(2)}, u32[]{:S(2)}) %collective-permute-start.1) | collective-permute-done | bytes 2080 | tf_op jit(solution)/shard_map/ppermute | solution.py:18
  10.4 4.2 %fusion.4 = bf16[256,4,768]{2,1,0:T(4,128)(2,1)} fusion(bf16[1,4,256]{2,1,0:T(4,128)(2,1)S(1)} %collective-permute-done.1, bf16[256,4,256]{2,1,0:T(4,128)(2,1)} %param.21, bf16[1,4,256]{2,1,0:T(4,128)(2,1)S(1)} %collective-permute-done), kind=kLoop, calls=%fused_computation.7 | loop fusion | flops 7864320 | bytes 2101248 | tf_op jit(solution)/shard_map/concatenate | solution.py:55
  14.6 3.7 %reshape.241 = bf16[1024,768]{1,0:T(8,128)(2,1)} reshape(bf16[256,4,768]{2,1,0:T(4,128)(2,1)} %fusion.4) | data formatting | bytes 3145728 | tf_op jit(solution)/shard_map/reshape | solution.py:57
  18.4 5.1 %convolution_convert_fusion.1 = bf16[1024,2048]{1,0:T(8,128)(2,1)S(1)} fusion(bf16[1024,768]{1,0:T(8,128)(2,1)} %reshape.241, bf16[768,2048]{1,0:T(8,128)(2,1)S(1)} %bitcast.41), kind=kOutput, calls=%fused_computation.1 | convolution fusion | flops 3223322624 | bytes 8912896 | tf_op jit(solution)/shard_map/dot_general | solution.py:58
  23.5 1.3 fusion.57
  24.8 1.7 %fusion.10 = f32[128,2048]{1,0:T(8,128)} fusion(bf16[1024,2048]{1,0:T(8,128)(2,1)S(1)} %convolution_convert_fusion.1, f32[1024,128]{1,0:T(8,128)S(1)} %get-tuple-element.118, f32[128]{0:T(128)S(1)} %get-tuple-element.104), kind=kOutput, calls=%fused_computation.19 | convolution fusion | flops 537133056 | bytes 5767680 | tf_op jit(solution)/shard_map/dot_general | solution.py:65
  26.5 0.6 fusion.49
  27.2 0.4 fusion.7
  27.5 0.6 fusion.50
  28.4 0.4 scatter.25
  28.8 1.3 maximum_bitcast_fusion
  30.1 25.0 %all_to_all.9 = f32[16,8,2176]{2,1,0:T(8,128)S(1)} all-to-all(f32[16,8,2176]{2,1,0:T(8,128)S(1)} %maximum_bitcast_fusion), channel_id=1, replica_groups=mesh['pos'=16,'exp'=16] {'exp'}, dimensions={0} | all-to-all | bytes 2228224 | tf_op jit(solution)/shard_map/all_to_all | solution.py:73
  55.1 1.0 copy-done.1
  56.3 0.6 fusion.51
  57.3 0.2 fusion.48
  57.5 0.6 fusion.52
  58.4 1.4 fusion.6
  59.8 1.7 %collective-permute-start.2 = (f32[8,2176]{1,0:T(8,128)S(1)}, f32[8,2176]{1,0:T(8,128)S(1)}, u32[]{:S(2)}, u32[]{:S(2)}) collective-permute-start(f32[8,2176]{1,0:T(8,128)S(1)} %pad_maximum_fusion.2), channel_id=1, source_target_pairs={{0,16},{16,0},{32,48},{48,32},{64,80},{80,64},{96,112},{112,96},{1... | collective-permute-start | bytes 208904 | tf_op jit(solution)/shard_map/ppermute | solution.py:46
  61.5 0.6 compare_reduce_fusion
  62.1 1.4 collective-permute-done.2
  63.5 0.2 exponential_reduce_fusion.5
  63.8 0.7 slice_select_fusion.2
  64.5 5.6 %collective-permute-start.3 = (f32[8,2176]{1,0:T(8,128)S(1)}, f32[8,2176]{1,0:T(8,128)S(1)}, u32[]{:S(2)}, u32[]{:S(2)}) collective-permute-start(f32[8,2176]{1,0:T(8,128)S(1)} %scatter.30), channel_id=1, source_target_pairs={{0,32},{16,48},{32,0},{48,16},{64,96},{80,112},{96,64},{112,80},{1... | collective-permute-start | bytes 208904 | tf_op jit(solution)/shard_map/ppermute | solution.py:46
  70.1 1.7 %collective-permute-done.3 = f32[8,2176]{1,0:T(8,128)S(1)} collective-permute-done((f32[8,2176]{1,0:T(8,128)S(1)}, f32[8,2176]{1,0:T(8,128)S(1)}, u32[]{:S(2)}, u32[]{:S(2)}) %collective-permute-start.3) | collective-permute-done | bytes 69664 | tf_op jit(solution)/shard_map/ppermute | solution.py:46
  72.0 0.7 slice_select_fusion.1
  72.8 3.2 %collective-permute-start.4 = (f32[8,2176]{1,0:T(8,128)S(1)}, f32[8,2176]{1,0:T(8,128)S(1)}, u32[]{:S(2)}, u32[]{:S(2)}) collective-permute-start(f32[8,2176]{1,0:T(8,128)S(1)} %scatter.31), channel_id=1, source_target_pairs={{0,64},{16,80},{32,96},{48,112},{64,0},{80,16},{96,32},{112,48},{1... | collective-permute-start | bytes 208904 | tf_op jit(solution)/shard_map/ppermute | solution.py:46
  76.0 4.0 %collective-permute-done.4 = f32[8,2176]{1,0:T(8,128)S(1)} collective-permute-done((f32[8,2176]{1,0:T(8,128)S(1)}, f32[8,2176]{1,0:T(8,128)S(1)}, u32[]{:S(2)}, u32[]{:S(2)}) %collective-permute-start.4) | collective-permute-done | bytes 69664 | tf_op jit(solution)/shard_map/ppermute | solution.py:46
  80.2 0.7 slice_select_fusion
  81.0 2.8 %collective-permute-start.5 = (f32[8,2176]{1,0:T(8,128)S(1)}, f32[8,2176]{1,0:T(8,128)S(1)}, u32[]{:S(2)}, u32[]{:S(2)}) collective-permute-start(f32[8,2176]{1,0:T(8,128)S(1)} %scatter.34), channel_id=1, source_target_pairs={{0,128},{16,144},{32,160},{48,176},{64,192},{80,208},{96,224},{112... | collective-permute-start | bytes 208904 | tf_op jit(solution)/shard_map/ppermute | solution.py:46
  83.8 1.9 %collective-permute-done.5 = f32[8,2176]{1,0:T(8,128)S(1)} collective-permute-done((f32[8,2176]{1,0:T(8,128)S(1)}, f32[8,2176]{1,0:T(8,128)S(1)}, u32[]{:S(2)}, u32[]{:S(2)}) %collective-permute-start.5) | collective-permute-done | bytes 69664 | tf_op jit(solution)/shard_map/ppermute | solution.py:46
  86.0 0.2 slice_reduce_fusion
  86.1 3.0 %fusion = f32[8,2048]{1,0:T(8,128)S(1)} fusion(bf16[1,512,2048]{2,1,0:T(8,128)(2,1)} %param.25, bf16[1,2048,512]{2,1,0:T(8,128)(2,1)} %param.24, f32[8,2176]{1,0:T(8,128)S(1)} %multiply_add_fusion, f32[8]{0:T(128)S(1)} %slice_reduce_fusion), kind=kOutput, calls=%fused_computation.2 | convolution fusion | flops 33624064 | bytes 4325888 | tf_op jit(solution)/shard_map/dot_general | solution.py:87
  89.1 1.3 collective-permute-start.6
  90.5 1.8 %collective-permute-done.6 = f32[8,2048]{1,0:T(8,128)S(1)} collective-permute-done((f32[8,2048]{1,0:T(8,128)S(1)}, f32[8,2048]{1,0:T(8,128)S(1)}, u32[]{:S(2)}, u32[]{:S(2)}) %collective-permute-start.6) | collective-permute-done | bytes 65568 | tf_op jit(solution)/shard_map/ppermute | solution.py:28
  92.3 2.9 %collective-permute-start.7 = (f32[8,2048]{1,0:T(8,128)S(1)}, f32[8,2048]{1,0:T(8,128)S(1)}, u32[]{:S(2)}, u32[]{:S(2)}) collective-permute-start(f32[8,2048]{1,0:T(8,128)S(1)} %add.60), channel_id=1, source_target_pairs={{0,32},{16,48},{32,0},{48,16},{64,96},{80,112},{96,64},{112,80},{1... | collective-permute-start | bytes 196616 | tf_op jit(solution)/shard_map/ppermute | solution.py:28
  95.2 1.7 %collective-permute-done.7 = f32[8,2048]{1,0:T(8,128)S(1)} collective-permute-done((f32[8,2048]{1,0:T(8,128)S(1)}, f32[8,2048]{1,0:T(8,128)S(1)}, u32[]{:S(2)}, u32[]{:S(2)}) %collective-permute-start.7) | collective-permute-done | bytes 65568 | tf_op jit(solution)/shard_map/ppermute | solution.py:28
  96.9 3.2 %collective-permute-start.8 = (f32[8,2048]{1,0:T(8,128)S(1)}, f32[8,2048]{1,0:T(8,128)S(1)}, u32[]{:S(2)}, u32[]{:S(2)}) collective-permute-start(f32[8,2048]{1,0:T(8,128)S(1)} %add.61), channel_id=1, source_target_pairs={{0,64},{16,80},{32,96},{48,112},{64,0},{80,16},{96,32},{112,48},{1... | collective-permute-start | bytes 196616 | tf_op jit(solution)/shard_map/ppermute | solution.py:28
  100.1 4.3 %collective-permute-done.8 = f32[8,2048]{1,0:T(8,128)S(1)} collective-permute-done((f32[8,2048]{1,0:T(8,128)S(1)}, f32[8,2048]{1,0:T(8,128)S(1)}, u32[]{:S(2)}, u32[]{:S(2)}) %collective-permute-start.8) | collective-permute-done | bytes 65568 | tf_op jit(solution)/shard_map/ppermute | solution.py:28
  104.4 3.7 %collective-permute-start.9 = (f32[8,2048]{1,0:T(8,128)S(1)}, f32[8,2048]{1,0:T(8,128)S(1)}, u32[]{:S(2)}, u32[]{:S(2)}) collective-permute-start(f32[8,2048]{1,0:T(8,128)S(1)} %add.62), channel_id=1, source_target_pairs={{0,128},{16,144},{32,160},{48,176},{64,192},{80,208},{96,224},{112... | collective-permute-start | bytes 196616 | tf_op jit(solution)/shard_map/ppermute | solution.py:28
  108.1 1.7 %collective-permute-done.9 = f32[8,2048]{1,0:T(8,128)S(1)} collective-permute-done((f32[8,2048]{1,0:T(8,128)S(1)}, f32[8,2048]{1,0:T(8,128)S(1)}, u32[]{:S(2)}, u32[]{:S(2)}) %collective-permute-start.9) | collective-permute-done | bytes 65568 | tf_op jit(solution)/shard_map/ppermute | solution.py:28
  109.8 27.2 %all_gather.3 = bf16[128,2048]{1,0:T(8,128)(2,1)S(1)} all-gather(bf16[8,2048]{1,0:T(8,128)(2,1)S(1)} %add_convert_fusion), channel_id=1, replica_groups=mesh['pos'=16,'exp'=16] {'exp'}, dimensions={0}, use_global_device_ids=true | all-gather | bytes 557056 | tf_op jit(solution)/shard_map/all_gather | solution.py:94
  137.0 4.3 %convolution_convert_fusion = bf16[1024,2048]{1,0:T(8,128)(2,1)} fusion(bf16[128,2048]{1,0:T(8,128)(2,1)S(1)} %all_gather.3, f32[1024,128]{1,0:T(8,128)} %copy-done.2, f32[1024]{0:T(1024)S(1)} %get-tuple-element.101, f32[1024]{0:T(1024)S(1)} %get-tuple-element.103), kind=kOutput, calls=%fused_computation | convolution fusion | flops 539361280 | bytes 5251072 | tf_op jit(solution)/shard_map/dot_general | solution.py:92
  141.3 7.2 %reshape.247 = bf16[256,4,2048]{2,1,0:T(4,128)(2,1)} reshape(bf16[1024,2048]{1,0:T(8,128)(2,1)} %convolution_convert_fusion) | data formatting | bytes 8388608 | tf_op jit(solution)/shard_map/reshape | solution.py:97
  (35 shorter events, 2.1 us)
Async XLA Ops:
  0.0 18.4 %copy-start = (bf16[3,256,2048]{2,1,0:T(8,128)(2,1)S(1)}, bf16[3,256,2048]{2,1,0:T(8,128)(2,1)}, u32[]{:S(2)}) copy-start(bf16[3,256,2048]{2,1,0:T(8,128)(2,1)} %param.22) | copy-start | bytes 9437188
  0.9 7.9 %collective-permute-start = (bf16[1,4,256]{2,1,0:T(4,128)(2,1)S(1)}, bf16[1,4,256]{2,1,0:T(4,128)(2,1)S(1)}, u32[]{:S(2)}, u32[]{:S(2)}) collective-permute-start(bf16[1,4,256]{2,1,0:T(4,128)(2,1)S(1)} %get-tuple-element.116), channel_id=1, source_target_pairs={{0,1},{1,2},{2,3},{3,4},{4,5},{5,6},{6,7},{7,8},{8,9},{9,10},{10,1... | collective-permute-start | bytes 6152 | tf_op jit(solution)/shard_map/ppermute | solution.py:17
  5.5 4.9 %collective-permute-start.1 = (bf16[1,4,256]{2,1,0:T(4,128)(2,1)S(1)}, bf16[1,4,256]{2,1,0:T(4,128)(2,1)S(1)}, u32[]{:S(2)}, u32[]{:S(2)}) collective-permute-start(bf16[1,4,256]{2,1,0:T(4,128)(2,1)S(1)} %get-tuple-element.117), channel_id=1, source_target_pairs={{1,0},{2,1},{3,2},{4,3},{5,4},{6,5},{7,6},{8,7},{9,8},{10,9},{11,1... | collective-permute-start | bytes 6152 | tf_op jit(solution)/shard_map/ppermute | solution.py:18
  18.4 5.1 %copy-start.3 = (bf16[2048,128]{1,0:T(8,128)(2,1)S(1)}, bf16[2048,128]{1,0:T(8,128)(2,1)}, u32[]{:S(2)}) copy-start(bf16[2048,128]{1,0:T(8,128)(2,1)} %param.23) | copy-start | bytes 1572868
  24.8 2.4 %copy-start.2 = (f32[1024,128]{1,0:T(8,128)}, f32[1024,128]{1,0:T(8,128)S(1)}, u32[]{:S(2)}) copy-start(f32[1024,128]{1,0:T(8,128)S(1)} %get-tuple-element.118) | copy-start | bytes 1572868
  55.1 1.0 copy-start.1
  59.8 3.8 %collective-permute-start.2 = (f32[8,2176]{1,0:T(8,128)S(1)}, f32[8,2176]{1,0:T(8,128)S(1)}, u32[]{:S(2)}, u32[]{:S(2)}) collective-permute-start(f32[8,2176]{1,0:T(8,128)S(1)} %pad_maximum_fusion.2), channel_id=1, source_target_pairs={{0,16},{16,0},{32,48},{48,32},{64,80},{80,64},{96,112},{112,96},{1... | collective-permute-start | bytes 208904 | tf_op jit(solution)/shard_map/ppermute | solution.py:46
  64.5 7.3 %collective-permute-start.3 = (f32[8,2176]{1,0:T(8,128)S(1)}, f32[8,2176]{1,0:T(8,128)S(1)}, u32[]{:S(2)}, u32[]{:S(2)}) collective-permute-start(f32[8,2176]{1,0:T(8,128)S(1)} %scatter.30), channel_id=1, source_target_pairs={{0,32},{16,48},{32,0},{48,16},{64,96},{80,112},{96,64},{112,80},{1... | collective-permute-start | bytes 208904 | tf_op jit(solution)/shard_map/ppermute | solution.py:46
  72.8 7.2 %collective-permute-start.4 = (f32[8,2176]{1,0:T(8,128)S(1)}, f32[8,2176]{1,0:T(8,128)S(1)}, u32[]{:S(2)}, u32[]{:S(2)}) collective-permute-start(f32[8,2176]{1,0:T(8,128)S(1)} %scatter.31), channel_id=1, source_target_pairs={{0,64},{16,80},{32,96},{48,112},{64,0},{80,16},{96,32},{112,48},{1... | collective-permute-start | bytes 208904 | tf_op jit(solution)/shard_map/ppermute | solution.py:46
  81.0 4.8 %collective-permute-start.5 = (f32[8,2176]{1,0:T(8,128)S(1)}, f32[8,2176]{1,0:T(8,128)S(1)}, u32[]{:S(2)}, u32[]{:S(2)}) collective-permute-start(f32[8,2176]{1,0:T(8,128)S(1)} %scatter.34), channel_id=1, source_target_pairs={{0,128},{16,144},{32,160},{48,176},{64,192},{80,208},{96,224},{112... | collective-permute-start | bytes 208904 | tf_op jit(solution)/shard_map/ppermute | solution.py:46
  89.1 3.1 %collective-permute-start.6 = (f32[8,2048]{1,0:T(8,128)S(1)}, f32[8,2048]{1,0:T(8,128)S(1)}, u32[]{:S(2)}, u32[]{:S(2)}) collective-permute-start(f32[8,2048]{1,0:T(8,128)S(1)} %fusion), channel_id=1, source_target_pairs={{0,16},{16,0},{32,48},{48,32},{64,80},{80,64},{96,112},{112,96},{1... | collective-permute-start | bytes 196616 | tf_op jit(solution)/shard_map/ppermute | solution.py:28
  92.3 4.6 %collective-permute-start.7 = (f32[8,2048]{1,0:T(8,128)S(1)}, f32[8,2048]{1,0:T(8,128)S(1)}, u32[]{:S(2)}, u32[]{:S(2)}) collective-permute-start(f32[8,2048]{1,0:T(8,128)S(1)} %add.60), channel_id=1, source_target_pairs={{0,32},{16,48},{32,0},{48,16},{64,96},{80,112},{96,64},{112,80},{1... | collective-permute-start | bytes 196616 | tf_op jit(solution)/shard_map/ppermute | solution.py:28
  96.9 7.6 %collective-permute-start.8 = (f32[8,2048]{1,0:T(8,128)S(1)}, f32[8,2048]{1,0:T(8,128)S(1)}, u32[]{:S(2)}, u32[]{:S(2)}) collective-permute-start(f32[8,2048]{1,0:T(8,128)S(1)} %add.61), channel_id=1, source_target_pairs={{0,64},{16,80},{32,96},{48,112},{64,0},{80,16},{96,32},{112,48},{1... | collective-permute-start | bytes 196616 | tf_op jit(solution)/shard_map/ppermute | solution.py:28
  104.4 5.4 %collective-permute-start.9 = (f32[8,2048]{1,0:T(8,128)S(1)}, f32[8,2048]{1,0:T(8,128)S(1)}, u32[]{:S(2)}, u32[]{:S(2)}) collective-permute-start(f32[8,2048]{1,0:T(8,128)S(1)} %add.62), channel_id=1, source_target_pairs={{0,128},{16,144},{32,160},{48,176},{64,192},{80,208},{96,224},{112... | collective-permute-start | bytes 196616 | tf_op jit(solution)/shard_map/ppermute | solution.py:28

commit v4 on v3

--- a/solution.py
+++ b/solution.py
@@ -51,10 +51,10 @@
 def per_device(patches, conv_weight, phi, w_in, w_out):
     channels, periods, samples = patches.shape
     every = ("pos", "exp")
-    padded = with_halo(patches, ((every, 0),), 1)
-    window = jnp.concatenate([padded[offset : offset + channels] for offset in range(3)], axis=2)
+    padded = with_halo(jnp.swapaxes(patches, 0, 1), ((every, 1),), 1)
+    window = jnp.concatenate([padded[:, offset : offset + channels] for offset in range(3)], axis=2)
+    window = window.reshape(periods * channels, 3 * samples)
     taps = conv_weight.reshape(3 * samples, D)
-    window = window.reshape(channels * periods, 3 * samples)
     flat = jnp.dot(window, taps, preferred_element_type=jnp.float32).astype(jnp.bfloat16)
     logits = jnp.dot(flat, phi, preferred_element_type=jnp.float32)
     slots = logits.shape[1]
@@ -94,7 +94,7 @@
         lax.all_gather(slot_out, "exp", axis=0, tiled=True),
         preferred_element_type=jnp.float32,
     )
-    return mixed.astype(jnp.bfloat16).reshape(channels, periods, D)
+    return jnp.swapaxes(mixed.astype(jnp.bfloat16).reshape(periods, channels, D), 0, 1)
 
 
 def solution(mesh):

time: 149 us -> 136 us (0.913)
  local copies, waits for them, and re-layouts: 14.3 us -> 9.09 us
  other arithmetic: 15.1 us -> 11.2 us
  matrix products: 15.4 us -> 12.1 us
    reshape x2 -> x1, local copies, waits for them, and re-layouts: 10.9 us -> 5.25 us  [per_device(): mixed.astype(jnp.bfloat16).reshape(periods, channels, D)]
    concatenate x1, other arithmetic: 4.24 us -> 0.27 us  [per_device(): jnp.concatenate([padded[:, offset:offset + channels] for offset in range(...]
    dot_general x1, matrix products: 4.3 us -> 2.37 us  [per_device(): jnp.dot(combine, lax.all_gather(slot_out, 'exp', axis=0, tiled=True), pre...]
where the time goes in v4:
time: 136 us
  blocking collectives  52.4 us (39%)
  starting transfers between devices  30.9 us (23%)
  waiting for transfers between devices  20.1 us (15%)
  matrix products  12.1 us (9%)
  other arithmetic  11.2 us (8%)
  local copies, waits for them, and re-layouts  9.09 us (7%)
    all_gather x1, blocking collectives, per_device(): lax.all_gather(slot_out, 'exp', axis=0, tiled=True)  27.4 us
    all_to_all x1, blocking collectives, per_device(): lax.all_to_all(packed, 'exp', 0, 0, tiled=True)  25 us
    ppermute x4, starting transfers between devices, butterfly_softmax_sum(): value = merge(value, lax.ppermute(value, axis, pairs))  13.4 us
    ppermute x4, starting transfers between devices, butterfly_sum(): value = value + lax.ppermute(value, axis, pairs)  11.1 us
    ppermute x4, waiting for transfers between devices, butterfly_sum(): value = value + lax.ppermute(value, axis, pairs)  9.47 us
    ppermute x4, waiting for transfers between devices, butterfly_softmax_sum(): value = merge(value, lax.ppermute(value, axis, pairs))  8.97 us
    reshape x1, local copies, waits for them, and re-layouts, per_device(): mixed.astype(jnp.bfloat16).reshape(periods, channels, D)  5.25 us
    another operation x7, other arithmetic  4.53 us
  transfers between devices with their start and end apart: 10, of which 9 were waited for; matrix products, arithmetic and copies ran while one was open for 1% of the time, Pallas kernels for 0%

profile of v4, /device:TPU:1, one launch (start us, length us, event | category | flops | bytes accessed | tf_op | source)
XLA Modules:
  0.0 136.0 jit_solution(183512765969925446)
XLA Ops:
  0.0 1.3 copy.64
  1.3 4.5 %collective-permute-start = (bf16[4,1,256]{2,1,0:T(2,128)(2,1)S(1)}, bf16[4,1,256]{2,1,0:T(2,128)(2,1)S(1)}, u32[]{:S(2)}, u32[]{:S(2)}) collective-permute-start(bf16[4,1,256]{2,1,0:T(2,128)(2,1)S(1)} %get-tuple-element.116), channel_id=1, source_target_pairs={{0,1},{1,2},{2,3},{3,4},{4,5},{5,6},{6,7},{7,8},{8,9},{9,10},{10,1... | collective-permute-start | bytes 6152 | tf_op jit(solution)/shard_map/ppermute | solution.py:17
  5.8 1.9 %collective-permute-start.1 = (bf16[4,1,256]{2,1,0:T(2,128)(2,1)S(1)}, bf16[4,1,256]{2,1,0:T(2,128)(2,1)S(1)}, u32[]{:S(2)}, u32[]{:S(2)}) collective-permute-start(bf16[4,1,256]{2,1,0:T(2,128)(2,1)S(1)} %get-tuple-element.117), channel_id=1, source_target_pairs={{1,0},{2,1},{3,2},{4,3},{5,4},{6,5},{7,6},{8,7},{9,8},{10,9},{11,1... | collective-permute-start | bytes 6152 | tf_op jit(solution)/shard_map/ppermute | solution.py:18
  7.7 0.7 compare_reduce_fusion.2
  8.4 0.6 compare_reduce_fusion.1
  9.1 1.6 %collective-permute-done.1 = bf16[4,1,256]{2,1,0:T(2,128)(2,1)S(1)} collective-permute-done((bf16[4,1,256]{2,1,0:T(2,128)(2,1)S(1)}, bf16[4,1,256]{2,1,0:T(2,128)(2,1)S(1)}, u32[]{:S(2)}, u32[]{:S(2)}) %collective-permute-start.1) | collective-permute-done | bytes 2080 | tf_op jit(solution)/shard_map/ppermute | solution.py:18
  10.7 0.3 fusion.4
  11.0 3.6 %convolution_convert_fusion.1 = bf16[1024,2048]{1,0:T(8,128)(2,1)S(1)} fusion(bf16[1024,768]{1,0:T(8,128)(2,1)S(1)} %bitcast.53, bf16[768,2048]{1,0:T(8,128)(2,1)S(1)} %bitcast.49), kind=kOutput, calls=%fused_computation.2 | convolution fusion | flops 3223322624 | bytes 8912896 | tf_op jit(solution)/shard_map/dot_general | solution.py:58
  14.7 1.3 fusion.57
  16.0 1.7 %fusion.10 = f32[128,2048]{1,0:T(8,128)} fusion(bf16[1024,2048]{1,0:T(8,128)(2,1)S(1)} %convolution_convert_fusion.1, f32[1024,128]{1,0:T(8,128)S(1)} %get-tuple-element.118, f32[128]{0:T(128)S(1)} %get-tuple-element.104), kind=kOutput, calls=%fused_computation.21 | convolution fusion | flops 537133056 | bytes 5767680 | tf_op jit(solution)/shard_map/dot_general | solution.py:65
  17.7 0.7 fusion.49
  18.4 0.4 fusion.7
  18.8 0.6 fusion.50
  19.6 0.4 scatter.25
  20.0 1.3 maximum_bitcast_fusion
  21.3 25.0 %all_to_all.9 = f32[16,8,2176]{2,1,0:T(8,128)S(1)} all-to-all(f32[16,8,2176]{2,1,0:T(8,128)S(1)} %maximum_bitcast_fusion), channel_id=1, replica_groups=mesh['pos'=16,'exp'=16] {'exp'}, dimensions={0} | all-to-all | bytes 2228224 | tf_op jit(solution)/shard_map/all_to_all | solution.py:73
  46.4 1.0 copy-done.1
  47.5 0.7 fusion.51
  48.6 0.2 fusion.48
  48.8 0.6 fusion.52
  49.6 1.4 %fusion.6 = f32[8,2048]{1,0:T(8,128)S(1)} fusion(f32[16,8,2176]{2,1,0:T(8,128)} %copy-done.1, f32[16,8]{1,0:T(8,128)S(1)} %copy.53), kind=kLoop, calls=%fused_computation.13 | loop fusion | flops 507904 | bytes 1114624 | tf_op jit(solution)/shard_map/reduce_sum | solution.py:77
  51.0 1.7 %collective-permute-start.2 = (f32[8,2176]{1,0:T(8,128)S(1)}, f32[8,2176]{1,0:T(8,128)S(1)}, u32[]{:S(2)}, u32[]{:S(2)}) collective-permute-start(f32[8,2176]{1,0:T(8,128)S(1)} %pad_maximum_fusion.2), channel_id=1, source_target_pairs={{0,16},{16,0},{32,48},{48,32},{64,80},{80,64},{96,112},{112,96},{1... | collective-permute-start | bytes 208904 | tf_op jit(solution)/shard_map/ppermute | solution.py:46
  52.7 0.6 compare_reduce_fusion
  53.4 1.4 %collective-permute-done.2 = f32[8,2176]{1,0:T(8,128)S(1)} collective-permute-done((f32[8,2176]{1,0:T(8,128)S(1)}, f32[8,2176]{1,0:T(8,128)S(1)}, u32[]{:S(2)}, u32[]{:S(2)}) %collective-permute-start.2) | collective-permute-done | bytes 69664 | tf_op jit(solution)/shard_map/ppermute | solution.py:46
  54.7 0.2 exponential_reduce_fusion.5
  55.0 0.7 slice_select_fusion.2
  55.7 5.6 %collective-permute-start.3 = (f32[8,2176]{1,0:T(8,128)S(1)}, f32[8,2176]{1,0:T(8,128)S(1)}, u32[]{:S(2)}, u32[]{:S(2)}) collective-permute-start(f32[8,2176]{1,0:T(8,128)S(1)} %scatter.30), channel_id=1, source_target_pairs={{0,32},{16,48},{32,0},{48,16},{64,96},{80,112},{96,64},{112,80},{1... | collective-permute-start | bytes 208904 | tf_op jit(solution)/shard_map/ppermute | solution.py:46
  61.3 1.7 %collective-permute-done.3 = f32[8,2176]{1,0:T(8,128)S(1)} collective-permute-done((f32[8,2176]{1,0:T(8,128)S(1)}, f32[8,2176]{1,0:T(8,128)S(1)}, u32[]{:S(2)}, u32[]{:S(2)}) %collective-permute-start.3) | collective-permute-done | bytes 69664 | tf_op jit(solution)/shard_map/ppermute | solution.py:46
  63.0 0.2 exponential_reduce_fusion.3
  63.3 0.7 slice_select_fusion.1
  64.0 3.2 %collective-permute-start.4 = (f32[8,2176]{1,0:T(8,128)S(1)}, f32[8,2176]{1,0:T(8,128)S(1)}, u32[]{:S(2)}, u32[]{:S(2)}) collective-permute-start(f32[8,2176]{1,0:T(8,128)S(1)} %scatter.31), channel_id=1, source_target_pairs={{0,64},{16,80},{32,96},{48,112},{64,0},{80,16},{96,32},{112,48},{1... | collective-permute-start | bytes 208904 | tf_op jit(solution)/shard_map/ppermute | solution.py:46
  67.2 4.0 %collective-permute-done.4 = f32[8,2176]{1,0:T(8,128)S(1)} collective-permute-done((f32[8,2176]{1,0:T(8,128)S(1)}, f32[8,2176]{1,0:T(8,128)S(1)}, u32[]{:S(2)}, u32[]{:S(2)}) %collective-permute-start.4) | collective-permute-done | bytes 69664 | tf_op jit(solution)/shard_map/ppermute | solution.py:46
  71.4 0.7 slice_select_fusion
  72.2 2.8 %collective-permute-start.5 = (f32[8,2176]{1,0:T(8,128)S(1)}, f32[8,2176]{1,0:T(8,128)S(1)}, u32[]{:S(2)}, u32[]{:S(2)}) collective-permute-start(f32[8,2176]{1,0:T(8,128)S(1)} %scatter.34), channel_id=1, source_target_pairs={{0,128},{16,144},{32,160},{48,176},{64,192},{80,208},{96,224},{112... | collective-permute-start | bytes 208904 | tf_op jit(solution)/shard_map/ppermute | solution.py:46
  75.0 1.9 %collective-permute-done.5 = f32[8,2176]{1,0:T(8,128)S(1)} collective-permute-done((f32[8,2176]{1,0:T(8,128)S(1)}, f32[8,2176]{1,0:T(8,128)S(1)}, u32[]{:S(2)}, u32[]{:S(2)}) %collective-permute-start.5) | collective-permute-done | bytes 69664 | tf_op jit(solution)/shard_map/ppermute | solution.py:46
  77.2 0.2 slice_reduce_fusion
  77.4 3.0 %fusion = f32[8,2048]{1,0:T(8,128)S(1)} fusion(bf16[1,512,2048]{2,1,0:T(8,128)(2,1)} %param.25, bf16[1,2048,512]{2,1,0:T(8,128)(2,1)} %param.24, f32[8,2176]{1,0:T(8,128)S(1)} %multiply_add_fusion, f32[8]{0:T(128)S(1)} %slice_reduce_fusion), kind=kOutput, calls=%fused_computation.3 | convolution fusion | flops 33624064 | bytes 4325888 | tf_op jit(solution)/shard_map/dot_general | solution.py:87
  80.4 1.3 collective-permute-start.6
  81.7 1.8 %collective-permute-done.6 = f32[8,2048]{1,0:T(8,128)S(1)} collective-permute-done((f32[8,2048]{1,0:T(8,128)S(1)}, f32[8,2048]{1,0:T(8,128)S(1)}, u32[]{:S(2)}, u32[]{:S(2)}) %collective-permute-start.6) | collective-permute-done | bytes 65568 | tf_op jit(solution)/shard_map/ppermute | solution.py:28
  83.5 2.9 %collective-permute-start.7 = (f32[8,2048]{1,0:T(8,128)S(1)}, f32[8,2048]{1,0:T(8,128)S(1)}, u32[]{:S(2)}, u32[]{:S(2)}) collective-permute-start(f32[8,2048]{1,0:T(8,128)S(1)} %add.60), channel_id=1, source_target_pairs={{0,32},{16,48},{32,0},{48,16},{64,96},{80,112},{96,64},{112,80},{1... | collective-permute-start | bytes 196616 | tf_op jit(solution)/shard_map/ppermute | solution.py:28
  86.4 1.7 %collective-permute-done.7 = f32[8,2048]{1,0:T(8,128)S(1)} collective-permute-done((f32[8,2048]{1,0:T(8,128)S(1)}, f32[8,2048]{1,0:T(8,128)S(1)}, u32[]{:S(2)}, u32[]{:S(2)}) %collective-permute-start.7) | collective-permute-done | bytes 65568 | tf_op jit(solution)/shard_map/ppermute | solution.py:28
  88.1 3.2 %collective-permute-start.8 = (f32[8,2048]{1,0:T(8,128)S(1)}, f32[8,2048]{1,0:T(8,128)S(1)}, u32[]{:S(2)}, u32[]{:S(2)}) collective-permute-start(f32[8,2048]{1,0:T(8,128)S(1)} %add.61), channel_id=1, source_target_pairs={{0,64},{16,80},{32,96},{48,112},{64,0},{80,16},{96,32},{112,48},{1... | collective-permute-start | bytes 196616 | tf_op jit(solution)/shard_map/ppermute | solution.py:28
  91.3 4.3 %collective-permute-done.8 = f32[8,2048]{1,0:T(8,128)S(1)} collective-permute-done((f32[8,2048]{1,0:T(8,128)S(1)}, f32[8,2048]{1,0:T(8,128)S(1)}, u32[]{:S(2)}, u32[]{:S(2)}) %collective-permute-start.8) | collective-permute-done | bytes 65568 | tf_op jit(solution)/shard_map/ppermute | solution.py:28
  95.6 3.7 %collective-permute-start.9 = (f32[8,2048]{1,0:T(8,128)S(1)}, f32[8,2048]{1,0:T(8,128)S(1)}, u32[]{:S(2)}, u32[]{:S(2)}) collective-permute-start(f32[8,2048]{1,0:T(8,128)S(1)} %add.62), channel_id=1, source_target_pairs={{0,128},{16,144},{32,160},{48,176},{64,192},{80,208},{96,224},{112... | collective-permute-start | bytes 196616 | tf_op jit(solution)/shard_map/ppermute | solution.py:28
  99.4 1.7 %collective-permute-done.9 = f32[8,2048]{1,0:T(8,128)S(1)} collective-permute-done((f32[8,2048]{1,0:T(8,128)S(1)}, f32[8,2048]{1,0:T(8,128)S(1)}, u32[]{:S(2)}, u32[]{:S(2)}) %collective-permute-start.9) | collective-permute-done | bytes 65568 | tf_op jit(solution)/shard_map/ppermute | solution.py:28
  101.0 27.4 %all_gather.3 = bf16[128,2048]{1,0:T(8,128)(2,1)S(1)} all-gather(bf16[8,2048]{1,0:T(8,128)(2,1)S(1)} %add_convert_fusion), channel_id=1, replica_groups=mesh['pos'=16,'exp'=16] {'exp'}, dimensions={0}, use_global_device_ids=true | all-gather | bytes 557056 | tf_op jit(solution)/shard_map/all_gather | solution.py:94
  128.4 2.4 %convolution_convert_fusion = bf16[1024,2048]{1,0:T(8,128)(2,1)S(1)} fusion(bf16[128,2048]{1,0:T(8,128)(2,1)S(1)} %all_gather.3, f32[1024,128]{1,0:T(8,128)} %copy-done.2, f32[1024]{0:T(1024)S(1)} %get-tuple-element.101, f32[1024]{0:T(1024)S(1)} %get-tuple-element.103), kind=kOutput, calls=%fused_computation.1 | convolution fusion | flops 539361280 | bytes 5251072 | tf_op jit(solution)/shard_map/dot_general | solution.py:92
  130.8 5.3 %copy.63 = bf16[4,256,2048]{2,0,1:T(4,128)(2,1)} copy(bf16[4,256,2048]{2,1,0:T(8,128)(2,1)S(1)} %bitcast.50) | data formatting | bytes 8388608 | tf_op jit(solution)/shard_map/reshape | solution.py:97
  (35 shorter events, 1.9 us)
Async XLA Ops:
  0.0 11.0 %copy-start = (bf16[3,256,2048]{2,1,0:T(8,128)(2,1)S(1)}, bf16[3,256,2048]{2,1,0:T(8,128)(2,1)}, u32[]{:S(2)}) copy-start(bf16[3,256,2048]{2,1,0:T(8,128)(2,1)} %param.22) | copy-start | bytes 9437188
  1.3 7.8 %collective-permute-start = (bf16[4,1,256]{2,1,0:T(2,128)(2,1)S(1)}, bf16[4,1,256]{2,1,0:T(2,128)(2,1)S(1)}, u32[]{:S(2)}, u32[]{:S(2)}) collective-permute-start(bf16[4,1,256]{2,1,0:T(2,128)(2,1)S(1)} %get-tuple-element.116), channel_id=1, source_target_pairs={{0,1},{1,2},{2,3},{3,4},{4,5},{5,6},{6,7},{7,8},{8,9},{9,10},{10,1... | collective-permute-start | bytes 6152 | tf_op jit(solution)/shard_map/ppermute | solution.py:17
  5.8 4.9 %collective-permute-start.1 = (bf16[4,1,256]{2,1,0:T(2,128)(2,1)S(1)}, bf16[4,1,256]{2,1,0:T(2,128)(2,1)S(1)}, u32[]{:S(2)}, u32[]{:S(2)}) collective-permute-start(bf16[4,1,256]{2,1,0:T(2,128)(2,1)S(1)} %get-tuple-element.117), channel_id=1, source_target_pairs={{1,0},{2,1},{3,2},{4,3},{5,4},{6,5},{7,6},{8,7},{9,8},{10,9},{11,1... | collective-permute-start | bytes 6152 | tf_op jit(solution)/shard_map/ppermute | solution.py:18
  11.0 3.7 %copy-start.3 = (bf16[2048,128]{1,0:T(8,128)(2,1)S(1)}, bf16[2048,128]{1,0:T(8,128)(2,1)}, u32[]{:S(2)}) copy-start(bf16[2048,128]{1,0:T(8,128)(2,1)} %param.23) | copy-start | bytes 1572868
  16.0 2.8 %copy-start.2 = (f32[1024,128]{1,0:T(8,128)}, f32[1024,128]{1,0:T(8,128)S(1)}, u32[]{:S(2)}) copy-start(f32[1024,128]{1,0:T(8,128)S(1)} %get-tuple-element.118) | copy-start | bytes 1572868
  46.4 1.0 copy-start.1
  51.0 3.7 %collective-permute-start.2 = (f32[8,2176]{1,0:T(8,128)S(1)}, f32[8,2176]{1,0:T(8,128)S(1)}, u32[]{:S(2)}, u32[]{:S(2)}) collective-permute-start(f32[8,2176]{1,0:T(8,128)S(1)} %pad_maximum_fusion.2), channel_id=1, source_target_pairs={{0,16},{16,0},{32,48},{48,32},{64,80},{80,64},{96,112},{112,96},{1... | collective-permute-start | bytes 208904 | tf_op jit(solution)/shard_map/ppermute | solution.py:46
  55.7 7.3 %collective-permute-start.3 = (f32[8,2176]{1,0:T(8,128)S(1)}, f32[8,2176]{1,0:T(8,128)S(1)}, u32[]{:S(2)}, u32[]{:S(2)}) collective-permute-start(f32[8,2176]{1,0:T(8,128)S(1)} %scatter.30), channel_id=1, source_target_pairs={{0,32},{16,48},{32,0},{48,16},{64,96},{80,112},{96,64},{112,80},{1... | collective-permute-start | bytes 208904 | tf_op jit(solution)/shard_map/ppermute | solution.py:46
  64.0 7.2 %collective-permute-start.4 = (f32[8,2176]{1,0:T(8,128)S(1)}, f32[8,2176]{1,0:T(8,128)S(1)}, u32[]{:S(2)}, u32[]{:S(2)}) collective-permute-start(f32[8,2176]{1,0:T(8,128)S(1)} %scatter.31), channel_id=1, source_target_pairs={{0,64},{16,80},{32,96},{48,112},{64,0},{80,16},{96,32},{112,48},{1... | collective-permute-start | bytes 208904 | tf_op jit(solution)/shard_map/ppermute | solution.py:46
  72.2 4.8 %collective-permute-start.5 = (f32[8,2176]{1,0:T(8,128)S(1)}, f32[8,2176]{1,0:T(8,128)S(1)}, u32[]{:S(2)}, u32[]{:S(2)}) collective-permute-start(f32[8,2176]{1,0:T(8,128)S(1)} %scatter.34), channel_id=1, source_target_pairs={{0,128},{16,144},{32,160},{48,176},{64,192},{80,208},{96,224},{112... | collective-permute-start | bytes 208904 | tf_op jit(solution)/shard_map/ppermute | solution.py:46
  80.4 3.1 %collective-permute-start.6 = (f32[8,2048]{1,0:T(8,128)S(1)}, f32[8,2048]{1,0:T(8,128)S(1)}, u32[]{:S(2)}, u32[]{:S(2)}) collective-permute-start(f32[8,2048]{1,0:T(8,128)S(1)} %fusion), channel_id=1, source_target_pairs={{0,16},{16,0},{32,48},{48,32},{64,80},{80,64},{96,112},{112,96},{1... | collective-permute-start | bytes 196616 | tf_op jit(solution)/shard_map/ppermute | solution.py:28
  83.5 4.6 %collective-permute-start.7 = (f32[8,2048]{1,0:T(8,128)S(1)}, f32[8,2048]{1,0:T(8,128)S(1)}, u32[]{:S(2)}, u32[]{:S(2)}) collective-permute-start(f32[8,2048]{1,0:T(8,128)S(1)} %add.60), channel_id=1, source_target_pairs={{0,32},{16,48},{32,0},{48,16},{64,96},{80,112},{96,64},{112,80},{1... | collective-permute-start | bytes 196616 | tf_op jit(solution)/shard_map/ppermute | solution.py:28
  88.1 7.5 %collective-permute-start.8 = (f32[8,2048]{1,0:T(8,128)S(1)}, f32[8,2048]{1,0:T(8,128)S(1)}, u32[]{:S(2)}, u32[]{:S(2)}) collective-permute-start(f32[8,2048]{1,0:T(8,128)S(1)} %add.61), channel_id=1, source_target_pairs={{0,64},{16,80},{32,96},{48,112},{64,0},{80,16},{96,32},{112,48},{1... | collective-permute-start | bytes 196616 | tf_op jit(solution)/shard_map/ppermute | solution.py:28
  95.6 5.4 %collective-permute-start.9 = (f32[8,2048]{1,0:T(8,128)S(1)}, f32[8,2048]{1,0:T(8,128)S(1)}, u32[]{:S(2)}, u32[]{:S(2)}) collective-permute-start(f32[8,2048]{1,0:T(8,128)S(1)} %add.62), channel_id=1, source_target_pairs={{0,128},{16,144},{32,160},{48,176},{64,192},{80,208},{96,224},{112... | collective-permute-start | bytes 196616 | tf_op jit(solution)/shard_map/ppermute | solution.py:28

commit v5 on v4

--- a/solution.py
+++ b/solution.py
@@ -48,6 +48,22 @@
     return value
 
 
+def exchange(value, axis):
+    count = lax.axis_size(axis)
+    spread = jnp.broadcast_to(value[None], (count,) + value.shape)
+    return lax.all_to_all(spread, axis, 0, 0, tiled=True)
+
+
+def merge_all(blocks):
+    peaks = blocks[:, :, D]
+    peak = jnp.max(peaks, axis=0)
+    scale = jnp.exp(peaks - peak)
+    sums = jnp.sum(blocks[:, :, :D] * scale[:, :, None], axis=0)
+    total = jnp.sum(blocks[:, :, D + 1] * scale, axis=0)
+    extra = jnp.zeros((blocks.shape[1], blocks.shape[2] - D), jnp.float32)
+    return jnp.concatenate([sums, extra.at[:, 0].set(peak).at[:, 1].set(total)], axis=1)
+
+
 def per_device(patches, conv_weight, phi, w_in, w_out):
     channels, periods, samples = patches.shape
     every = ("pos", "exp")
@@ -71,21 +87,14 @@
     packed = jnp.concatenate([every_slot, extra], axis=1)
     groups = lax.axis_size("exp")
     mine = lax.all_to_all(packed, "exp", 0, 0, tiled=True).reshape(groups, SLOTS_PER, -1)
-    peaks = mine[:, :, D]
-    peak = jnp.max(peaks, axis=0)
-    scale = jnp.exp(peaks - peak)
-    sums = jnp.sum(mine[:, :, :D] * scale[:, :, None], axis=0)
-    total = jnp.sum(mine[:, :, D + 1] * scale, axis=0)
-    owned = jnp.concatenate(
-        [sums, jnp.zeros((SLOTS_PER, 128), jnp.float32).at[:, 0].set(peak).at[:, 1].set(total)], axis=1
-    )
-    owned = butterfly_softmax_sum(owned, "pos")
+    owned = merge_all(mine)
+    owned = merge_all(exchange(owned, "pos"))
     slot_in = (owned[:, :D] / owned[:, D + 1 : D + 2]).astype(jnp.bfloat16)
     hidden = jax.nn.gelu(
         jnp.dot(slot_in, w_in[0], preferred_element_type=jnp.float32), approximate=True
     ).astype(jnp.bfloat16)
     expert_term = jnp.dot(hidden, w_out[0], preferred_element_type=jnp.float32)
-    slot_out = butterfly_sum(expert_term, "pos").astype(jnp.bfloat16)
+    slot_out = jnp.sum(exchange(expert_term, "pos"), axis=0).astype(jnp.bfloat16)
     row_peak = jnp.max(logits, axis=1, keepdims=True)
     row_weights = jnp.exp(logits - row_peak)
     combine = (row_weights / jnp.sum(row_weights, axis=1, keepdims=True)).astype(jnp.bfloat16)

time: 136 us -> 161 us (1.18)
  blocking collectives: 52.4 us -> 117 us
  starting transfers between devices: 30.9 us -> 6.42 us
  waiting for transfers between devices: 20.1 us -> 1.65 us
  local copies, waits for them, and re-layouts: 9.09 us -> 11.3 us
    all_to_all x0 -> x2, blocking collectives: none -> 70.6 us  [exchange(): return lax.all_to_all(spread, axis, 0, 0, tiled=True)]
    ppermute x8 -> x0, starting transfers between devices: 24.5 us -> none  [the longest x4 13.4 us: butterfly_softmax_sum(): value = merge(value, lax.ppermute(value, axis, pairs))]
    ppermute x8 -> x0, waiting for transfers between devices: 18.4 us -> none  [the longest x4 9.47 us: butterfly_sum(): value = value + lax.ppermute(value, axis, pairs)]
    all_gather x1, blocking collectives: 27.4 us -> 21.6 us  [per_device(): lax.all_gather(slot_out, 'exp', axis=0, tiled=True)]
    reduce_sum x2 -> x5, other arithmetic: 1.56 us -> 4.41 us  [the longest x2 2.75 us: merge_all(): sums = jnp.sum(blocks[:, :, :D] * scale[:, :, None], axis=0)]
    unnamed x11 -> x16, local copies, waits for them, and re-layouts: 2.52 us -> 5.08 us
    another operation x7 -> x6, other arithmetic: 4.53 us -> 3.88 us
  transfers between devices with their start and end apart: 10 -> 2, of which waited for: 9 -> 1; matrix products, arithmetic and copies ran while one was open for 1% -> 1% of each run, Pallas kernels for 0% -> 0%
where the time goes in v5:
time: 161 us; the launch traced here: 160 us
  blocking collectives  117 us (73%)
  matrix products  12.4 us (8%)
  local copies, waits for them, and re-layouts  11.3 us (7%)
  other arithmetic  11.2 us (7%)
  starting transfers between devices  6.42 us (4%)
  waiting for transfers between devices  1.65 us (1%)
    all_to_all x2, blocking collectives, exchange(): return lax.all_to_all(spread, axis, 0, 0, tiled=True)  70.6 us
    all_to_all x1, blocking collectives, per_device(): lax.all_to_all(packed, 'exp', 0, 0, tiled=True)  25 us
    all_gather x1, blocking collectives, per_device(): lax.all_gather(slot_out, 'exp', axis=0, tiled=True)  21.6 us
    reshape x1, local copies, waits for them, and re-layouts, per_device(): mixed.astype(jnp.bfloat16).reshape(periods, channels, D)  5.25 us
    unnamed x16, local copies, waits for them, and re-layouts  5.08 us
    ppermute x1, starting transfers between devices, with_halo(): before = lax.ppermute(last, axis, up)  4.5 us
    another operation x6, other arithmetic  3.88 us
    dot_general x1, matrix products, per_device(): jnp.dot(window, taps, preferred_element_type=jnp.float32)  3.63 us
  transfers between devices with their start and end apart: 2, of which 1 were waited for; matrix products, arithmetic and copies ran while one was open for 1% of the time, Pallas kernels for 0%

profile of v5, /device:TPU:1, one launch (start us, length us, event | category | flops | bytes accessed | tf_op | source)
XLA Modules:
  0.0 160.4 jit_solution(11600015539834591952)
XLA Ops:
  0.0 1.3 copy.49
  1.3 4.5 %collective-permute-start = (bf16[4,1,256]{2,1,0:T(2,128)(2,1)S(1)}, bf16[4,1,256]{2,1,0:T(2,128)(2,1)S(1)}, u32[]{:S(2)}, u32[]{:S(2)}) collective-permute-start(bf16[4,1,256]{2,1,0:T(2,128)(2,1)S(1)} %get-tuple-element.87), channel_id=1, source_target_pairs={{0,1},{1,2},{2,3},{3,4},{4,5},{5,6},{6,7},{7,8},{8,9},{9,10},{10,1... | collective-permute-start | bytes 6152 | tf_op jit(solution)/shard_map/ppermute | solution.py:17
  5.8 1.9 %collective-permute-start.1 = (bf16[4,1,256]{2,1,0:T(2,128)(2,1)S(1)}, bf16[4,1,256]{2,1,0:T(2,128)(2,1)S(1)}, u32[]{:S(2)}, u32[]{:S(2)}) collective-permute-start(bf16[4,1,256]{2,1,0:T(2,128)(2,1)S(1)} %get-tuple-element.88), channel_id=1, source_target_pairs={{1,0},{2,1},{3,2},{4,3},{5,4},{6,5},{7,6},{8,7},{9,8},{10,9},{11,1... | collective-permute-start | bytes 6152 | tf_op jit(solution)/shard_map/ppermute | solution.py:18
  7.7 0.7 compare_reduce_fusion.1
  8.4 0.6 compare_reduce_fusion
  9.1 1.6 %collective-permute-done.1 = bf16[4,1,256]{2,1,0:T(2,128)(2,1)S(1)} collective-permute-done((bf16[4,1,256]{2,1,0:T(2,128)(2,1)S(1)}, bf16[4,1,256]{2,1,0:T(2,128)(2,1)S(1)}, u32[]{:S(2)}, u32[]{:S(2)}) %collective-permute-start.1) | collective-permute-done | bytes 2080 | tf_op jit(solution)/shard_map/ppermute | solution.py:18
  10.7 0.3 fusion.4
  11.0 3.6 %convolution_convert_fusion.1 = bf16[1024,2048]{1,0:T(8,128)(2,1)S(1)} fusion(bf16[1024,768]{1,0:T(8,128)(2,1)S(1)} %bitcast.65, bf16[768,2048]{1,0:T(8,128)(2,1)S(1)} %bitcast.61), kind=kOutput, calls=%fused_computation.2 | convolution fusion | flops 3223322624 | bytes 8912896 | tf_op jit(solution)/shard_map/dot_general | solution.py:74
  14.7 1.3 fusion.49
  16.0 1.7 %fusion.12 = f32[128,2048]{1,0:T(8,128)} fusion(bf16[1024,2048]{1,0:T(8,128)(2,1)S(1)} %convolution_convert_fusion.1, f32[1024,128]{1,0:T(8,128)S(1)} %get-tuple-element.89, f32[128]{0:T(128)S(1)} %get-tuple-element.80), kind=kOutput, calls=%fused_computation.25 | convolution fusion | flops 537133056 | bytes 5767680 | tf_op jit(solution)/shard_map/dot_general | solution.py:81
  17.7 0.7 fusion.41
  18.4 0.4 fusion.9
  18.8 0.6 fusion.42
  19.4 0.1 copy.29
  19.5 0.1 copy.28
  19.6 0.4 scatter.15
  20.0 1.3 maximum_bitcast_fusion
  21.3 25.0 %all_to_all.19 = f32[16,8,2176]{2,1,0:T(8,128)S(1)} all-to-all(f32[16,8,2176]{2,1,0:T(8,128)S(1)} %maximum_bitcast_fusion), channel_id=1, replica_groups=mesh['pos'=16,'exp'=16] {'exp'}, dimensions={0} | all-to-all | bytes 2228224 | tf_op jit(solution)/shard_map/all_to_all | solution.py:89
  46.3 1.0 copy-done.1
  47.3 0.1 fusion.51
  47.5 0.7 fusion.43
  48.2 0.1 copy.41
  48.3 0.1 copy.40
  48.4 0.1 exponential_bitcast_fusion.1
  48.5 0.2 fusion.40
  48.7 0.6 fusion.44
  49.3 0.1 copy.31
  49.4 0.1 copy.33
  49.4 1.4 fusion.7
  50.8 0.1 broadcast_in_dim.4
  50.9 40.4 %all_to_all.20 = f32[16,8,2176]{2,1,0:T(8,128)S(1)} all-to-all(f32[16,8,2176]{2,1,0:T(8,128)S(1)} %broadcast_in_dim.4), channel_id=1, replica_groups=mesh['pos'=16,'exp'=16] {'pos'}, dimensions={0} | all-to-all | bytes 2228224 | tf_op jit(solution)/shard_map/all_to_all | solution.py:54
  91.3 1.0 copy-done.2
  92.3 0.1 fusion.50
  92.5 0.1 copy.43
  92.6 0.1 copy.42
  92.7 0.1 exponential_bitcast_fusion
  92.8 0.2 fusion.37
  93.0 0.6 broadcast_select_fusion
  93.6 0.1 copy.35
  93.6 1.4 fusion.6
  95.0 1.3 copy.39
  96.3 3.3 %fusion = f32[8,2048]{1,0:T(8,128)S(1)} fusion(bf16[1,512,2048]{2,1,0:T(8,128)(2,1)} %param.21, bf16[1,2048,512]{2,1,0:T(8,128)(2,1)} %param.20, f32[8,2048]{0,1:T(8,128)} %copy.39, f32[8]{0:T(128)S(1)} %broadcast_select_fusion), kind=kOutput, calls=%fused_computation.3 | convolution fusion | flops 33624064 | bytes 4325408 | tf_op jit(solution)/shard_map/dot_general | solution.py:96
  99.6 0.1 broadcast_in_dim.5
  99.8 30.2 %all_to_all.21 = f32[16,8,2048]{2,1,0:T(8,128)} all-to-all(f32[16,8,2048]{2,1,0:T(8,128)S(1)} %broadcast_in_dim.5), channel_id=1, replica_groups=mesh['pos'=16,'exp'=16] {'pos'}, dimensions={0} | all-to-all | bytes 2097152 | tf_op jit(solution)/shard_map/all_to_all | solution.py:54
  129.9 1.3 reduce_sum.69
  131.2 21.6 %all_gather.3 = bf16[128,2048]{1,0:T(8,128)(2,1)S(1)} all-gather(bf16[8,2048]{1,0:T(8,128)(2,1)S(1)} %reduce_sum.69), channel_id=1, replica_groups=mesh['pos'=16,'exp'=16] {'exp'}, dimensions={0}, use_global_device_ids=true | all-gather | bytes 557056 | tf_op jit(solution)/shard_map/all_gather | solution.py:103
  152.8 2.4 %convolution_convert_fusion = bf16[1024,2048]{1,0:T(8,128)(2,1)S(1)} fusion(bf16[128,2048]{1,0:T(8,128)(2,1)S(1)} %all_gather.3, f32[1024,128]{1,0:T(8,128)} %copy-done.3, f32[1024]{0:T(1024)S(1)} %get-tuple-element.77, f32[1024]{0:T(1024)S(1)} %get-tuple-element.79), kind=kOutput, calls=%fused_computation.1 | convolution fusion | flops 539361280 | bytes 5251072 | tf_op jit(solution)/shard_map/dot_general | solution.py:101
  155.2 5.3 %copy.48 = bf16[4,256,2048]{2,0,1:T(4,128)(2,1)} copy(bf16[4,256,2048]{2,1,0:T(8,128)(2,1)S(1)} %bitcast.62) | data formatting | bytes 8388608 | tf_op jit(solution)/shard_map/reshape | solution.py:106
  (14 shorter events, 0.1 us)
Async XLA Ops:
  0.0 11.0 %copy-start = (bf16[3,256,2048]{2,1,0:T(8,128)(2,1)S(1)}, bf16[3,256,2048]{2,1,0:T(8,128)(2,1)}, u32[]{:S(2)}) copy-start(bf16[3,256,2048]{2,1,0:T(8,128)(2,1)} %param.18) | copy-start | bytes 9437188
  1.3 7.8 %collective-permute-start = (bf16[4,1,256]{2,1,0:T(2,128)(2,1)S(1)}, bf16[4,1,256]{2,1,0:T(2,128)(2,1)S(1)}, u32[]{:S(2)}, u32[]{:S(2)}) collective-permute-start(bf16[4,1,256]{2,1,0:T(2,128)(2,1)S(1)} %get-tuple-element.87), channel_id=1, source_target_pairs={{0,1},{1,2},{2,3},{3,4},{4,5},{5,6},{6,7},{7,8},{8,9},{9,10},{10,1... | collective-permute-start | bytes 6152 | tf_op jit(solution)/shard_map/ppermute | solution.py:17
  5.8 4.9 %collective-permute-start.1 = (bf16[4,1,256]{2,1,0:T(2,128)(2,1)S(1)}, bf16[4,1,256]{2,1,0:T(2,128)(2,1)S(1)}, u32[]{:S(2)}, u32[]{:S(2)}) collective-permute-start(bf16[4,1,256]{2,1,0:T(2,128)(2,1)S(1)} %get-tuple-element.88), channel_id=1, source_target_pairs={{1,0},{2,1},{3,2},{4,3},{5,4},{6,5},{7,6},{8,7},{9,8},{10,9},{11,1... | collective-permute-start | bytes 6152 | tf_op jit(solution)/shard_map/ppermute | solution.py:18
  11.0 3.7 %copy-start.4 = (bf16[2048,128]{1,0:T(8,128)(2,1)S(1)}, bf16[2048,128]{1,0:T(8,128)(2,1)}, u32[]{:S(2)}) copy-start(bf16[2048,128]{1,0:T(8,128)(2,1)} %param.19) | copy-start | bytes 1572868
  16.0 2.4 %copy-start.3 = (f32[1024,128]{1,0:T(8,128)}, f32[1024,128]{1,0:T(8,128)S(1)}, u32[]{:S(2)}) copy-start(f32[1024,128]{1,0:T(8,128)S(1)} %get-tuple-element.89) | copy-start | bytes 1572868
  46.3 1.0 copy-start.1
  91.3 1.0 copy-start.2

commit v6 on v4

--- a/solution.py
+++ b/solution.py
@@ -1,6 +1,7 @@
 import jax
 import jax.numpy as jnp
 from jax import lax
+from jax.experimental import pallas as pl
 from jax.sharding import PartitionSpec as P
 
 D = 2048
@@ -48,6 +49,32 @@
     return value
 
 
+def mix_kernel(combine_ref, slots_ref, out_ref):
+    for period in range(combine_ref.shape[0]):
+        part = jnp.dot(combine_ref[period], slots_ref[...], preferred_element_type=jnp.float32)
+        out_ref[:, period, :] = part.astype(out_ref.dtype)
+
+
+def mix(combine, slot_all, block=64):
+    periods, channels, slots = combine.shape
+    width = slot_all.shape[1]
+    return pl.pallas_call(
+        mix_kernel,
+        grid=(channels // block,),
+        in_specs=[
+            pl.BlockSpec((periods, block, slots), lambda i: (0, i, 0)),
+            pl.BlockSpec((slots, width), lambda i: (0, 0)),
+        ],
+        out_specs=pl.BlockSpec((block, periods, width), lambda i: (i, 0, 0)),
+        out_shape=jax.ShapeDtypeStruct((channels, periods, width), jnp.bfloat16),
+        cost_estimate=pl.CostEstimate(
+            flops=2 * periods * channels * slots * width,
+            bytes_accessed=2 * (periods * channels * (slots + width) + slots * width),
+            transcendentals=0,
+        ),
+    )(combine, slot_all)
+
+
 def per_device(patches, conv_weight, phi, w_in, w_out):
     channels, periods, samples = patches.shape
     every = ("pos", "exp")
@@ -89,12 +116,8 @@
     row_peak = jnp.max(logits, axis=1, keepdims=True)
     row_weights = jnp.exp(logits - row_peak)
     combine = (row_weights / jnp.sum(row_weights, axis=1, keepdims=True)).astype(jnp.bfloat16)
-    mixed = jnp.dot(
-        combine,
-        lax.all_gather(slot_out, "exp", axis=0, tiled=True),
-        preferred_element_type=jnp.float32,
-    )
-    return jnp.swapaxes(mixed.astype(jnp.bfloat16).reshape(periods, channels, D), 0, 1)
+    slot_all = lax.all_gather(slot_out, "exp", axis=0, tiled=True)
+    return mix(combine.reshape(periods, channels, slots), slot_all)
 
 
 def solution(mesh):

time: 136 us -> 136 us (level)
  Pallas kernels: 0 us -> 5.73 us
  local copies, waits for them, and re-layouts: 9.09 us -> 3.84 us
  matrix products: 12.1 us -> 9.69 us
  other arithmetic: 11.2 us -> 13.3 us
  waiting for transfers between devices: 20.1 us -> 18.5 us
    pallas_call x0 -> x1, Pallas kernels: none -> 5.73 us  [mix(): pl.pallas_call(mix_kernel, grid=(channels // block,), in_specs=[pl.BlockS...]
    reshape x1 -> x0, local copies, waits for them, and re-layouts: 5.25 us -> none  [per_device(): mixed.astype(jnp.bfloat16).reshape(periods, channels, D)]
    dot_general x1 -> x0, matrix products: 2.37 us -> none  [per_device(): jnp.dot(combine, lax.all_gather(slot_out, 'exp', axis=0, tiled=True), pre...]
    convert_element_type x0 -> x1, other arithmetic: none -> 2.09 us  [per_device(): (row_weights / jnp.sum(row_weights, axis=1, keepdims=True)).astype(jnp.bf...]
    ppermute x4, waiting for transfers between devices: 9.47 us -> 7.83 us  [butterfly_sum(): value = value + lax.ppermute(value, axis, pairs)]
  transfers between devices with their start and end apart: 10 -> 10, of which waited for: 9 -> 8; matrix products, arithmetic and copies ran while one was open for 1% -> 3% of each run, Pallas kernels for 0% -> 0%
where the time goes in v6:
time: 136 us; the launch traced here: 135 us
  blocking collectives  53.1 us (39%)
  starting transfers between devices  30.9 us (23%)
  waiting for transfers between devices  18.5 us (14%)
  other arithmetic  13.3 us (10%)
  matrix products  9.69 us (7%)
  Pallas kernels  5.73 us (4%)
  local copies, waits for them, and re-layouts  3.84 us (3%)
    all_gather x1, blocking collectives, per_device(): slot_all = lax.all_gather(slot_out, 'exp', axis=0, tiled=True)  28 us
    all_to_all x1, blocking collectives, per_device(): lax.all_to_all(packed, 'exp', 0, 0, tiled=True)  25 us
    ppermute x4, starting transfers between devices, butterfly_softmax_sum(): value = merge(value, lax.ppermute(value, axis, pairs))  13.3 us
    ppermute x4, starting transfers between devices, butterfly_sum(): value = value + lax.ppermute(value, axis, pairs)  11.1 us
    ppermute x4, waiting for transfers between devices, butterfly_softmax_sum(): value = merge(value, lax.ppermute(value, axis, pairs))  9 us
    ppermute x4, waiting for transfers between devices, butterfly_sum(): value = value + lax.ppermute(value, axis, pairs)  7.83 us
    pallas_call x1, Pallas kernels, mix(): pl.pallas_call(mix_kernel, grid=(channels // block,), in_specs=[pl.BlockS...  5.73 us
    another operation x7, other arithmetic  4.53 us
  transfers between devices with their start and end apart: 10, of which 8 were waited for; matrix products, arithmetic and copies ran while one was open for 3% of the time, Pallas kernels for 0%

profile of v6, /device:TPU:1, one launch (start us, length us, event | category | flops | bytes accessed | tf_op | source)
XLA Modules:
  0.0 135.2 jit_solution(8849520450813725088)
XLA Ops:
  0.0 1.3 copy.57
  1.3 4.5 %collective-permute-start = (bf16[4,1,256]{2,1,0:T(2,128)(2,1)S(1)}, bf16[4,1,256]{2,1,0:T(2,128)(2,1)S(1)}, u32[]{:S(2)}, u32[]{:S(2)}) collective-permute-start(bf16[4,1,256]{2,1,0:T(2,128)(2,1)S(1)} %get-tuple-element.116), channel_id=1, source_target_pairs={{0,1},{1,2},{2,3},{3,4},{4,5},{5,6},{6,7},{7,8},{8,9},{9,10},{10,1... | collective-permute-start | bytes 6152 | tf_op jit(solution)/shard_map/ppermute | solution.py:18
  5.8 1.9 %collective-permute-start.1 = (bf16[4,1,256]{2,1,0:T(2,128)(2,1)S(1)}, bf16[4,1,256]{2,1,0:T(2,128)(2,1)S(1)}, u32[]{:S(2)}, u32[]{:S(2)}) collective-permute-start(bf16[4,1,256]{2,1,0:T(2,128)(2,1)S(1)} %get-tuple-element.117), channel_id=1, source_target_pairs={{1,0},{2,1},{3,2},{4,3},{5,4},{6,5},{7,6},{8,7},{9,8},{10,9},{11,1... | collective-permute-start | bytes 6152 | tf_op jit(solution)/shard_map/ppermute | solution.py:19
  7.7 0.7 compare_reduce_fusion.2
  8.4 0.6 compare_reduce_fusion.1
  9.1 1.6 %collective-permute-done.1 = bf16[4,1,256]{2,1,0:T(2,128)(2,1)S(1)} collective-permute-done((bf16[4,1,256]{2,1,0:T(2,128)(2,1)S(1)}, bf16[4,1,256]{2,1,0:T(2,128)(2,1)S(1)}, u32[]{:S(2)}, u32[]{:S(2)}) %collective-permute-start.1) | collective-permute-done | bytes 2080 | tf_op jit(solution)/shard_map/ppermute | solution.py:19
  10.7 0.3 fusion.4
  11.0 3.6 %convolution_convert_fusion = bf16[1024,2048]{1,0:T(8,128)(2,1)S(1)} fusion(bf16[1024,768]{1,0:T(8,128)(2,1)S(1)} %bitcast.48, bf16[768,2048]{1,0:T(8,128)(2,1)S(1)} %bitcast.45), kind=kOutput, calls=%fused_computation | convolution fusion | flops 3223322624 | bytes 8912896 | tf_op jit(solution)/shard_map/dot_general | solution.py:85
  14.7 1.3 fusion.55
  16.0 1.7 %fusion.10 = f32[128,2048]{1,0:T(8,128)} fusion(bf16[1024,2048]{1,0:T(8,128)(2,1)S(1)} %convolution_convert_fusion, f32[1024,128]{1,0:T(8,128)S(1)} %get-tuple-element.118, f32[128]{0:T(128)S(1)} %get-tuple-element.103), kind=kOutput, calls=%fused_computation.19 | convolution fusion | flops 537133056 | bytes 5767680 | tf_op jit(solution)/shard_map/dot_general | solution.py:92
  17.7 0.7 fusion.47
  18.4 0.4 fusion.8
  18.8 0.6 fusion.48
  19.6 0.4 scatter.25
  20.0 1.3 maximum_bitcast_fusion
  21.3 25.0 %all_to_all.9 = f32[16,8,2176]{2,1,0:T(8,128)S(1)} all-to-all(f32[16,8,2176]{2,1,0:T(8,128)S(1)} %maximum_bitcast_fusion), channel_id=1, replica_groups=mesh['pos'=16,'exp'=16] {'exp'}, dimensions={0} | all-to-all | bytes 2228224 | tf_op jit(solution)/shard_map/all_to_all | solution.py:100
  46.3 1.0 copy-done.1
  47.5 0.7 fusion.49
  48.6 0.2 fusion.46
  48.8 0.6 fusion.50
  49.6 1.4 %fusion.6 = f32[8,2048]{1,0:T(8,128)S(1)} fusion(f32[16,8,2176]{2,1,0:T(8,128)} %copy-done.1, f32[16,8]{1,0:T(8,128)S(1)} %copy.49), kind=kLoop, calls=%fused_computation.11 | loop fusion | flops 507904 | bytes 1114624 | tf_op jit(solution)/shard_map/reduce_sum | solution.py:104
  51.0 1.7 %collective-permute-start.2 = (f32[8,2176]{1,0:T(8,128)S(1)}, f32[8,2176]{1,0:T(8,128)S(1)}, u32[]{:S(2)}, u32[]{:S(2)}) collective-permute-start(f32[8,2176]{1,0:T(8,128)S(1)} %pad_maximum_fusion.2), channel_id=1, source_target_pairs={{0,16},{16,0},{32,48},{48,32},{64,80},{80,64},{96,112},{112,96},{1... | collective-permute-start | bytes 208904 | tf_op jit(solution)/shard_map/ppermute | solution.py:47
  52.7 0.6 compare_reduce_fusion
  53.4 1.4 %collective-permute-done.2 = f32[8,2176]{1,0:T(8,128)S(1)} collective-permute-done((f32[8,2176]{1,0:T(8,128)S(1)}, f32[8,2176]{1,0:T(8,128)S(1)}, u32[]{:S(2)}, u32[]{:S(2)}) %collective-permute-start.2) | collective-permute-done | bytes 69664 | tf_op jit(solution)/shard_map/ppermute | solution.py:47
  54.8 0.2 exponential_reduce_fusion.5
  55.0 0.7 slice_select_fusion.2
  55.7 5.6 %collective-permute-start.3 = (f32[8,2176]{1,0:T(8,128)S(1)}, f32[8,2176]{1,0:T(8,128)S(1)}, u32[]{:S(2)}, u32[]{:S(2)}) collective-permute-start(f32[8,2176]{1,0:T(8,128)S(1)} %scatter.30), channel_id=1, source_target_pairs={{0,32},{16,48},{32,0},{48,16},{64,96},{80,112},{96,64},{112,80},{1... | collective-permute-start | bytes 208904 | tf_op jit(solution)/shard_map/ppermute | solution.py:47
  61.3 1.7 %collective-permute-done.3 = f32[8,2176]{1,0:T(8,128)S(1)} collective-permute-done((f32[8,2176]{1,0:T(8,128)S(1)}, f32[8,2176]{1,0:T(8,128)S(1)}, u32[]{:S(2)}, u32[]{:S(2)}) %collective-permute-start.3) | collective-permute-done | bytes 69664 | tf_op jit(solution)/shard_map/ppermute | solution.py:47
  63.0 0.2 exponential_reduce_fusion.3
  63.3 0.7 slice_select_fusion.1
  64.0 3.2 %collective-permute-start.4 = (f32[8,2176]{1,0:T(8,128)S(1)}, f32[8,2176]{1,0:T(8,128)S(1)}, u32[]{:S(2)}, u32[]{:S(2)}) collective-permute-start(f32[8,2176]{1,0:T(8,128)S(1)} %scatter.31), channel_id=1, source_target_pairs={{0,64},{16,80},{32,96},{48,112},{64,0},{80,16},{96,32},{112,48},{1... | collective-permute-start | bytes 208904 | tf_op jit(solution)/shard_map/ppermute | solution.py:47
  67.2 4.0 %collective-permute-done.4 = f32[8,2176]{1,0:T(8,128)S(1)} collective-permute-done((f32[8,2176]{1,0:T(8,128)S(1)}, f32[8,2176]{1,0:T(8,128)S(1)}, u32[]{:S(2)}, u32[]{:S(2)}) %collective-permute-start.4) | collective-permute-done | bytes 69664 | tf_op jit(solution)/shard_map/ppermute | solution.py:47
  71.2 0.2 exponential_reduce_fusion.1
  71.5 0.7 slice_select_fusion
  72.2 2.8 %collective-permute-start.5 = (f32[8,2176]{1,0:T(8,128)S(1)}, f32[8,2176]{1,0:T(8,128)S(1)}, u32[]{:S(2)}, u32[]{:S(2)}) collective-permute-start(f32[8,2176]{1,0:T(8,128)S(1)} %scatter.34), channel_id=1, source_target_pairs={{0,128},{16,144},{32,160},{48,176},{64,192},{80,208},{96,224},{112... | collective-permute-start | bytes 208904 | tf_op jit(solution)/shard_map/ppermute | solution.py:47
  75.0 1.9 %collective-permute-done.5 = f32[8,2176]{1,0:T(8,128)S(1)} collective-permute-done((f32[8,2176]{1,0:T(8,128)S(1)}, f32[8,2176]{1,0:T(8,128)S(1)}, u32[]{:S(2)}, u32[]{:S(2)}) %collective-permute-start.5) | collective-permute-done | bytes 69664 | tf_op jit(solution)/shard_map/ppermute | solution.py:47
  77.2 0.2 slice_reduce_fusion
  77.4 3.0 %fusion = f32[8,2048]{1,0:T(8,128)S(1)} fusion(bf16[1,512,2048]{2,1,0:T(8,128)(2,1)} %param.25, bf16[1,2048,512]{2,1,0:T(8,128)(2,1)} %param.24, f32[8,2176]{1,0:T(8,128)S(1)} %multiply_add_fusion, f32[8]{0:T(128)S(1)} %slice_reduce_fusion), kind=kOutput, calls=%fused_computation.1 | convolution fusion | flops 33624064 | bytes 4325888 | tf_op jit(solution)/shard_map/dot_general | solution.py:114
  80.4 1.3 collective-permute-start.6
  81.7 1.8 %collective-permute-done.6 = f32[8,2048]{1,0:T(8,128)S(1)} collective-permute-done((f32[8,2048]{1,0:T(8,128)S(1)}, f32[8,2048]{1,0:T(8,128)S(1)}, u32[]{:S(2)}, u32[]{:S(2)}) %collective-permute-start.6) | collective-permute-done | bytes 65568 | tf_op jit(solution)/shard_map/ppermute | solution.py:29
  83.5 2.9 %collective-permute-start.7 = (f32[8,2048]{1,0:T(8,128)S(1)}, f32[8,2048]{1,0:T(8,128)S(1)}, u32[]{:S(2)}, u32[]{:S(2)}) collective-permute-start(f32[8,2048]{1,0:T(8,128)S(1)} %add.60), channel_id=1, source_target_pairs={{0,32},{16,48},{32,0},{48,16},{64,96},{80,112},{96,64},{112,80},{1... | collective-permute-start | bytes 196616 | tf_op jit(solution)/shard_map/ppermute | solution.py:29
  86.4 1.7 %collective-permute-done.7 = f32[8,2048]{1,0:T(8,128)S(1)} collective-permute-done((f32[8,2048]{1,0:T(8,128)S(1)}, f32[8,2048]{1,0:T(8,128)S(1)}, u32[]{:S(2)}, u32[]{:S(2)}) %collective-permute-start.7) | collective-permute-done | bytes 65568 | tf_op jit(solution)/shard_map/ppermute | solution.py:29
  88.1 3.2 %collective-permute-start.8 = (f32[8,2048]{1,0:T(8,128)S(1)}, f32[8,2048]{1,0:T(8,128)S(1)}, u32[]{:S(2)}, u32[]{:S(2)}) collective-permute-start(f32[8,2048]{1,0:T(8,128)S(1)} %add.61), channel_id=1, source_target_pairs={{0,64},{16,80},{32,96},{48,112},{64,0},{80,16},{96,32},{112,48},{1... | collective-permute-start | bytes 196616 | tf_op jit(solution)/shard_map/ppermute | solution.py:29
  91.3 4.3 %collective-permute-done.8 = f32[8,2048]{1,0:T(8,128)S(1)} collective-permute-done((f32[8,2048]{1,0:T(8,128)S(1)}, f32[8,2048]{1,0:T(8,128)S(1)}, u32[]{:S(2)}, u32[]{:S(2)}) %collective-permute-start.8) | collective-permute-done | bytes 65568 | tf_op jit(solution)/shard_map/ppermute | solution.py:29
  95.7 3.7 %collective-permute-start.9 = (f32[8,2048]{1,0:T(8,128)S(1)}, f32[8,2048]{1,0:T(8,128)S(1)}, u32[]{:S(2)}, u32[]{:S(2)}) collective-permute-start(f32[8,2048]{1,0:T(8,128)S(1)} %add.62), channel_id=1, source_target_pairs={{0,128},{16,144},{32,160},{48,176},{64,192},{80,208},{96,224},{112... | collective-permute-start | bytes 196616 | tf_op jit(solution)/shard_map/ppermute | solution.py:29
  99.3 2.1 %divide_convert_fusion = bf16[1024,128]{1,0:T(8,128)(2,1)} fusion(f32[1024,128]{1,0:T(8,128)} %copy-done.2, f32[1024]{0:T(1024)S(1)} %get-tuple-element.102, f32[1024]{0:T(1024)S(1)} %get-tuple-element.104), kind=kLoop, calls=%fused_computation.14 | loop fusion | flops 393216 | bytes 794624 | tf_op jit(solution)/shard_map/convert_element_type | solution.py:118
  101.4 28.0 %all_gather.3.slots_ref = bf16[128,2048]{1,0:T(8,128)(2,1)} all-gather(bf16[8,2048]{1,0:T(8,128)(2,1)S(1)} %add_convert_fusion), channel_id=1, replica_groups=mesh['pos'=16,'exp'=16] {'exp'}, dimensions={0}, use_global_device_ids=true | all-gather | bytes 557056 | tf_op jit(solution)/shard_map/all_gather | solution.py:119
  129.5 5.7 %shard_map.55 = bf16[256,4,2048]{2,1,0:T(4,128)(2,1)} custom-call(bf16[4,256,128]{2,1,0:T(8,128)(2,1)} %bitcast.49, bf16[128,2048]{1,0:T(8,128)(2,1)} %all_gather.3.slots_ref), custom_call_target="tpu_custom_call" | custom-call | flops 536870912 | bytes 4980736 | tf_op jit(solution)/shard_map/pallas_call | solution.py:61
  (35 shorter events, 1.8 us)
Async XLA Ops:
  0.0 11.0 %copy-start = (bf16[3,256,2048]{2,1,0:T(8,128)(2,1)S(1)}, bf16[3,256,2048]{2,1,0:T(8,128)(2,1)}, u32[]{:S(2)}) copy-start(bf16[3,256,2048]{2,1,0:T(8,128)(2,1)} %param.22) | copy-start | bytes 9437188
  1.3 7.8 %collective-permute-start = (bf16[4,1,256]{2,1,0:T(2,128)(2,1)S(1)}, bf16[4,1,256]{2,1,0:T(2,128)(2,1)S(1)}, u32[]{:S(2)}, u32[]{:S(2)}) collective-permute-start(bf16[4,1,256]{2,1,0:T(2,128)(2,1)S(1)} %get-tuple-element.116), channel_id=1, source_target_pairs={{0,1},{1,2},{2,3},{3,4},{4,5},{5,6},{6,7},{7,8},{8,9},{9,10},{10,1... | collective-permute-start | bytes 6152 | tf_op jit(solution)/shard_map/ppermute | solution.py:18
  5.8 4.9 %collective-permute-start.1 = (bf16[4,1,256]{2,1,0:T(2,128)(2,1)S(1)}, bf16[4,1,256]{2,1,0:T(2,128)(2,1)S(1)}, u32[]{:S(2)}, u32[]{:S(2)}) collective-permute-start(bf16[4,1,256]{2,1,0:T(2,128)(2,1)S(1)} %get-tuple-element.117), channel_id=1, source_target_pairs={{1,0},{2,1},{3,2},{4,3},{5,4},{6,5},{7,6},{8,7},{9,8},{10,9},{11,1... | collective-permute-start | bytes 6152 | tf_op jit(solution)/shard_map/ppermute | solution.py:19
  11.0 3.7 %copy-start.3 = (bf16[2048,128]{1,0:T(8,128)(2,1)S(1)}, bf16[2048,128]{1,0:T(8,128)(2,1)}, u32[]{:S(2)}) copy-start(bf16[2048,128]{1,0:T(8,128)(2,1)} %param.23) | copy-start | bytes 1572868
  16.0 2.4 %copy-start.2 = (f32[1024,128]{1,0:T(8,128)}, f32[1024,128]{1,0:T(8,128)S(1)}, u32[]{:S(2)}) copy-start(f32[1024,128]{1,0:T(8,128)S(1)} %get-tuple-element.118) | copy-start | bytes 1572868
  46.3 1.0 copy-start.1
  51.0 3.8 %collective-permute-start.2 = (f32[8,2176]{1,0:T(8,128)S(1)}, f32[8,2176]{1,0:T(8,128)S(1)}, u32[]{:S(2)}, u32[]{:S(2)}) collective-permute-start(f32[8,2176]{1,0:T(8,128)S(1)} %pad_maximum_fusion.2), channel_id=1, source_target_pairs={{0,16},{16,0},{32,48},{48,32},{64,80},{80,64},{96,112},{112,96},{1... | collective-permute-start | bytes 208904 | tf_op jit(solution)/shard_map/ppermute | solution.py:47
  55.7 7.3 %collective-permute-start.3 = (f32[8,2176]{1,0:T(8,128)S(1)}, f32[8,2176]{1,0:T(8,128)S(1)}, u32[]{:S(2)}, u32[]{:S(2)}) collective-permute-start(f32[8,2176]{1,0:T(8,128)S(1)} %scatter.30), channel_id=1, source_target_pairs={{0,32},{16,48},{32,0},{48,16},{64,96},{80,112},{96,64},{112,80},{1... | collective-permute-start | bytes 208904 | tf_op jit(solution)/shard_map/ppermute | solution.py:47
  64.0 7.2 %collective-permute-start.4 = (f32[8,2176]{1,0:T(8,128)S(1)}, f32[8,2176]{1,0:T(8,128)S(1)}, u32[]{:S(2)}, u32[]{:S(2)}) collective-permute-start(f32[8,2176]{1,0:T(8,128)S(1)} %scatter.31), channel_id=1, source_target_pairs={{0,64},{16,80},{32,96},{48,112},{64,0},{80,16},{96,32},{112,48},{1... | collective-permute-start | bytes 208904 | tf_op jit(solution)/shard_map/ppermute | solution.py:47
  72.2 4.8 %collective-permute-start.5 = (f32[8,2176]{1,0:T(8,128)S(1)}, f32[8,2176]{1,0:T(8,128)S(1)}, u32[]{:S(2)}, u32[]{:S(2)}) collective-permute-start(f32[8,2176]{1,0:T(8,128)S(1)} %scatter.34), channel_id=1, source_target_pairs={{0,128},{16,144},{32,160},{48,176},{64,192},{80,208},{96,224},{112... | collective-permute-start | bytes 208904 | tf_op jit(solution)/shard_map/ppermute | solution.py:47
  80.4 3.1 %collective-permute-start.6 = (f32[8,2048]{1,0:T(8,128)S(1)}, f32[8,2048]{1,0:T(8,128)S(1)}, u32[]{:S(2)}, u32[]{:S(2)}) collective-permute-start(f32[8,2048]{1,0:T(8,128)S(1)} %fusion), channel_id=1, source_target_pairs={{0,16},{16,0},{32,48},{48,32},{64,80},{80,64},{96,112},{112,96},{1... | collective-permute-start | bytes 196616 | tf_op jit(solution)/shard_map/ppermute | solution.py:29
  83.5 4.6 %collective-permute-start.7 = (f32[8,2048]{1,0:T(8,128)S(1)}, f32[8,2048]{1,0:T(8,128)S(1)}, u32[]{:S(2)}, u32[]{:S(2)}) collective-permute-start(f32[8,2048]{1,0:T(8,128)S(1)} %add.60), channel_id=1, source_target_pairs={{0,32},{16,48},{32,0},{48,16},{64,96},{80,112},{96,64},{112,80},{1... | collective-permute-start | bytes 196616 | tf_op jit(solution)/shard_map/ppermute | solution.py:29
  88.1 7.5 %collective-permute-start.8 = (f32[8,2048]{1,0:T(8,128)S(1)}, f32[8,2048]{1,0:T(8,128)S(1)}, u32[]{:S(2)}, u32[]{:S(2)}) collective-permute-start(f32[8,2048]{1,0:T(8,128)S(1)} %add.61), channel_id=1, source_target_pairs={{0,64},{16,80},{32,96},{48,112},{64,0},{80,16},{96,32},{112,48},{1... | collective-permute-start | bytes 196616 | tf_op jit(solution)/shard_map/ppermute | solution.py:29
  95.7 5.8 %collective-permute-start.9 = (f32[8,2048]{1,0:T(8,128)S(1)}, f32[8,2048]{1,0:T(8,128)S(1)}, u32[]{:S(2)}, u32[]{:S(2)}) collective-permute-start(f32[8,2048]{1,0:T(8,128)S(1)} %add.62), channel_id=1, source_target_pairs={{0,128},{16,144},{32,160},{48,176},{64,192},{80,208},{96,224},{112... | collective-permute-start | bytes 196616 | tf_op jit(solution)/shard_map/ppermute | solution.py:29

commit v7 on v6

--- a/solution.py
+++ b/solution.py
@@ -50,26 +50,26 @@
 
 
 def mix_kernel(combine_ref, slots_ref, out_ref):
-    for period in range(combine_ref.shape[0]):
-        part = jnp.dot(combine_ref[period], slots_ref[...], preferred_element_type=jnp.float32)
-        out_ref[:, period, :] = part.astype(out_ref.dtype)
+    part = jnp.dot(combine_ref[...], slots_ref[...], preferred_element_type=jnp.float32)
+    out_ref[...] = part.astype(out_ref.dtype).reshape(out_ref.shape)
 
 
-def mix(combine, slot_all, block=64):
-    periods, channels, slots = combine.shape
+def mix(combine, slot_all, periods, block=64):
+    rows, slots = combine.shape
+    channels = rows // periods
     width = slot_all.shape[1]
     return pl.pallas_call(
         mix_kernel,
         grid=(channels // block,),
         in_specs=[
-            pl.BlockSpec((periods, block, slots), lambda i: (0, i, 0)),
+            pl.BlockSpec((block * periods, slots), lambda i: (i, 0)),
             pl.BlockSpec((slots, width), lambda i: (0, 0)),
         ],
         out_specs=pl.BlockSpec((block, periods, width), lambda i: (i, 0, 0)),
         out_shape=jax.ShapeDtypeStruct((channels, periods, width), jnp.bfloat16),
         cost_estimate=pl.CostEstimate(
-            flops=2 * periods * channels * slots * width,
-            bytes_accessed=2 * (periods * channels * (slots + width) + slots * width),
+            flops=2 * rows * slots * width,
+            bytes_accessed=2 * (rows * (slots + width) + slots * width),
             transcendentals=0,
         ),
     )(combine, slot_all)
@@ -117,7 +117,8 @@
     row_weights = jnp.exp(logits - row_peak)
     combine = (row_weights / jnp.sum(row_weights, axis=1, keepdims=True)).astype(jnp.bfloat16)
     slot_all = lax.all_gather(slot_out, "exp", axis=0, tiled=True)
-    return mix(combine.reshape(periods, channels, slots), slot_all)
+    by_channel = jnp.swapaxes(combine.reshape(periods, channels, slots), 0, 1).reshape(channels * periods, slots)
+    return mix(by_channel, slot_all, periods)
 
 
 def solution(mesh):

time: 136 us -> 135 us (level)
  no operation moved by 1% of the time
where the time goes in v7:
time: 135 us; the launch traced here: 134 us
  blocking collectives  52.9 us (39%)
  starting transfers between devices  30.9 us (23%)
  waiting for transfers between devices  18.5 us (14%)
  other arithmetic  12.6 us (9%)
  matrix products  9.69 us (7%)
  local copies, waits for them, and re-layouts  4.75 us (4%)
  Pallas kernels  4.71 us (3%)
    all_gather x1, blocking collectives, per_device(): slot_all = lax.all_gather(slot_out, 'exp', axis=0, tiled=True)  27.8 us
    all_to_all x1, blocking collectives, per_device(): lax.all_to_all(packed, 'exp', 0, 0, tiled=True)  25 us
    ppermute x4, starting transfers between devices, butterfly_softmax_sum(): value = merge(value, lax.ppermute(value, axis, pairs))  13.3 us
    ppermute x4, starting transfers between devices, butterfly_sum(): value = value + lax.ppermute(value, axis, pairs)  11.1 us
    ppermute x4, waiting for transfers between devices, butterfly_softmax_sum(): value = merge(value, lax.ppermute(value, axis, pairs))  9 us
    ppermute x4, waiting for transfers between devices, butterfly_sum(): value = value + lax.ppermute(value, axis, pairs)  7.83 us
    pallas_call x1, Pallas kernels, mix(): pl.pallas_call(mix_kernel, grid=(channels // block,), in_specs=[pl.BlockS...  4.71 us
    another operation x7, other arithmetic  4.53 us
  transfers between devices with their start and end apart: 10, of which 8 were waited for; matrix products, arithmetic and copies ran while one was open for 3% of the time, Pallas kernels for 0%

profile of v7, /device:TPU:1, one launch (start us, length us, event | category | flops | bytes accessed | tf_op | source)
XLA Modules:
  0.0 134.2 jit_solution(10592369831930324097)
XLA Ops:
  0.0 1.3 copy.62
  1.3 4.5 %collective-permute-start = (bf16[4,1,256]{2,1,0:T(2,128)(2,1)S(1)}, bf16[4,1,256]{2,1,0:T(2,128)(2,1)S(1)}, u32[]{:S(2)}, u32[]{:S(2)}) collective-permute-start(bf16[4,1,256]{2,1,0:T(2,128)(2,1)S(1)} %get-tuple-element.116), channel_id=1, source_target_pairs={{0,1},{1,2},{2,3},{3,4},{4,5},{5,6},{6,7},{7,8},{8,9},{9,10},{10,1... | collective-permute-start | bytes 6152 | tf_op jit(solution)/shard_map/ppermute | solution.py:18
  5.8 1.9 %collective-permute-start.1 = (bf16[4,1,256]{2,1,0:T(2,128)(2,1)S(1)}, bf16[4,1,256]{2,1,0:T(2,128)(2,1)S(1)}, u32[]{:S(2)}, u32[]{:S(2)}) collective-permute-start(bf16[4,1,256]{2,1,0:T(2,128)(2,1)S(1)} %get-tuple-element.117), channel_id=1, source_target_pairs={{1,0},{2,1},{3,2},{4,3},{5,4},{6,5},{7,6},{8,7},{9,8},{10,9},{11,1... | collective-permute-start | bytes 6152 | tf_op jit(solution)/shard_map/ppermute | solution.py:19
  7.7 0.7 compare_reduce_fusion.2
  8.4 0.6 compare_reduce_fusion.1
  9.1 1.6 %collective-permute-done.1 = bf16[4,1,256]{2,1,0:T(2,128)(2,1)S(1)} collective-permute-done((bf16[4,1,256]{2,1,0:T(2,128)(2,1)S(1)}, bf16[4,1,256]{2,1,0:T(2,128)(2,1)S(1)}, u32[]{:S(2)}, u32[]{:S(2)}) %collective-permute-start.1) | collective-permute-done | bytes 2080 | tf_op jit(solution)/shard_map/ppermute | solution.py:19
  10.7 0.3 fusion.4
  11.0 3.6 %convolution_convert_fusion = bf16[1024,2048]{1,0:T(8,128)(2,1)S(1)} fusion(bf16[1024,768]{1,0:T(8,128)(2,1)S(1)} %bitcast.51, bf16[768,2048]{1,0:T(8,128)(2,1)S(1)} %bitcast.48), kind=kOutput, calls=%fused_computation | convolution fusion | flops 3223322624 | bytes 8912896 | tf_op jit(solution)/shard_map/dot_general | solution.py:85
  14.7 1.3 fusion.55
  16.0 1.7 %fusion.10 = f32[128,2048]{1,0:T(8,128)} fusion(bf16[1024,2048]{1,0:T(8,128)(2,1)S(1)} %convolution_convert_fusion, f32[1024,128]{1,0:T(8,128)S(1)} %get-tuple-element.118, f32[128]{0:T(128)S(1)} %get-tuple-element.103), kind=kOutput, calls=%fused_computation.19 | convolution fusion | flops 537133056 | bytes 5767680 | tf_op jit(solution)/shard_map/dot_general | solution.py:92
  17.7 0.7 fusion.47
  18.4 0.4 fusion.8
  18.8 0.6 fusion.48
  19.6 0.4 scatter.25
  20.0 1.3 maximum_bitcast_fusion
  21.3 25.0 %all_to_all.9 = f32[16,8,2176]{2,1,0:T(8,128)S(1)} all-to-all(f32[16,8,2176]{2,1,0:T(8,128)S(1)} %maximum_bitcast_fusion), channel_id=1, replica_groups=mesh['pos'=16,'exp'=16] {'exp'}, dimensions={0} | all-to-all | bytes 2228224 | tf_op jit(solution)/shard_map/all_to_all | solution.py:100
  46.3 1.0 copy-done.1
  47.5 0.7 fusion.49
  48.6 0.2 fusion.46
  48.8 0.6 fusion.50
  49.6 1.4 %fusion.6 = f32[8,2048]{1,0:T(8,128)S(1)} fusion(f32[16,8,2176]{2,1,0:T(8,128)} %copy-done.1, f32[16,8]{1,0:T(8,128)S(1)} %copy.54), kind=kLoop, calls=%fused_computation.11 | loop fusion | flops 507904 | bytes 1114624 | tf_op jit(solution)/shard_map/reduce_sum | solution.py:104
  51.0 1.7 %collective-permute-start.2 = (f32[8,2176]{1,0:T(8,128)S(1)}, f32[8,2176]{1,0:T(8,128)S(1)}, u32[]{:S(2)}, u32[]{:S(2)}) collective-permute-start(f32[8,2176]{1,0:T(8,128)S(1)} %pad_maximum_fusion.2), channel_id=1, source_target_pairs={{0,16},{16,0},{32,48},{48,32},{64,80},{80,64},{96,112},{112,96},{1... | collective-permute-start | bytes 208904 | tf_op jit(solution)/shard_map/ppermute | solution.py:47
  52.7 0.6 compare_reduce_fusion
  53.4 1.4 %collective-permute-done.2 = f32[8,2176]{1,0:T(8,128)S(1)} collective-permute-done((f32[8,2176]{1,0:T(8,128)S(1)}, f32[8,2176]{1,0:T(8,128)S(1)}, u32[]{:S(2)}, u32[]{:S(2)}) %collective-permute-start.2) | collective-permute-done | bytes 69664 | tf_op jit(solution)/shard_map/ppermute | solution.py:47
  54.8 0.2 exponential_reduce_fusion.5
  55.0 0.7 slice_select_fusion.2
  55.7 5.6 %collective-permute-start.3 = (f32[8,2176]{1,0:T(8,128)S(1)}, f32[8,2176]{1,0:T(8,128)S(1)}, u32[]{:S(2)}, u32[]{:S(2)}) collective-permute-start(f32[8,2176]{1,0:T(8,128)S(1)} %scatter.30), channel_id=1, source_target_pairs={{0,32},{16,48},{32,0},{48,16},{64,96},{80,112},{96,64},{112,80},{1... | collective-permute-start | bytes 208904 | tf_op jit(solution)/shard_map/ppermute | solution.py:47
  61.3 1.7 %collective-permute-done.3 = f32[8,2176]{1,0:T(8,128)S(1)} collective-permute-done((f32[8,2176]{1,0:T(8,128)S(1)}, f32[8,2176]{1,0:T(8,128)S(1)}, u32[]{:S(2)}, u32[]{:S(2)}) %collective-permute-start.3) | collective-permute-done | bytes 69664 | tf_op jit(solution)/shard_map/ppermute | solution.py:47
  63.0 0.2 exponential_reduce_fusion.3
  63.3 0.7 slice_select_fusion.1
  64.0 3.2 %collective-permute-start.4 = (f32[8,2176]{1,0:T(8,128)S(1)}, f32[8,2176]{1,0:T(8,128)S(1)}, u32[]{:S(2)}, u32[]{:S(2)}) collective-permute-start(f32[8,2176]{1,0:T(8,128)S(1)} %scatter.31), channel_id=1, source_target_pairs={{0,64},{16,80},{32,96},{48,112},{64,0},{80,16},{96,32},{112,48},{1... | collective-permute-start | bytes 208904 | tf_op jit(solution)/shard_map/ppermute | solution.py:47
  67.2 4.0 %collective-permute-done.4 = f32[8,2176]{1,0:T(8,128)S(1)} collective-permute-done((f32[8,2176]{1,0:T(8,128)S(1)}, f32[8,2176]{1,0:T(8,128)S(1)}, u32[]{:S(2)}, u32[]{:S(2)}) %collective-permute-start.4) | collective-permute-done | bytes 69664 | tf_op jit(solution)/shard_map/ppermute | solution.py:47
  71.5 0.7 slice_select_fusion
  72.2 2.8 %collective-permute-start.5 = (f32[8,2176]{1,0:T(8,128)S(1)}, f32[8,2176]{1,0:T(8,128)S(1)}, u32[]{:S(2)}, u32[]{:S(2)}) collective-permute-start(f32[8,2176]{1,0:T(8,128)S(1)} %scatter.34), channel_id=1, source_target_pairs={{0,128},{16,144},{32,160},{48,176},{64,192},{80,208},{96,224},{112... | collective-permute-start | bytes 208904 | tf_op jit(solution)/shard_map/ppermute | solution.py:47
  75.0 1.9 %collective-permute-done.5 = f32[8,2176]{1,0:T(8,128)S(1)} collective-permute-done((f32[8,2176]{1,0:T(8,128)S(1)}, f32[8,2176]{1,0:T(8,128)S(1)}, u32[]{:S(2)}, u32[]{:S(2)}) %collective-permute-start.5) | collective-permute-done | bytes 69664 | tf_op jit(solution)/shard_map/ppermute | solution.py:47
  77.2 0.2 slice_reduce_fusion
  77.4 3.0 %fusion = f32[8,2048]{1,0:T(8,128)S(1)} fusion(bf16[1,512,2048]{2,1,0:T(8,128)(2,1)} %param.25, bf16[1,2048,512]{2,1,0:T(8,128)(2,1)} %param.24, f32[8,2176]{1,0:T(8,128)S(1)} %multiply_add_fusion, f32[8]{0:T(128)S(1)} %slice_reduce_fusion), kind=kOutput, calls=%fused_computation.1 | convolution fusion | flops 33624064 | bytes 4325888 | tf_op jit(solution)/shard_map/dot_general | solution.py:114
  80.4 1.3 collective-permute-start.6
  81.7 1.8 %collective-permute-done.6 = f32[8,2048]{1,0:T(8,128)S(1)} collective-permute-done((f32[8,2048]{1,0:T(8,128)S(1)}, f32[8,2048]{1,0:T(8,128)S(1)}, u32[]{:S(2)}, u32[]{:S(2)}) %collective-permute-start.6) | collective-permute-done | bytes 65568 | tf_op jit(solution)/shard_map/ppermute | solution.py:29
  83.5 2.9 %collective-permute-start.7 = (f32[8,2048]{1,0:T(8,128)S(1)}, f32[8,2048]{1,0:T(8,128)S(1)}, u32[]{:S(2)}, u32[]{:S(2)}) collective-permute-start(f32[8,2048]{1,0:T(8,128)S(1)} %add.60), channel_id=1, source_target_pairs={{0,32},{16,48},{32,0},{48,16},{64,96},{80,112},{96,64},{112,80},{1... | collective-permute-start | bytes 196616 | tf_op jit(solution)/shard_map/ppermute | solution.py:29
  86.4 1.7 %collective-permute-done.7 = f32[8,2048]{1,0:T(8,128)S(1)} collective-permute-done((f32[8,2048]{1,0:T(8,128)S(1)}, f32[8,2048]{1,0:T(8,128)S(1)}, u32[]{:S(2)}, u32[]{:S(2)}) %collective-permute-start.7) | collective-permute-done | bytes 65568 | tf_op jit(solution)/shard_map/ppermute | solution.py:29
  88.1 3.2 %collective-permute-start.8 = (f32[8,2048]{1,0:T(8,128)S(1)}, f32[8,2048]{1,0:T(8,128)S(1)}, u32[]{:S(2)}, u32[]{:S(2)}) collective-permute-start(f32[8,2048]{1,0:T(8,128)S(1)} %add.61), channel_id=1, source_target_pairs={{0,64},{16,80},{32,96},{48,112},{64,0},{80,16},{96,32},{112,48},{1... | collective-permute-start | bytes 196616 | tf_op jit(solution)/shard_map/ppermute | solution.py:29
  91.3 4.3 %collective-permute-done.8 = f32[8,2048]{1,0:T(8,128)S(1)} collective-permute-done((f32[8,2048]{1,0:T(8,128)S(1)}, f32[8,2048]{1,0:T(8,128)S(1)}, u32[]{:S(2)}, u32[]{:S(2)}) %collective-permute-start.8) | collective-permute-done | bytes 65568 | tf_op jit(solution)/shard_map/ppermute | solution.py:29
  95.7 3.7 %collective-permute-start.9 = (f32[8,2048]{1,0:T(8,128)S(1)}, f32[8,2048]{1,0:T(8,128)S(1)}, u32[]{:S(2)}, u32[]{:S(2)}) collective-permute-start(f32[8,2048]{1,0:T(8,128)S(1)} %add.62), channel_id=1, source_target_pairs={{0,128},{16,144},{32,160},{48,176},{64,192},{80,208},{96,224},{112... | collective-permute-start | bytes 196616 | tf_op jit(solution)/shard_map/ppermute | solution.py:29
  99.3 1.4 %divide_convert_fusion = bf16[1024,128]{1,0:T(8,128)(2,1)S(1)} fusion(f32[1024,128]{1,0:T(8,128)} %copy-done.2, f32[1024]{0:T(1024)S(1)} %get-tuple-element.102, f32[1024]{0:T(1024)S(1)} %get-tuple-element.104), kind=kLoop, calls=%fused_computation.14 | loop fusion | flops 393216 | bytes 794624 | tf_op jit(solution)/shard_map/convert_element_type | solution.py:118
  100.7 0.9 copy.50
  101.7 27.8 %all_gather.3.slots_ref = bf16[128,2048]{1,0:T(8,128)(2,1)} all-gather(bf16[8,2048]{1,0:T(8,128)(2,1)S(1)} %add_convert_fusion), channel_id=1, replica_groups=mesh['pos'=16,'exp'=16] {'exp'}, dimensions={0}, use_global_device_ids=true | all-gather | bytes 557056 | tf_op jit(solution)/shard_map/all_gather | solution.py:119
  129.5 4.7 %shard_map.55 = bf16[256,4,2048]{2,1,0:T(4,128)(2,1)} custom-call(bf16[1024,128]{1,0:T(8,128)(2,1)} %bitcast.52, bf16[128,2048]{1,0:T(8,128)(2,1)} %all_gather.3.slots_ref), custom_call_target="tpu_custom_call" | custom-call | flops 536870912 | bytes 4980736 | tf_op jit(solution)/shard_map/pallas_call | solution.py:61
  (36 shorter events, 1.9 us)
Async XLA Ops:
  0.0 11.0 %copy-start = (bf16[3,256,2048]{2,1,0:T(8,128)(2,1)S(1)}, bf16[3,256,2048]{2,1,0:T(8,128)(2,1)}, u32[]{:S(2)}) copy-start(bf16[3,256,2048]{2,1,0:T(8,128)(2,1)} %param.22) | copy-start | bytes 9437188
  1.3 7.8 %collective-permute-start = (bf16[4,1,256]{2,1,0:T(2,128)(2,1)S(1)}, bf16[4,1,256]{2,1,0:T(2,128)(2,1)S(1)}, u32[]{:S(2)}, u32[]{:S(2)}) collective-permute-start(bf16[4,1,256]{2,1,0:T(2,128)(2,1)S(1)} %get-tuple-element.116), channel_id=1, source_target_pairs={{0,1},{1,2},{2,3},{3,4},{4,5},{5,6},{6,7},{7,8},{8,9},{9,10},{10,1... | collective-permute-start | bytes 6152 | tf_op jit(solution)/shard_map/ppermute | solution.py:18
  5.8 4.9 %collective-permute-start.1 = (bf16[4,1,256]{2,1,0:T(2,128)(2,1)S(1)}, bf16[4,1,256]{2,1,0:T(2,128)(2,1)S(1)}, u32[]{:S(2)}, u32[]{:S(2)}) collective-permute-start(bf16[4,1,256]{2,1,0:T(2,128)(2,1)S(1)} %get-tuple-element.117), channel_id=1, source_target_pairs={{1,0},{2,1},{3,2},{4,3},{5,4},{6,5},{7,6},{8,7},{9,8},{10,9},{11,1... | collective-permute-start | bytes 6152 | tf_op jit(solution)/shard_map/ppermute | solution.py:19
  11.0 3.7 %copy-start.3 = (bf16[2048,128]{1,0:T(8,128)(2,1)S(1)}, bf16[2048,128]{1,0:T(8,128)(2,1)}, u32[]{:S(2)}) copy-start(bf16[2048,128]{1,0:T(8,128)(2,1)} %param.23) | copy-start | bytes 1572868
  16.0 2.4 %copy-start.2 = (f32[1024,128]{1,0:T(8,128)}, f32[1024,128]{1,0:T(8,128)S(1)}, u32[]{:S(2)}) copy-start(f32[1024,128]{1,0:T(8,128)S(1)} %get-tuple-element.118) | copy-start | bytes 1572868
  46.3 1.0 copy-start.1
  51.0 3.8 %collective-permute-start.2 = (f32[8,2176]{1,0:T(8,128)S(1)}, f32[8,2176]{1,0:T(8,128)S(1)}, u32[]{:S(2)}, u32[]{:S(2)}) collective-permute-start(f32[8,2176]{1,0:T(8,128)S(1)} %pad_maximum_fusion.2), channel_id=1, source_target_pairs={{0,16},{16,0},{32,48},{48,32},{64,80},{80,64},{96,112},{112,96},{1... | collective-permute-start | bytes 208904 | tf_op jit(solution)/shard_map/ppermute | solution.py:47
  55.7 7.3 %collective-permute-start.3 = (f32[8,2176]{1,0:T(8,128)S(1)}, f32[8,2176]{1,0:T(8,128)S(1)}, u32[]{:S(2)}, u32[]{:S(2)}) collective-permute-start(f32[8,2176]{1,0:T(8,128)S(1)} %scatter.30), channel_id=1, source_target_pairs={{0,32},{16,48},{32,0},{48,16},{64,96},{80,112},{96,64},{112,80},{1... | collective-permute-start | bytes 208904 | tf_op jit(solution)/shard_map/ppermute | solution.py:47
  64.0 7.2 %collective-permute-start.4 = (f32[8,2176]{1,0:T(8,128)S(1)}, f32[8,2176]{1,0:T(8,128)S(1)}, u32[]{:S(2)}, u32[]{:S(2)}) collective-permute-start(f32[8,2176]{1,0:T(8,128)S(1)} %scatter.31), channel_id=1, source_target_pairs={{0,64},{16,80},{32,96},{48,112},{64,0},{80,16},{96,32},{112,48},{1... | collective-permute-start | bytes 208904 | tf_op jit(solution)/shard_map/ppermute | solution.py:47
  72.2 4.8 %collective-permute-start.5 = (f32[8,2176]{1,0:T(8,128)S(1)}, f32[8,2176]{1,0:T(8,128)S(1)}, u32[]{:S(2)}, u32[]{:S(2)}) collective-permute-start(f32[8,2176]{1,0:T(8,128)S(1)} %scatter.34), channel_id=1, source_target_pairs={{0,128},{16,144},{32,160},{48,176},{64,192},{80,208},{96,224},{112... | collective-permute-start | bytes 208904 | tf_op jit(solution)/shard_map/ppermute | solution.py:47
  80.4 3.1 %collective-permute-start.6 = (f32[8,2048]{1,0:T(8,128)S(1)}, f32[8,2048]{1,0:T(8,128)S(1)}, u32[]{:S(2)}, u32[]{:S(2)}) collective-permute-start(f32[8,2048]{1,0:T(8,128)S(1)} %fusion), channel_id=1, source_target_pairs={{0,16},{16,0},{32,48},{48,32},{64,80},{80,64},{96,112},{112,96},{1... | collective-permute-start | bytes 196616 | tf_op jit(solution)/shard_map/ppermute | solution.py:29
  83.5 4.6 %collective-permute-start.7 = (f32[8,2048]{1,0:T(8,128)S(1)}, f32[8,2048]{1,0:T(8,128)S(1)}, u32[]{:S(2)}, u32[]{:S(2)}) collective-permute-start(f32[8,2048]{1,0:T(8,128)S(1)} %add.60), channel_id=1, source_target_pairs={{0,32},{16,48},{32,0},{48,16},{64,96},{80,112},{96,64},{112,80},{1... | collective-permute-start | bytes 196616 | tf_op jit(solution)/shard_map/ppermute | solution.py:29
  88.1 7.5 %collective-permute-start.8 = (f32[8,2048]{1,0:T(8,128)S(1)}, f32[8,2048]{1,0:T(8,128)S(1)}, u32[]{:S(2)}, u32[]{:S(2)}) collective-permute-start(f32[8,2048]{1,0:T(8,128)S(1)} %add.61), channel_id=1, source_target_pairs={{0,64},{16,80},{32,96},{48,112},{64,0},{80,16},{96,32},{112,48},{1... | collective-permute-start | bytes 196616 | tf_op jit(solution)/shard_map/ppermute | solution.py:29
  95.7 6.0 %collective-permute-start.9 = (f32[8,2048]{1,0:T(8,128)S(1)}, f32[8,2048]{1,0:T(8,128)S(1)}, u32[]{:S(2)}, u32[]{:S(2)}) collective-permute-start(f32[8,2048]{1,0:T(8,128)S(1)} %add.62), channel_id=1, source_target_pairs={{0,128},{16,144},{32,160},{48,176},{64,192},{80,208},{96,224},{112... | collective-permute-start | bytes 196616 | tf_op jit(solution)/shard_map/ppermute | solution.py:29

commit v8 on v7

--- a/solution.py
+++ b/solution.py
@@ -78,11 +78,28 @@
 def per_device(patches, conv_weight, phi, w_in, w_out):
     channels, periods, samples = patches.shape
     every = ("pos", "exp")
-    padded = with_halo(jnp.swapaxes(patches, 0, 1), ((every, 1),), 1)
+    by_period = jnp.swapaxes(patches, 0, 1)
+    taps = conv_weight.reshape(3 * samples, D)
+    padded = jnp.pad(by_period, ((0, 0), (1, 1), (0, 0)))
     window = jnp.concatenate([padded[:, offset : offset + channels] for offset in range(3)], axis=2)
     window = window.reshape(periods * channels, 3 * samples)
-    taps = conv_weight.reshape(3 * samples, D)
     flat = jnp.dot(window, taps, preferred_element_type=jnp.float32).astype(jnp.bfloat16)
+    flat, first, last = lax.optimization_barrier((flat, by_period[:, :1], by_period[:, -1:]))
+    count = lax.axis_size(every)
+    up = [(i, i + 1) for i in range(count - 1)]
+    before = lax.ppermute(last, every, up)
+    after = lax.ppermute(first, every, [(j, i) for i, j in up])
+    edges = jnp.concatenate(
+        [
+            jnp.concatenate([before, by_period[:, 0:2]], axis=1),
+            jnp.concatenate([by_period[:, -2:], after], axis=1),
+        ],
+        axis=0,
+    ).reshape(2 * periods, 3 * samples)
+    edge_rows = jnp.dot(edges, taps, preferred_element_type=jnp.float32).astype(jnp.bfloat16)
+    flat = flat.reshape(periods, channels, D)
+    flat = flat.at[:, 0].set(edge_rows[:periods]).at[:, channels - 1].set(edge_rows[periods:])
+    flat = flat.reshape(periods * channels, D)
     logits = jnp.dot(flat, phi, preferred_element_type=jnp.float32)
     slots = logits.shape[1]
 

time: 135 us -> 145 us (1.074)
  local copies, waits for them, and re-layouts: 4.75 us -> 10.4 us
  matrix products: 9.69 us -> 14 us
    scatter x0 -> x2, local copies, waits for them, and re-layouts: none -> 3.39 us  [per_device(): flat.at[:, 0].set(edge_rows[:periods]).at[:, channels - 1]]
    slice x1 -> x3, local copies, waits for them, and re-layouts: 0.01 us -> 3.22 us  [the longest x1 1.8 us: per_device(): padded[:, offset:offset + channels]]
    dot_general x1, matrix products: 1.32 us -> 3.78 us  [per_device(): logits = jnp.dot(flat, phi, preferred_element_type=jnp.float32)]
where the time goes in v8:
time: 145 us
  blocking collectives  52.9 us (36%)
  starting transfers between devices  30.9 us (21%)
  waiting for transfers between devices  17.7 us (12%)
  other arithmetic  14 us (10%)
  matrix products  14 us (10%)
  local copies, waits for them, and re-layouts  10.4 us (7%)
  Pallas kernels  4.71 us (3%)
    all_gather x1, blocking collectives, per_device(): slot_all = lax.all_gather(slot_out, 'exp', axis=0, tiled=True)  27.8 us
    all_to_all x1, blocking collectives, per_device(): lax.all_to_all(packed, 'exp', 0, 0, tiled=True)  25 us
    ppermute x4, starting transfers between devices, butterfly_softmax_sum(): value = merge(value, lax.ppermute(value, axis, pairs))  13.4 us
    ppermute x4, starting transfers between devices, butterfly_sum(): value = value + lax.ppermute(value, axis, pairs)  11.1 us
    ppermute x4, waiting for transfers between devices, butterfly_softmax_sum(): value = merge(value, lax.ppermute(value, axis, pairs))  8.98 us
    ppermute x4, waiting for transfers between devices, butterfly_sum(): value = value + lax.ppermute(value, axis, pairs)  7.82 us
    dot_general x1, matrix products, per_device(): jnp.dot(window, taps, preferred_element_type=jnp.float32)  4.94 us
    pallas_call x1, Pallas kernels, mix(): pl.pallas_call(mix_kernel, grid=(channels // block,), in_specs=[pl.BlockS...  4.71 us
  transfers between devices with their start and end apart: 10, of which 8 were waited for; matrix products, arithmetic and copies ran while one was open for 3% of the time, Pallas kernels for 0%

profile of v8, /device:TPU:1, one launch (start us, length us, event | category | flops | bytes accessed | tf_op | source)
XLA Modules:
  0.0 144.8 jit_solution(9607387896201616044)
XLA Ops:
  0.0 1.8 %pad_slice_fusion.1 = (bf16[4,256,256]{2,0,1:T(4,128)(2,1)S(1)}, bf16[4,256,256]{2,0,1:T(4,128)(2,1)S(1)}) fusion(bf16[4,256,256]{2,0,1:T(4,128)(2,1)} %bitcast.61), kind=kLoop, calls=%fused_computation.18 | loop fusion | bytes 1572864 | tf_op jit(solution)/shard_map/slice | solution.py:84
  1.8 0.7 fusion.65
  2.5 1.7 %pad_maximum_fusion = bf16[4,256,768]{2,0,1:T(4,128)(2,1)S(1)} fusion(bf16[4,256,256]{2,0,1:T(4,128)(2,1)S(1)} %get-tuple-element.151, bf16[4,256,256]{2,0,1:T(4,128)(2,1)} %bitcast.63, bf16[4,256,256]{2,0,1:T(4,128)(2,1)S(1)} %get-tuple-element.150), kind=kLoop, calls=%fused_computation.7 | loop fusion | flops 4718592 | bytes 3145728 | tf_op jit(solution)/shard_map/concatenate | solution.py:84
  4.4 4.9 %convolution_convert_fusion = bf16[1024,2048]{1,0:T(8,128)(2,1)} fusion(bf16[1024,768]{1,0:T(8,128)(2,1)S(1)} %bitcast.65, bf16[768,2048]{1,0:T(8,128)(2,1)S(1)} %bitcast.57), kind=kOutput, calls=%fused_computation | convolution fusion | flops 3223322624 | bytes 8912896 | tf_op jit(solution)/shard_map/dot_general | solution.py:86
  9.4 4.5 %collective-permute-start = (bf16[4,1,256]{2,0,1:T(4,128)(2,1)S(1)}, bf16[4,1,256]{2,0,1:T(4,128)(2,1)S(1)}, u32[]{:S(2)}, u32[]{:S(2)}) collective-permute-start(bf16[4,1,256]{2,0,1:T(4,128)(2,1)S(1)} %get-tuple-element.129), channel_id=1, source_target_pairs={{0,1},{1,2},{2,3},{3,4},{4,5},{5,6},{6,7},{7,8},{8,9},{9,10},{10,1... | collective-permute-start | bytes 6152 | tf_op jit(solution)/shard_map/ppermute | solution.py:90
  13.9 1.9 %collective-permute-start.1 = (bf16[4,1,256]{2,0,1:T(4,128)(2,1)S(1)}, bf16[4,1,256]{2,0,1:T(4,128)(2,1)S(1)}, u32[]{:S(2)}, u32[]{:S(2)}) collective-permute-start(bf16[4,1,256]{2,0,1:T(4,128)(2,1)S(1)} %get-tuple-element.130), channel_id=1, source_target_pairs={{1,0},{2,1},{3,2},{4,3},{5,4},{6,5},{7,6},{8,7},{9,8},{10,9},{11,1... | collective-permute-start | bytes 6152 | tf_op jit(solution)/shard_map/ppermute | solution.py:91
  15.8 0.7 fusion.64
  16.5 0.7 compare_reduce_fusion.1
  17.2 0.6 compare_reduce_fusion.2
  17.9 0.9 collective-permute-done.1
  18.8 0.5 fusion
  19.4 1.7 %scatter.30 = bf16[4,256,2048]{2,1,0:T(8,128)(2,1)} dynamic-update-slice(bf16[4,256,2048]{2,1,0:T(8,128)(2,1)} %bitcast.58, bf16[4,1,2048]{2,1,0:T(2,128)(2,1)S(1)} %copy.58, s32[]{:T(128)} %constant.238.clone.1, s32[]{:T(128)} %constant.238.clone.1, s32[]{:T(128)} %constant.238.clone.1) | dynamic-update-slice | bytes 32772 | tf_op jit(solution)/shard_map/scatter | solution.py:101
  21.1 1.7 %scatter.31 = bf16[4,256,2048]{2,1,0:T(8,128)(2,1)} dynamic-update-slice(bf16[4,256,2048]{2,1,0:T(8,128)(2,1)} %scatter.30, bf16[4,1,2048]{2,1,0:T(2,128)(2,1)S(1)} %copy.59, s32[]{:T(128)} %constant.238.clone.1, s32[]{:T(128)} %constant.239.clone.1, s32[]{:T(128)} %constant.238.clone.1) | dynamic-update-slice | bytes 32772 | tf_op jit(solution)/shard_map/scatter | solution.py:101
  22.8 3.8 %fusion.62 = (f32[128]{0:T(128)S(1)}, f32[1024]{0:T(1024)S(1)}, f32[1024,128]{1,0:T(8,128)S(1)}) fusion(bf16[1024,2048]{1,0:T(8,128)(2,1)} %bitcast.59, bf16[2048,128]{1,0:T(8,128)(2,1)} %param.27), kind=kOutput, calls=%fused_computation.94 | convolution fusion | flops 537131904 | bytes 5247488 | tf_op jit(solution)/shard_map/dot_general | solution.py:103
  26.6 1.7 %fusion.9 = f32[128,2048]{1,0:T(8,128)} fusion(bf16[1024,2048]{1,0:T(8,128)(2,1)S(1)} %bitcast.60, f32[1024,128]{1,0:T(8,128)S(1)} %get-tuple-element.154, f32[128]{0:T(128)S(1)} %get-tuple-element.133), kind=kOutput, calls=%fused_computation.19 | convolution fusion | flops 537133056 | bytes 5767680 | tf_op jit(solution)/shard_map/dot_general | solution.py:109
  28.3 0.4 fusion.7
  28.7 0.7 fusion.54
  29.5 0.6 fusion.53
  30.6 1.3 maximum_bitcast_fusion
  31.9 25.0 %all_to_all.9 = f32[16,8,2176]{2,1,0:T(8,128)S(1)} all-to-all(f32[16,8,2176]{2,1,0:T(8,128)S(1)} %maximum_bitcast_fusion), channel_id=1, replica_groups=mesh['pos'=16,'exp'=16] {'exp'}, dimensions={0} | all-to-all | bytes 2228224 | tf_op jit(solution)/shard_map/all_to_all | solution.py:117
  56.9 1.0 copy-done.1
  58.2 0.6 fusion.55
  59.2 0.7 fusion.56
  60.2 1.4 fusion.5
  61.6 1.7 %collective-permute-start.2 = (f32[8,2176]{1,0:T(8,128)S(1)}, f32[8,2176]{1,0:T(8,128)S(1)}, u32[]{:S(2)}, u32[]{:S(2)}) collective-permute-start(f32[8,2176]{1,0:T(8,128)S(1)} %pad_maximum_fusion.1), channel_id=1, source_target_pairs={{0,16},{16,0},{32,48},{48,32},{64,80},{80,64},{96,112},{112,96},{1... | collective-permute-start | bytes 208904 | tf_op jit(solution)/shard_map/ppermute | solution.py:47
  63.3 0.6 compare_reduce_fusion
  63.9 1.4 collective-permute-done.2
  65.6 0.7 slice_select_fusion.2
  66.3 5.6 %collective-permute-start.3 = (f32[8,2176]{1,0:T(8,128)S(1)}, f32[8,2176]{1,0:T(8,128)S(1)}, u32[]{:S(2)}, u32[]{:S(2)}) collective-permute-start(f32[8,2176]{1,0:T(8,128)S(1)} %scatter.40), channel_id=1, source_target_pairs={{0,32},{16,48},{32,0},{48,16},{64,96},{80,112},{96,64},{112,80},{1... | collective-permute-start | bytes 208904 | tf_op jit(solution)/shard_map/ppermute | solution.py:47
  71.9 1.7 %collective-permute-done.3 = f32[8,2176]{1,0:T(8,128)S(1)} collective-permute-done((f32[8,2176]{1,0:T(8,128)S(1)}, f32[8,2176]{1,0:T(8,128)S(1)}, u32[]{:S(2)}, u32[]{:S(2)}) %collective-permute-start.3) | collective-permute-done | bytes 69664 | tf_op jit(solution)/shard_map/ppermute | solution.py:47
  73.8 0.7 slice_select_fusion.1
  74.6 3.2 %collective-permute-start.4 = (f32[8,2176]{1,0:T(8,128)S(1)}, f32[8,2176]{1,0:T(8,128)S(1)}, u32[]{:S(2)}, u32[]{:S(2)}) collective-permute-start(f32[8,2176]{1,0:T(8,128)S(1)} %scatter.41), channel_id=1, source_target_pairs={{0,64},{16,80},{32,96},{48,112},{64,0},{80,16},{96,32},{112,48},{1... | collective-permute-start | bytes 208904 | tf_op jit(solution)/shard_map/ppermute | solution.py:47
  77.8 4.0 %collective-permute-done.4 = f32[8,2176]{1,0:T(8,128)S(1)} collective-permute-done((f32[8,2176]{1,0:T(8,128)S(1)}, f32[8,2176]{1,0:T(8,128)S(1)}, u32[]{:S(2)}, u32[]{:S(2)}) %collective-permute-start.4) | collective-permute-done | bytes 69664 | tf_op jit(solution)/shard_map/ppermute | solution.py:47
  82.0 0.7 slice_select_fusion
  82.8 2.8 %collective-permute-start.5 = (f32[8,2176]{1,0:T(8,128)S(1)}, f32[8,2176]{1,0:T(8,128)S(1)}, u32[]{:S(2)}, u32[]{:S(2)}) collective-permute-start(f32[8,2176]{1,0:T(8,128)S(1)} %scatter.44), channel_id=1, source_target_pairs={{0,128},{16,144},{32,160},{48,176},{64,192},{80,208},{96,224},{112... | collective-permute-start | bytes 208904 | tf_op jit(solution)/shard_map/ppermute | solution.py:47
  85.6 1.9 %collective-permute-done.5 = f32[8,2176]{1,0:T(8,128)S(1)} collective-permute-done((f32[8,2176]{1,0:T(8,128)S(1)}, f32[8,2176]{1,0:T(8,128)S(1)}, u32[]{:S(2)}, u32[]{:S(2)}) %collective-permute-start.5) | collective-permute-done | bytes 69664 | tf_op jit(solution)/shard_map/ppermute | solution.py:47
  87.9 3.0 %fusion.1 = f32[8,2048]{1,0:T(8,128)S(1)} fusion(bf16[1,512,2048]{2,1,0:T(8,128)(2,1)} %param.29, bf16[1,2048,512]{2,1,0:T(8,128)(2,1)} %param.28, f32[8,2176]{1,0:T(8,128)S(1)} %multiply_add_fusion, f32[8]{0:T(128)S(1)} %slice_reduce_fusion), kind=kOutput, calls=%fused_computation.3 | convolution fusion | flops 33624064 | bytes 4325888 | tf_op jit(solution)/shard_map/dot_general | solution.py:131
  90.9 1.3 collective-permute-start.6
  92.3 1.8 %collective-permute-done.6 = f32[8,2048]{1,0:T(8,128)S(1)} collective-permute-done((f32[8,2048]{1,0:T(8,128)S(1)}, f32[8,2048]{1,0:T(8,128)S(1)}, u32[]{:S(2)}, u32[]{:S(2)}) %collective-permute-start.6) | collective-permute-done | bytes 65568 | tf_op jit(solution)/shard_map/ppermute | solution.py:29
  94.1 2.9 %collective-permute-start.7 = (f32[8,2048]{1,0:T(8,128)S(1)}, f32[8,2048]{1,0:T(8,128)S(1)}, u32[]{:S(2)}, u32[]{:S(2)}) collective-permute-start(f32[8,2048]{1,0:T(8,128)S(1)} %add.66), channel_id=1, source_target_pairs={{0,32},{16,48},{32,0},{48,16},{64,96},{80,112},{96,64},{112,80},{1... | collective-permute-start | bytes 196616 | tf_op jit(solution)/shard_map/ppermute | solution.py:29
  97.0 1.7 %collective-permute-done.7 = f32[8,2048]{1,0:T(8,128)S(1)} collective-permute-done((f32[8,2048]{1,0:T(8,128)S(1)}, f32[8,2048]{1,0:T(8,128)S(1)}, u32[]{:S(2)}, u32[]{:S(2)}) %collective-permute-start.7) | collective-permute-done | bytes 65568 | tf_op jit(solution)/shard_map/ppermute | solution.py:29
  98.7 3.2 %collective-permute-start.8 = (f32[8,2048]{1,0:T(8,128)S(1)}, f32[8,2048]{1,0:T(8,128)S(1)}, u32[]{:S(2)}, u32[]{:S(2)}) collective-permute-start(f32[8,2048]{1,0:T(8,128)S(1)} %add.67), channel_id=1, source_target_pairs={{0,64},{16,80},{32,96},{48,112},{64,0},{80,16},{96,32},{112,48},{1... | collective-permute-start | bytes 196616 | tf_op jit(solution)/shard_map/ppermute | solution.py:29
  101.9 4.3 %collective-permute-done.8 = f32[8,2048]{1,0:T(8,128)S(1)} collective-permute-done((f32[8,2048]{1,0:T(8,128)S(1)}, f32[8,2048]{1,0:T(8,128)S(1)}, u32[]{:S(2)}, u32[]{:S(2)}) %collective-permute-start.8) | collective-permute-done | bytes 65568 | tf_op jit(solution)/shard_map/ppermute | solution.py:29
  106.2 3.7 %collective-permute-start.9 = (f32[8,2048]{1,0:T(8,128)S(1)}, f32[8,2048]{1,0:T(8,128)S(1)}, u32[]{:S(2)}, u32[]{:S(2)}) collective-permute-start(f32[8,2048]{1,0:T(8,128)S(1)} %add.68), channel_id=1, source_target_pairs={{0,128},{16,144},{32,160},{48,176},{64,192},{80,208},{96,224},{112... | collective-permute-start | bytes 196616 | tf_op jit(solution)/shard_map/ppermute | solution.py:29
  109.9 1.4 divide_convert_fusion
  111.3 0.9 copy.60
  112.2 27.8 %all_gather.3.slots_ref = bf16[128,2048]{1,0:T(8,128)(2,1)} all-gather(bf16[8,2048]{1,0:T(8,128)(2,1)S(1)} %add_convert_fusion), channel_id=1, replica_groups=mesh['pos'=16,'exp'=16] {'exp'}, dimensions={0}, use_global_device_ids=true | all-gather | bytes 557056 | tf_op jit(solution)/shard_map/all_gather | solution.py:136
  140.1 4.7 %shard_map.55 = bf16[256,4,2048]{2,1,0:T(4,128)(2,1)} custom-call(bf16[1024,128]{1,0:T(8,128)(2,1)} %bitcast.66, bf16[128,2048]{1,0:T(8,128)(2,1)} %all_gather.3.slots_ref), custom_call_target="tpu_custom_call" | custom-call | flops 536870912 | bytes 4980736 | tf_op jit(solution)/shard_map/pallas_call | solution.py:61
  (44 shorter events, 3.2 us)
Async XLA Ops:
  0.0 4.4 %copy-start = (bf16[3,256,2048]{2,1,0:T(8,128)(2,1)S(1)}, bf16[3,256,2048]{2,1,0:T(8,128)(2,1)}, u32[]{:S(2)}) copy-start(bf16[3,256,2048]{2,1,0:T(8,128)(2,1)} %param.26) | copy-start | bytes 9437188
  9.4 8.5 %collective-permute-start = (bf16[4,1,256]{2,0,1:T(4,128)(2,1)S(1)}, bf16[4,1,256]{2,0,1:T(4,128)(2,1)S(1)}, u32[]{:S(2)}, u32[]{:S(2)}) collective-permute-start(bf16[4,1,256]{2,0,1:T(4,128)(2,1)S(1)} %get-tuple-element.129), channel_id=1, source_target_pairs={{0,1},{1,2},{2,3},{3,4},{4,5},{5,6},{6,7},{7,8},{8,9},{9,10},{10,1... | collective-permute-start | bytes 6152 | tf_op jit(solution)/shard_map/ppermute | solution.py:90
  13.9 4.9 %collective-permute-start.1 = (bf16[4,1,256]{2,0,1:T(4,128)(2,1)S(1)}, bf16[4,1,256]{2,0,1:T(4,128)(2,1)S(1)}, u32[]{:S(2)}, u32[]{:S(2)}) collective-permute-start(bf16[4,1,256]{2,0,1:T(4,128)(2,1)S(1)} %get-tuple-element.130), channel_id=1, source_target_pairs={{1,0},{2,1},{3,2},{4,3},{5,4},{6,5},{7,6},{8,7},{9,8},{10,9},{11,1... | collective-permute-start | bytes 6152 | tf_op jit(solution)/shard_map/ppermute | solution.py:91
  22.8 3.8 %copy-start.3 = (bf16[4,256,2048]{2,1,0:T(8,128)(2,1)S(1)}, bf16[4,256,2048]{2,1,0:T(8,128)(2,1)}, u32[]{:S(2)}) copy-start(bf16[4,256,2048]{2,1,0:T(8,128)(2,1)} %scatter.31) | copy-start | bytes 12582916
  26.6 1.7 %copy-start.2 = (f32[1024,128]{1,0:T(8,128)}, f32[1024,128]{1,0:T(8,128)S(1)}, u32[]{:S(2)}) copy-start(f32[1024,128]{1,0:T(8,128)S(1)} %get-tuple-element.154) | copy-start | bytes 1572868
  56.9 1.0 copy-start.1
  61.6 3.7 %collective-permute-start.2 = (f32[8,2176]{1,0:T(8,128)S(1)}, f32[8,2176]{1,0:T(8,128)S(1)}, u32[]{:S(2)}, u32[]{:S(2)}) collective-permute-start(f32[8,2176]{1,0:T(8,128)S(1)} %pad_maximum_fusion.1), channel_id=1, source_target_pairs={{0,16},{16,0},{32,48},{48,32},{64,80},{80,64},{96,112},{112,96},{1... | collective-permute-start | bytes 208904 | tf_op jit(solution)/shard_map/ppermute | solution.py:47
  66.3 7.3 %collective-permute-start.3 = (f32[8,2176]{1,0:T(8,128)S(1)}, f32[8,2176]{1,0:T(8,128)S(1)}, u32[]{:S(2)}, u32[]{:S(2)}) collective-permute-start(f32[8,2176]{1,0:T(8,128)S(1)} %scatter.40), channel_id=1, source_target_pairs={{0,32},{16,48},{32,0},{48,16},{64,96},{80,112},{96,64},{112,80},{1... | collective-permute-start | bytes 208904 | tf_op jit(solution)/shard_map/ppermute | solution.py:47
  74.6 7.2 %collective-permute-start.4 = (f32[8,2176]{1,0:T(8,128)S(1)}, f32[8,2176]{1,0:T(8,128)S(1)}, u32[]{:S(2)}, u32[]{:S(2)}) collective-permute-start(f32[8,2176]{1,0:T(8,128)S(1)} %scatter.41), channel_id=1, source_target_pairs={{0,64},{16,80},{32,96},{48,112},{64,0},{80,16},{96,32},{112,48},{1... | collective-permute-start | bytes 208904 | tf_op jit(solution)/shard_map/ppermute | solution.py:47
  82.8 4.8 %collective-permute-start.5 = (f32[8,2176]{1,0:T(8,128)S(1)}, f32[8,2176]{1,0:T(8,128)S(1)}, u32[]{:S(2)}, u32[]{:S(2)}) collective-permute-start(f32[8,2176]{1,0:T(8,128)S(1)} %scatter.44), channel_id=1, source_target_pairs={{0,128},{16,144},{32,160},{48,176},{64,192},{80,208},{96,224},{112... | collective-permute-start | bytes 208904 | tf_op jit(solution)/shard_map/ppermute | solution.py:47
  90.9 3.1 %collective-permute-start.6 = (f32[8,2048]{1,0:T(8,128)S(1)}, f32[8,2048]{1,0:T(8,128)S(1)}, u32[]{:S(2)}, u32[]{:S(2)}) collective-permute-start(f32[8,2048]{1,0:T(8,128)S(1)} %fusion.1), channel_id=1, source_target_pairs={{0,16},{16,0},{32,48},{48,32},{64,80},{80,64},{96,112},{112,96},{1... | collective-permute-start | bytes 196616 | tf_op jit(solution)/shard_map/ppermute | solution.py:29
  94.1 4.6 %collective-permute-start.7 = (f32[8,2048]{1,0:T(8,128)S(1)}, f32[8,2048]{1,0:T(8,128)S(1)}, u32[]{:S(2)}, u32[]{:S(2)}) collective-permute-start(f32[8,2048]{1,0:T(8,128)S(1)} %add.66), channel_id=1, source_target_pairs={{0,32},{16,48},{32,0},{48,16},{64,96},{80,112},{96,64},{112,80},{1... | collective-permute-start | bytes 196616 | tf_op jit(solution)/shard_map/ppermute | solution.py:29
  98.7 7.5 %collective-permute-start.8 = (f32[8,2048]{1,0:T(8,128)S(1)}, f32[8,2048]{1,0:T(8,128)S(1)}, u32[]{:S(2)}, u32[]{:S(2)}) collective-permute-start(f32[8,2048]{1,0:T(8,128)S(1)} %add.67), channel_id=1, source_target_pairs={{0,64},{16,80},{32,96},{48,112},{64,0},{80,16},{96,32},{112,48},{1... | collective-permute-start | bytes 196616 | tf_op jit(solution)/shard_map/ppermute | solution.py:29
  106.2 6.0 %collective-permute-start.9 = (f32[8,2048]{1,0:T(8,128)S(1)}, f32[8,2048]{1,0:T(8,128)S(1)}, u32[]{:S(2)}, u32[]{:S(2)}) collective-permute-start(f32[8,2048]{1,0:T(8,128)S(1)} %add.68), channel_id=1, source_target_pairs={{0,128},{16,144},{32,160},{48,176},{64,192},{80,208},{96,224},{112... | collective-permute-start | bytes 196616 | tf_op jit(solution)/shard_map/ppermute | solution.py:29

commit v9 on v7

--- a/solution.py
+++ b/solution.py
@@ -32,11 +32,10 @@
 
 
 def merge(mine, theirs):
-    peak = jnp.maximum(mine[:, D], theirs[:, D])
-    a = jnp.exp(mine[:, D] - peak)[:, None]
-    b = jnp.exp(theirs[:, D] - peak)[:, None]
-    merged = mine * a + theirs * b
-    return merged.at[:, D].set(peak)
+    peak = jnp.maximum(mine[:, D : D + 1], theirs[:, D : D + 1])
+    merged = mine * jnp.exp(mine[:, D : D + 1] - peak) + theirs * jnp.exp(theirs[:, D : D + 1] - peak)
+    column = lax.broadcasted_iota(jnp.int32, mine.shape, 1)
+    return jnp.where(column == D, peak, merged)
 
 
 def butterfly_softmax_sum(value, axis):
@@ -54,7 +53,7 @@
     out_ref[...] = part.astype(out_ref.dtype).reshape(out_ref.shape)
 
 
-def mix(combine, slot_all, periods, block=64):
+def mix(combine, slot_all, periods, block=128):
     rows, slots = combine.shape
     channels = rows // periods
     width = slot_all.shape[1]

time: 135 us -> 131 us (0.970)
  other arithmetic: 12.6 us -> 9.84 us
    slice x3 -> x0, other arithmetic: 1.95 us -> none  [merge(): a = jnp.exp(mine[:, D] - peak)[:, None]]
    another operation x7 -> x6, other arithmetic: 4.53 us -> 3.89 us
where the time goes in v9:
time: 131 us
  blocking collectives  52.9 us (40%)
  starting transfers between devices  30.9 us (24%)
  waiting for transfers between devices  19.1 us (15%)
  other arithmetic  9.84 us (8%)
  matrix products  9.69 us (7%)
  local copies, waits for them, and re-layouts  4.46 us (3%)
  Pallas kernels  3.85 us (3%)
    all_gather x1, blocking collectives, per_device(): slot_all = lax.all_gather(slot_out, 'exp', axis=0, tiled=True)  27.8 us
    all_to_all x1, blocking collectives, per_device(): lax.all_to_all(packed, 'exp', 0, 0, tiled=True)  25 us
    ppermute x4, starting transfers between devices, butterfly_softmax_sum(): value = merge(value, lax.ppermute(value, axis, pairs))  13.3 us
    ppermute x4, starting transfers between devices, butterfly_sum(): value = value + lax.ppermute(value, axis, pairs)  11.1 us
    ppermute x4, waiting for transfers between devices, butterfly_softmax_sum(): value = merge(value, lax.ppermute(value, axis, pairs))  9.64 us
    ppermute x4, waiting for transfers between devices, butterfly_sum(): value = value + lax.ppermute(value, axis, pairs)  7.83 us
    ppermute x1, starting transfers between devices, with_halo(): before = lax.ppermute(last, axis, up)  4.5 us
    another operation x6, other arithmetic  3.89 us
  transfers between devices with their start and end apart: 10, of which 8 were waited for; matrix products, arithmetic and copies ran while one was open for 3% of the time, Pallas kernels for 0%

profile of v9, /device:TPU:1, one launch (start us, length us, event | category | flops | bytes accessed | tf_op | source)
XLA Modules:
  0.0 130.9 jit_solution(11318249003472080798)
XLA Ops:
  0.0 1.3 copy.38
  1.3 4.5 %collective-permute-start = (bf16[4,1,256]{2,1,0:T(2,128)(2,1)S(1)}, bf16[4,1,256]{2,1,0:T(2,128)(2,1)S(1)}, u32[]{:S(2)}, u32[]{:S(2)}) collective-permute-start(bf16[4,1,256]{2,1,0:T(2,128)(2,1)S(1)} %get-tuple-element.69), channel_id=1, source_target_pairs={{0,1},{1,2},{2,3},{3,4},{4,5},{5,6},{6,7},{7,8},{8,9},{9,10},{10,1... | collective-permute-start | bytes 6152 | tf_op jit(solution)/shard_map/ppermute | solution.py:18
  5.8 1.9 %collective-permute-start.1 = (bf16[4,1,256]{2,1,0:T(2,128)(2,1)S(1)}, bf16[4,1,256]{2,1,0:T(2,128)(2,1)S(1)}, u32[]{:S(2)}, u32[]{:S(2)}) collective-permute-start(bf16[4,1,256]{2,1,0:T(2,128)(2,1)S(1)} %get-tuple-element.70), channel_id=1, source_target_pairs={{1,0},{2,1},{3,2},{4,3},{5,4},{6,5},{7,6},{8,7},{9,8},{10,9},{11,1... | collective-permute-start | bytes 6152 | tf_op jit(solution)/shard_map/ppermute | solution.py:19
  7.7 0.7 compare_reduce_fusion.1
  8.4 0.6 compare_reduce_fusion
  9.1 1.6 %collective-permute-done.1 = bf16[4,1,256]{2,1,0:T(2,128)(2,1)S(1)} collective-permute-done((bf16[4,1,256]{2,1,0:T(2,128)(2,1)S(1)}, bf16[4,1,256]{2,1,0:T(2,128)(2,1)S(1)}, u32[]{:S(2)}, u32[]{:S(2)}) %collective-permute-start.1) | collective-permute-done | bytes 2080 | tf_op jit(solution)/shard_map/ppermute | solution.py:19
  10.7 0.3 fusion.4
  11.0 3.6 %convolution_convert_fusion = bf16[1024,2048]{1,0:T(8,128)(2,1)S(1)} fusion(bf16[1024,768]{1,0:T(8,128)(2,1)S(1)} %bitcast.57, bf16[768,2048]{1,0:T(8,128)(2,1)S(1)} %bitcast.54), kind=kOutput, calls=%fused_computation | convolution fusion | flops 3223322624 | bytes 8912896 | tf_op jit(solution)/shard_map/dot_general | solution.py:84
  14.7 1.3 %fusion.55 = (f32[128]{0:T(128)S(1)}, f32[1024]{0:T(1024)S(1)}, f32[1024,128]{1,0:T(8,128)S(1)}) fusion(bf16[1024,2048]{1,0:T(8,128)(2,1)S(1)} %convolution_convert_fusion, bf16[2048,128]{1,0:T(8,128)(2,1)S(1)} %copy-done.3), kind=kOutput, calls=%fused_computation.82 | convolution fusion | flops 537131904 | bytes 5247488 | tf_op jit(solution)/shard_map/dot_general | solution.py:85
  16.0 1.7 %fusion.10 = f32[128,2048]{1,0:T(8,128)} fusion(bf16[1024,2048]{1,0:T(8,128)(2,1)S(1)} %convolution_convert_fusion, f32[1024,128]{1,0:T(8,128)S(1)} %get-tuple-element.74, f32[128]{0:T(128)S(1)} %get-tuple-element.55), kind=kOutput, calls=%fused_computation.19 | convolution fusion | flops 537133056 | bytes 5767680 | tf_op jit(solution)/shard_map/dot_general | solution.py:91
  17.7 0.7 fusion.44
  18.4 0.4 fusion.8
  18.8 0.6 fusion.45
  19.6 0.4 scatter.15
  20.0 1.3 maximum_bitcast_fusion
  21.3 25.0 %all_to_all.9 = f32[16,8,2176]{2,1,0:T(8,128)S(1)} all-to-all(f32[16,8,2176]{2,1,0:T(8,128)S(1)} %maximum_bitcast_fusion), channel_id=1, replica_groups=mesh['pos'=16,'exp'=16] {'exp'}, dimensions={0} | all-to-all | bytes 2228224 | tf_op jit(solution)/shard_map/all_to_all | solution.py:99
  46.3 1.0 copy-done.1
  47.3 0.1 fusion.56
  47.5 0.7 fusion.43
  48.2 0.1 copy.34
  48.3 0.1 copy.33
  48.5 0.2 fusion.42
  48.7 0.6 fusion.46
  49.4 1.4 %fusion.6 = f32[8,2048]{1,0:T(8,128)S(1)} fusion(f32[16,8,2176]{2,1,0:T(8,128)} %copy-done.1, f32[16,8]{1,0:T(8,128)S(1)} %copy.30), kind=kLoop, calls=%fused_computation.11 | loop fusion | flops 507904 | bytes 1114624 | tf_op jit(solution)/shard_map/reduce_sum | solution.py:103
  50.9 1.7 %collective-permute-start.2 = (f32[8,2176]{1,0:T(8,128)S(1)}, f32[8,2176]{1,0:T(8,128)S(1)}, u32[]{:S(2)}, u32[]{:S(2)}) collective-permute-start(f32[8,2176]{1,0:T(8,128)S(1)} %pad_maximum_fusion.2), channel_id=1, source_target_pairs={{0,16},{16,0},{32,48},{48,32},{64,80},{80,64},{96,112},{112,96},{1... | collective-permute-start | bytes 208904 | tf_op jit(solution)/shard_map/ppermute | solution.py:46
  52.6 2.0 %collective-permute-done.2 = f32[8,2176]{1,0:T(8,128)S(1)} collective-permute-done((f32[8,2176]{1,0:T(8,128)S(1)}, f32[8,2176]{1,0:T(8,128)S(1)}, u32[]{:S(2)}, u32[]{:S(2)}) %collective-permute-start.2) | collective-permute-done | bytes 69664 | tf_op jit(solution)/shard_map/ppermute | solution.py:46
  54.8 5.6 %collective-permute-start.3 = (f32[8,2176]{1,0:T(8,128)S(1)}, f32[8,2176]{1,0:T(8,128)S(1)}, u32[]{:S(2)}, u32[]{:S(2)}) collective-permute-start(f32[8,2176]{1,0:T(8,128)S(1)} %add_select_fusion.3), channel_id=1, source_target_pairs={{0,32},{16,48},{32,0},{48,16},{64,96},{80,112},{96,64},{112,80},{1... | collective-permute-start | bytes 208904 | tf_op jit(solution)/shard_map/ppermute | solution.py:46
  60.4 1.7 %collective-permute-done.3 = f32[8,2176]{1,0:T(8,128)S(1)} collective-permute-done((f32[8,2176]{1,0:T(8,128)S(1)}, f32[8,2176]{1,0:T(8,128)S(1)}, u32[]{:S(2)}, u32[]{:S(2)}) %collective-permute-start.3) | collective-permute-done | bytes 69664 | tf_op jit(solution)/shard_map/ppermute | solution.py:46
  62.1 0.1 fusion.52
  62.3 3.2 %collective-permute-start.4 = (f32[8,2176]{1,0:T(8,128)S(1)}, f32[8,2176]{1,0:T(8,128)S(1)}, u32[]{:S(2)}, u32[]{:S(2)}) collective-permute-start(f32[8,2176]{1,0:T(8,128)S(1)} %add_select_fusion.2), channel_id=1, source_target_pairs={{0,64},{16,80},{32,96},{48,112},{64,0},{80,16},{96,32},{112,48},{1... | collective-permute-start | bytes 208904 | tf_op jit(solution)/shard_map/ppermute | solution.py:46
  65.5 4.0 %collective-permute-done.4 = f32[8,2176]{1,0:T(8,128)S(1)} collective-permute-done((f32[8,2176]{1,0:T(8,128)S(1)}, f32[8,2176]{1,0:T(8,128)S(1)}, u32[]{:S(2)}, u32[]{:S(2)}) %collective-permute-start.4) | collective-permute-done | bytes 69664 | tf_op jit(solution)/shard_map/ppermute | solution.py:46
  69.5 0.1 fusion.53
  69.8 2.8 %collective-permute-start.5 = (f32[8,2176]{1,0:T(8,128)S(1)}, f32[8,2176]{1,0:T(8,128)S(1)}, u32[]{:S(2)}, u32[]{:S(2)}) collective-permute-start(f32[8,2176]{1,0:T(8,128)S(1)} %add_select_fusion.1), channel_id=1, source_target_pairs={{0,128},{16,144},{32,160},{48,176},{64,192},{80,208},{96,224},{112... | collective-permute-start | bytes 208904 | tf_op jit(solution)/shard_map/ppermute | solution.py:46
  72.6 1.9 %collective-permute-done.5 = f32[8,2176]{1,0:T(8,128)S(1)} collective-permute-done((f32[8,2176]{1,0:T(8,128)S(1)}, f32[8,2176]{1,0:T(8,128)S(1)}, u32[]{:S(2)}, u32[]{:S(2)}) %collective-permute-start.5) | collective-permute-done | bytes 69664 | tf_op jit(solution)/shard_map/ppermute | solution.py:46
  74.5 0.1 fusion.54
  74.8 0.2 slice_reduce_fusion
  74.9 3.0 %fusion = f32[8,2048]{1,0:T(8,128)S(1)} fusion(bf16[1,512,2048]{2,1,0:T(8,128)(2,1)} %param.17, bf16[1,2048,512]{2,1,0:T(8,128)(2,1)} %param.16, f32[8,2176]{1,0:T(8,128)S(1)} %add_select_fusion, f32[8]{0:T(128)S(1)} %slice_reduce_fusion), kind=kOutput, calls=%fused_computation.1 | convolution fusion | flops 33624064 | bytes 4325888 | tf_op jit(solution)/shard_map/dot_general | solution.py:113
  77.9 1.3 collective-permute-start.6
  79.3 1.8 %collective-permute-done.6 = f32[8,2048]{1,0:T(8,128)S(1)} collective-permute-done((f32[8,2048]{1,0:T(8,128)S(1)}, f32[8,2048]{1,0:T(8,128)S(1)}, u32[]{:S(2)}, u32[]{:S(2)}) %collective-permute-start.6) | collective-permute-done | bytes 65568 | tf_op jit(solution)/shard_map/ppermute | solution.py:29
  81.1 2.9 %collective-permute-start.7 = (f32[8,2048]{1,0:T(8,128)S(1)}, f32[8,2048]{1,0:T(8,128)S(1)}, u32[]{:S(2)}, u32[]{:S(2)}) collective-permute-start(f32[8,2048]{1,0:T(8,128)S(1)} %add.52), channel_id=1, source_target_pairs={{0,32},{16,48},{32,0},{48,16},{64,96},{80,112},{96,64},{112,80},{1... | collective-permute-start | bytes 196616 | tf_op jit(solution)/shard_map/ppermute | solution.py:29
  84.0 1.7 %collective-permute-done.7 = f32[8,2048]{1,0:T(8,128)S(1)} collective-permute-done((f32[8,2048]{1,0:T(8,128)S(1)}, f32[8,2048]{1,0:T(8,128)S(1)}, u32[]{:S(2)}, u32[]{:S(2)}) %collective-permute-start.7) | collective-permute-done | bytes 65568 | tf_op jit(solution)/shard_map/ppermute | solution.py:29
  85.7 3.2 %collective-permute-start.8 = (f32[8,2048]{1,0:T(8,128)S(1)}, f32[8,2048]{1,0:T(8,128)S(1)}, u32[]{:S(2)}, u32[]{:S(2)}) collective-permute-start(f32[8,2048]{1,0:T(8,128)S(1)} %add.53), channel_id=1, source_target_pairs={{0,64},{16,80},{32,96},{48,112},{64,0},{80,16},{96,32},{112,48},{1... | collective-permute-start | bytes 196616 | tf_op jit(solution)/shard_map/ppermute | solution.py:29
  88.9 4.3 %collective-permute-done.8 = f32[8,2048]{1,0:T(8,128)S(1)} collective-permute-done((f32[8,2048]{1,0:T(8,128)S(1)}, f32[8,2048]{1,0:T(8,128)S(1)}, u32[]{:S(2)}, u32[]{:S(2)}) %collective-permute-start.8) | collective-permute-done | bytes 65568 | tf_op jit(solution)/shard_map/ppermute | solution.py:29
  93.2 3.7 %collective-permute-start.9 = (f32[8,2048]{1,0:T(8,128)S(1)}, f32[8,2048]{1,0:T(8,128)S(1)}, u32[]{:S(2)}, u32[]{:S(2)}) collective-permute-start(f32[8,2048]{1,0:T(8,128)S(1)} %add.54), channel_id=1, source_target_pairs={{0,128},{16,144},{32,160},{48,176},{64,192},{80,208},{96,224},{112... | collective-permute-start | bytes 196616 | tf_op jit(solution)/shard_map/ppermute | solution.py:29
  96.9 1.4 %divide_convert_fusion = bf16[1024,128]{1,0:T(8,128)(2,1)S(1)} fusion(f32[1024,128]{1,0:T(8,128)} %copy-done.2, f32[1024]{0:T(1024)S(1)} %get-tuple-element.54, f32[1024]{0:T(1024)S(1)} %get-tuple-element.56), kind=kLoop, calls=%fused_computation.14 | loop fusion | flops 393216 | bytes 794624 | tf_op jit(solution)/shard_map/convert_element_type | solution.py:117
  98.3 0.9 copy.25
  99.2 27.8 %all_gather.3.slots_ref = bf16[128,2048]{1,0:T(8,128)(2,1)} all-gather(bf16[8,2048]{1,0:T(8,128)(2,1)S(1)} %add_convert_fusion), channel_id=1, replica_groups=mesh['pos'=16,'exp'=16] {'exp'}, dimensions={0}, use_global_device_ids=true | all-gather | bytes 557056 | tf_op jit(solution)/shard_map/all_gather | solution.py:118
  127.0 3.8 %shard_map.55 = bf16[256,4,2048]{2,1,0:T(4,128)(2,1)} custom-call(bf16[1024,128]{1,0:T(8,128)(2,1)} %bitcast.58, bf16[128,2048]{1,0:T(8,128)(2,1)} %all_gather.3.slots_ref), custom_call_target="tpu_custom_call" | custom-call | flops 536870912 | bytes 4980736 | tf_op jit(solution)/shard_map/pallas_call | solution.py:60
  (31 shorter events, 1.0 us)
Async XLA Ops:
  0.0 11.0 %copy-start = (bf16[3,256,2048]{2,1,0:T(8,128)(2,1)S(1)}, bf16[3,256,2048]{2,1,0:T(8,128)(2,1)}, u32[]{:S(2)}) copy-start(bf16[3,256,2048]{2,1,0:T(8,128)(2,1)} %param.14) | copy-start | bytes 9437188
  1.3 7.8 %collective-permute-start = (bf16[4,1,256]{2,1,0:T(2,128)(2,1)S(1)}, bf16[4,1,256]{2,1,0:T(2,128)(2,1)S(1)}, u32[]{:S(2)}, u32[]{:S(2)}) collective-permute-start(bf16[4,1,256]{2,1,0:T(2,128)(2,1)S(1)} %get-tuple-element.69), channel_id=1, source_target_pairs={{0,1},{1,2},{2,3},{3,4},{4,5},{5,6},{6,7},{7,8},{8,9},{9,10},{10,1... | collective-permute-start | bytes 6152 | tf_op jit(solution)/shard_map/ppermute | solution.py:18
  5.8 4.9 %collective-permute-start.1 = (bf16[4,1,256]{2,1,0:T(2,128)(2,1)S(1)}, bf16[4,1,256]{2,1,0:T(2,128)(2,1)S(1)}, u32[]{:S(2)}, u32[]{:S(2)}) collective-permute-start(bf16[4,1,256]{2,1,0:T(2,128)(2,1)S(1)} %get-tuple-element.70), channel_id=1, source_target_pairs={{1,0},{2,1},{3,2},{4,3},{5,4},{6,5},{7,6},{8,7},{9,8},{10,9},{11,1... | collective-permute-start | bytes 6152 | tf_op jit(solution)/shard_map/ppermute | solution.py:19
  11.0 3.7 %copy-start.3 = (bf16[2048,128]{1,0:T(8,128)(2,1)S(1)}, bf16[2048,128]{1,0:T(8,128)(2,1)}, u32[]{:S(2)}) copy-start(bf16[2048,128]{1,0:T(8,128)(2,1)} %param.15) | copy-start | bytes 1572868
  16.0 2.4 %copy-start.2 = (f32[1024,128]{1,0:T(8,128)}, f32[1024,128]{1,0:T(8,128)S(1)}, u32[]{:S(2)}) copy-start(f32[1024,128]{1,0:T(8,128)S(1)} %get-tuple-element.74) | copy-start | bytes 1572868
  46.3 1.0 copy-start.1
  50.9 3.8 %collective-permute-start.2 = (f32[8,2176]{1,0:T(8,128)S(1)}, f32[8,2176]{1,0:T(8,128)S(1)}, u32[]{:S(2)}, u32[]{:S(2)}) collective-permute-start(f32[8,2176]{1,0:T(8,128)S(1)} %pad_maximum_fusion.2), channel_id=1, source_target_pairs={{0,16},{16,0},{32,48},{48,32},{64,80},{80,64},{96,112},{112,96},{1... | collective-permute-start | bytes 208904 | tf_op jit(solution)/shard_map/ppermute | solution.py:46
  54.8 7.3 %collective-permute-start.3 = (f32[8,2176]{1,0:T(8,128)S(1)}, f32[8,2176]{1,0:T(8,128)S(1)}, u32[]{:S(2)}, u32[]{:S(2)}) collective-permute-start(f32[8,2176]{1,0:T(8,128)S(1)} %add_select_fusion.3), channel_id=1, source_target_pairs={{0,32},{16,48},{32,0},{48,16},{64,96},{80,112},{96,64},{112,80},{1... | collective-permute-start | bytes 208904 | tf_op jit(solution)/shard_map/ppermute | solution.py:46
  62.3 7.2 %collective-permute-start.4 = (f32[8,2176]{1,0:T(8,128)S(1)}, f32[8,2176]{1,0:T(8,128)S(1)}, u32[]{:S(2)}, u32[]{:S(2)}) collective-permute-start(f32[8,2176]{1,0:T(8,128)S(1)} %add_select_fusion.2), channel_id=1, source_target_pairs={{0,64},{16,80},{32,96},{48,112},{64,0},{80,16},{96,32},{112,48},{1... | collective-permute-start | bytes 208904 | tf_op jit(solution)/shard_map/ppermute | solution.py:46
  69.8 4.8 %collective-permute-start.5 = (f32[8,2176]{1,0:T(8,128)S(1)}, f32[8,2176]{1,0:T(8,128)S(1)}, u32[]{:S(2)}, u32[]{:S(2)}) collective-permute-start(f32[8,2176]{1,0:T(8,128)S(1)} %add_select_fusion.1), channel_id=1, source_target_pairs={{0,128},{16,144},{32,160},{48,176},{64,192},{80,208},{96,224},{112... | collective-permute-start | bytes 208904 | tf_op jit(solution)/shard_map/ppermute | solution.py:46
  77.9 3.1 %collective-permute-start.6 = (f32[8,2048]{1,0:T(8,128)S(1)}, f32[8,2048]{1,0:T(8,128)S(1)}, u32[]{:S(2)}, u32[]{:S(2)}) collective-permute-start(f32[8,2048]{1,0:T(8,128)S(1)} %fusion), channel_id=1, source_target_pairs={{0,16},{16,0},{32,48},{48,32},{64,80},{80,64},{96,112},{112,96},{1... | collective-permute-start | bytes 196616 | tf_op jit(solution)/shard_map/ppermute | solution.py:29
  81.1 4.6 %collective-permute-start.7 = (f32[8,2048]{1,0:T(8,128)S(1)}, f32[8,2048]{1,0:T(8,128)S(1)}, u32[]{:S(2)}, u32[]{:S(2)}) collective-permute-start(f32[8,2048]{1,0:T(8,128)S(1)} %add.52), channel_id=1, source_target_pairs={{0,32},{16,48},{32,0},{48,16},{64,96},{80,112},{96,64},{112,80},{1... | collective-permute-start | bytes 196616 | tf_op jit(solution)/shard_map/ppermute | solution.py:29
  85.7 7.5 %collective-permute-start.8 = (f32[8,2048]{1,0:T(8,128)S(1)}, f32[8,2048]{1,0:T(8,128)S(1)}, u32[]{:S(2)}, u32[]{:S(2)}) collective-permute-start(f32[8,2048]{1,0:T(8,128)S(1)} %add.53), channel_id=1, source_target_pairs={{0,64},{16,80},{32,96},{48,112},{64,0},{80,16},{96,32},{112,48},{1... | collective-permute-start | bytes 196616 | tf_op jit(solution)/shard_map/ppermute | solution.py:29
  93.2 6.0 %collective-permute-start.9 = (f32[8,2048]{1,0:T(8,128)S(1)}, f32[8,2048]{1,0:T(8,128)S(1)}, u32[]{:S(2)}, u32[]{:S(2)}) collective-permute-start(f32[8,2048]{1,0:T(8,128)S(1)} %add.54), channel_id=1, source_target_pairs={{0,128},{16,144},{32,160},{48,176},{64,192},{80,208},{96,224},{112... | collective-permute-start | bytes 196616 | tf_op jit(solution)/shard_map/ppermute | solution.py:29

commit v10 on v9

--- a/solution.py
+++ b/solution.py
@@ -53,7 +53,7 @@
     out_ref[...] = part.astype(out_ref.dtype).reshape(out_ref.shape)
 
 
-def mix(combine, slot_all, periods, block=128):
+def mix(combine, slot_all, periods, block=256):
     rows, slots = combine.shape
     channels = rows // periods
     width = slot_all.shape[1]

time: 131 us -> 132 us (level)
  no operation moved by 1% of the time
where the time goes in v10:
time: 132 us; the launch traced here: 131 us
  blocking collectives  52.9 us (40%)
  starting transfers between devices  30.9 us (23%)
  waiting for transfers between devices  19.1 us (14%)
  other arithmetic  9.84 us (7%)
  matrix products  9.69 us (7%)
  local copies, waits for them, and re-layouts  4.46 us (3%)
  Pallas kernels  4.38 us (3%)
    all_gather x1, blocking collectives, per_device(): slot_all = lax.all_gather(slot_out, 'exp', axis=0, tiled=True)  27.8 us
    all_to_all x1, blocking collectives, per_device(): lax.all_to_all(packed, 'exp', 0, 0, tiled=True)  25 us
    ppermute x4, starting transfers between devices, butterfly_softmax_sum(): value = merge(value, lax.ppermute(value, axis, pairs))  13.3 us
    ppermute x4, starting transfers between devices, butterfly_sum(): value = value + lax.ppermute(value, axis, pairs)  11.1 us
    ppermute x4, waiting for transfers between devices, butterfly_softmax_sum(): value = merge(value, lax.ppermute(value, axis, pairs))  9.64 us
    ppermute x4, waiting for transfers between devices, butterfly_sum(): value = value + lax.ppermute(value, axis, pairs)  7.83 us
    ppermute x1, starting transfers between devices, with_halo(): before = lax.ppermute(last, axis, up)  4.5 us
    pallas_call x1, Pallas kernels, mix(): pl.pallas_call(mix_kernel, grid=(channels // block,), in_specs=[pl.BlockS...  4.38 us
  transfers between devices with their start and end apart: 10, of which 8 were waited for; matrix products, arithmetic and copies ran while one was open for 3% of the time, Pallas kernels for 0%

profile of v10, /device:TPU:1, one launch (start us, length us, event | category | flops | bytes accessed | tf_op | source)
XLA Modules:
  0.0 131.4 jit_solution(16841081649949045520)
XLA Ops:
  0.0 1.3 copy.38
  1.3 4.5 %collective-permute-start = (bf16[4,1,256]{2,1,0:T(2,128)(2,1)S(1)}, bf16[4,1,256]{2,1,0:T(2,128)(2,1)S(1)}, u32[]{:S(2)}, u32[]{:S(2)}) collective-permute-start(bf16[4,1,256]{2,1,0:T(2,128)(2,1)S(1)} %get-tuple-element.69), channel_id=1, source_target_pairs={{0,1},{1,2},{2,3},{3,4},{4,5},{5,6},{6,7},{7,8},{8,9},{9,10},{10,1... | collective-permute-start | bytes 6152 | tf_op jit(solution)/shard_map/ppermute | solution.py:18
  5.8 1.9 %collective-permute-start.1 = (bf16[4,1,256]{2,1,0:T(2,128)(2,1)S(1)}, bf16[4,1,256]{2,1,0:T(2,128)(2,1)S(1)}, u32[]{:S(2)}, u32[]{:S(2)}) collective-permute-start(bf16[4,1,256]{2,1,0:T(2,128)(2,1)S(1)} %get-tuple-element.70), channel_id=1, source_target_pairs={{1,0},{2,1},{3,2},{4,3},{5,4},{6,5},{7,6},{8,7},{9,8},{10,9},{11,1... | collective-permute-start | bytes 6152 | tf_op jit(solution)/shard_map/ppermute | solution.py:19
  7.7 0.7 compare_reduce_fusion.1
  8.4 0.6 compare_reduce_fusion
  9.1 1.6 %collective-permute-done.1 = bf16[4,1,256]{2,1,0:T(2,128)(2,1)S(1)} collective-permute-done((bf16[4,1,256]{2,1,0:T(2,128)(2,1)S(1)}, bf16[4,1,256]{2,1,0:T(2,128)(2,1)S(1)}, u32[]{:S(2)}, u32[]{:S(2)}) %collective-permute-start.1) | collective-permute-done | bytes 2080 | tf_op jit(solution)/shard_map/ppermute | solution.py:19
  10.7 0.3 fusion.4
  11.0 3.6 %convolution_convert_fusion = bf16[1024,2048]{1,0:T(8,128)(2,1)S(1)} fusion(bf16[1024,768]{1,0:T(8,128)(2,1)S(1)} %bitcast.57, bf16[768,2048]{1,0:T(8,128)(2,1)S(1)} %bitcast.54), kind=kOutput, calls=%fused_computation | convolution fusion | flops 3223322624 | bytes 8912896 | tf_op jit(solution)/shard_map/dot_general | solution.py:84
  14.7 1.3 %fusion.55 = (f32[128]{0:T(128)S(1)}, f32[1024]{0:T(1024)S(1)}, f32[1024,128]{1,0:T(8,128)S(1)}) fusion(bf16[1024,2048]{1,0:T(8,128)(2,1)S(1)} %convolution_convert_fusion, bf16[2048,128]{1,0:T(8,128)(2,1)S(1)} %copy-done.3), kind=kOutput, calls=%fused_computation.82 | convolution fusion | flops 537131904 | bytes 5247488 | tf_op jit(solution)/shard_map/dot_general | solution.py:85
  16.0 1.7 %fusion.10 = f32[128,2048]{1,0:T(8,128)} fusion(bf16[1024,2048]{1,0:T(8,128)(2,1)S(1)} %convolution_convert_fusion, f32[1024,128]{1,0:T(8,128)S(1)} %get-tuple-element.74, f32[128]{0:T(128)S(1)} %get-tuple-element.55), kind=kOutput, calls=%fused_computation.19 | convolution fusion | flops 537133056 | bytes 5767680 | tf_op jit(solution)/shard_map/dot_general | solution.py:91
  17.7 0.7 fusion.44
  18.4 0.4 fusion.8
  18.8 0.6 fusion.45
  19.6 0.4 scatter.15
  20.0 1.3 maximum_bitcast_fusion
  21.3 25.0 %all_to_all.9 = f32[16,8,2176]{2,1,0:T(8,128)S(1)} all-to-all(f32[16,8,2176]{2,1,0:T(8,128)S(1)} %maximum_bitcast_fusion), channel_id=1, replica_groups=mesh['pos'=16,'exp'=16] {'exp'}, dimensions={0} | all-to-all | bytes 2228224 | tf_op jit(solution)/shard_map/all_to_all | solution.py:99
  46.3 1.0 copy-done.1
  47.3 0.1 fusion.56
  47.5 0.7 fusion.43
  48.2 0.1 copy.34
  48.3 0.1 copy.33
  48.5 0.2 fusion.42
  48.7 0.6 fusion.46
  49.4 1.4 %fusion.6 = f32[8,2048]{1,0:T(8,128)S(1)} fusion(f32[16,8,2176]{2,1,0:T(8,128)} %copy-done.1, f32[16,8]{1,0:T(8,128)S(1)} %copy.30), kind=kLoop, calls=%fused_computation.11 | loop fusion | flops 507904 | bytes 1114624 | tf_op jit(solution)/shard_map/reduce_sum | solution.py:103
  50.9 1.7 %collective-permute-start.2 = (f32[8,2176]{1,0:T(8,128)S(1)}, f32[8,2176]{1,0:T(8,128)S(1)}, u32[]{:S(2)}, u32[]{:S(2)}) collective-permute-start(f32[8,2176]{1,0:T(8,128)S(1)} %pad_maximum_fusion.2), channel_id=1, source_target_pairs={{0,16},{16,0},{32,48},{48,32},{64,80},{80,64},{96,112},{112,96},{1... | collective-permute-start | bytes 208904 | tf_op jit(solution)/shard_map/ppermute | solution.py:46
  52.6 2.0 %collective-permute-done.2 = f32[8,2176]{1,0:T(8,128)S(1)} collective-permute-done((f32[8,2176]{1,0:T(8,128)S(1)}, f32[8,2176]{1,0:T(8,128)S(1)}, u32[]{:S(2)}, u32[]{:S(2)}) %collective-permute-start.2) | collective-permute-done | bytes 69664 | tf_op jit(solution)/shard_map/ppermute | solution.py:46
  54.8 5.6 %collective-permute-start.3 = (f32[8,2176]{1,0:T(8,128)S(1)}, f32[8,2176]{1,0:T(8,128)S(1)}, u32[]{:S(2)}, u32[]{:S(2)}) collective-permute-start(f32[8,2176]{1,0:T(8,128)S(1)} %add_select_fusion.3), channel_id=1, source_target_pairs={{0,32},{16,48},{32,0},{48,16},{64,96},{80,112},{96,64},{112,80},{1... | collective-permute-start | bytes 208904 | tf_op jit(solution)/shard_map/ppermute | solution.py:46
  60.4 1.7 %collective-permute-done.3 = f32[8,2176]{1,0:T(8,128)S(1)} collective-permute-done((f32[8,2176]{1,0:T(8,128)S(1)}, f32[8,2176]{1,0:T(8,128)S(1)}, u32[]{:S(2)}, u32[]{:S(2)}) %collective-permute-start.3) | collective-permute-done | bytes 69664 | tf_op jit(solution)/shard_map/ppermute | solution.py:46
  62.1 0.1 fusion.52
  62.3 3.2 %collective-permute-start.4 = (f32[8,2176]{1,0:T(8,128)S(1)}, f32[8,2176]{1,0:T(8,128)S(1)}, u32[]{:S(2)}, u32[]{:S(2)}) collective-permute-start(f32[8,2176]{1,0:T(8,128)S(1)} %add_select_fusion.2), channel_id=1, source_target_pairs={{0,64},{16,80},{32,96},{48,112},{64,0},{80,16},{96,32},{112,48},{1... | collective-permute-start | bytes 208904 | tf_op jit(solution)/shard_map/ppermute | solution.py:46
  65.5 4.0 %collective-permute-done.4 = f32[8,2176]{1,0:T(8,128)S(1)} collective-permute-done((f32[8,2176]{1,0:T(8,128)S(1)}, f32[8,2176]{1,0:T(8,128)S(1)}, u32[]{:S(2)}, u32[]{:S(2)}) %collective-permute-start.4) | collective-permute-done | bytes 69664 | tf_op jit(solution)/shard_map/ppermute | solution.py:46
  69.5 0.1 fusion.53
  69.8 2.8 %collective-permute-start.5 = (f32[8,2176]{1,0:T(8,128)S(1)}, f32[8,2176]{1,0:T(8,128)S(1)}, u32[]{:S(2)}, u32[]{:S(2)}) collective-permute-start(f32[8,2176]{1,0:T(8,128)S(1)} %add_select_fusion.1), channel_id=1, source_target_pairs={{0,128},{16,144},{32,160},{48,176},{64,192},{80,208},{96,224},{112... | collective-permute-start | bytes 208904 | tf_op jit(solution)/shard_map/ppermute | solution.py:46
  72.6 1.9 %collective-permute-done.5 = f32[8,2176]{1,0:T(8,128)S(1)} collective-permute-done((f32[8,2176]{1,0:T(8,128)S(1)}, f32[8,2176]{1,0:T(8,128)S(1)}, u32[]{:S(2)}, u32[]{:S(2)}) %collective-permute-start.5) | collective-permute-done | bytes 69664 | tf_op jit(solution)/shard_map/ppermute | solution.py:46
  74.5 0.1 fusion.54
  74.8 0.2 slice_reduce_fusion
  74.9 3.0 %fusion = f32[8,2048]{1,0:T(8,128)S(1)} fusion(bf16[1,512,2048]{2,1,0:T(8,128)(2,1)} %param.17, bf16[1,2048,512]{2,1,0:T(8,128)(2,1)} %param.16, f32[8,2176]{1,0:T(8,128)S(1)} %add_select_fusion, f32[8]{0:T(128)S(1)} %slice_reduce_fusion), kind=kOutput, calls=%fused_computation.1 | convolution fusion | flops 33624064 | bytes 4325888 | tf_op jit(solution)/shard_map/dot_general | solution.py:113
  77.9 1.3 collective-permute-start.6
  79.3 1.8 %collective-permute-done.6 = f32[8,2048]{1,0:T(8,128)S(1)} collective-permute-done((f32[8,2048]{1,0:T(8,128)S(1)}, f32[8,2048]{1,0:T(8,128)S(1)}, u32[]{:S(2)}, u32[]{:S(2)}) %collective-permute-start.6) | collective-permute-done | bytes 65568 | tf_op jit(solution)/shard_map/ppermute | solution.py:29
  81.1 2.9 %collective-permute-start.7 = (f32[8,2048]{1,0:T(8,128)S(1)}, f32[8,2048]{1,0:T(8,128)S(1)}, u32[]{:S(2)}, u32[]{:S(2)}) collective-permute-start(f32[8,2048]{1,0:T(8,128)S(1)} %add.52), channel_id=1, source_target_pairs={{0,32},{16,48},{32,0},{48,16},{64,96},{80,112},{96,64},{112,80},{1... | collective-permute-start | bytes 196616 | tf_op jit(solution)/shard_map/ppermute | solution.py:29
  84.0 1.7 %collective-permute-done.7 = f32[8,2048]{1,0:T(8,128)S(1)} collective-permute-done((f32[8,2048]{1,0:T(8,128)S(1)}, f32[8,2048]{1,0:T(8,128)S(1)}, u32[]{:S(2)}, u32[]{:S(2)}) %collective-permute-start.7) | collective-permute-done | bytes 65568 | tf_op jit(solution)/shard_map/ppermute | solution.py:29
  85.7 3.2 %collective-permute-start.8 = (f32[8,2048]{1,0:T(8,128)S(1)}, f32[8,2048]{1,0:T(8,128)S(1)}, u32[]{:S(2)}, u32[]{:S(2)}) collective-permute-start(f32[8,2048]{1,0:T(8,128)S(1)} %add.53), channel_id=1, source_target_pairs={{0,64},{16,80},{32,96},{48,112},{64,0},{80,16},{96,32},{112,48},{1... | collective-permute-start | bytes 196616 | tf_op jit(solution)/shard_map/ppermute | solution.py:29
  88.9 4.3 %collective-permute-done.8 = f32[8,2048]{1,0:T(8,128)S(1)} collective-permute-done((f32[8,2048]{1,0:T(8,128)S(1)}, f32[8,2048]{1,0:T(8,128)S(1)}, u32[]{:S(2)}, u32[]{:S(2)}) %collective-permute-start.8) | collective-permute-done | bytes 65568 | tf_op jit(solution)/shard_map/ppermute | solution.py:29
  93.2 3.7 %collective-permute-start.9 = (f32[8,2048]{1,0:T(8,128)S(1)}, f32[8,2048]{1,0:T(8,128)S(1)}, u32[]{:S(2)}, u32[]{:S(2)}) collective-permute-start(f32[8,2048]{1,0:T(8,128)S(1)} %add.54), channel_id=1, source_target_pairs={{0,128},{16,144},{32,160},{48,176},{64,192},{80,208},{96,224},{112... | collective-permute-start | bytes 196616 | tf_op jit(solution)/shard_map/ppermute | solution.py:29
  96.9 1.4 %divide_convert_fusion = bf16[1024,128]{1,0:T(8,128)(2,1)S(1)} fusion(f32[1024,128]{1,0:T(8,128)} %copy-done.2, f32[1024]{0:T(1024)S(1)} %get-tuple-element.54, f32[1024]{0:T(1024)S(1)} %get-tuple-element.56), kind=kLoop, calls=%fused_computation.14 | loop fusion | flops 393216 | bytes 794624 | tf_op jit(solution)/shard_map/convert_element_type | solution.py:117
  98.3 0.9 copy.25
  99.2 27.8 %all_gather.3.slots_ref = bf16[128,2048]{1,0:T(8,128)(2,1)} all-gather(bf16[8,2048]{1,0:T(8,128)(2,1)S(1)} %add_convert_fusion), channel_id=1, replica_groups=mesh['pos'=16,'exp'=16] {'exp'}, dimensions={0}, use_global_device_ids=true | all-gather | bytes 557056 | tf_op jit(solution)/shard_map/all_gather | solution.py:118
  127.0 4.4 %shard_map.55 = bf16[256,4,2048]{2,1,0:T(4,128)(2,1)} custom-call(bf16[1024,128]{1,0:T(8,128)(2,1)} %bitcast.58, bf16[128,2048]{1,0:T(8,128)(2,1)} %all_gather.3.slots_ref), custom_call_target="tpu_custom_call" | custom-call | flops 536870912 | bytes 4980736 | tf_op jit(solution)/shard_map/pallas_call | solution.py:60
  (31 shorter events, 1.0 us)
Async XLA Ops:
  0.0 11.0 %copy-start = (bf16[3,256,2048]{2,1,0:T(8,128)(2,1)S(1)}, bf16[3,256,2048]{2,1,0:T(8,128)(2,1)}, u32[]{:S(2)}) copy-start(bf16[3,256,2048]{2,1,0:T(8,128)(2,1)} %param.14) | copy-start | bytes 9437188
  1.3 7.8 %collective-permute-start = (bf16[4,1,256]{2,1,0:T(2,128)(2,1)S(1)}, bf16[4,1,256]{2,1,0:T(2,128)(2,1)S(1)}, u32[]{:S(2)}, u32[]{:S(2)}) collective-permute-start(bf16[4,1,256]{2,1,0:T(2,128)(2,1)S(1)} %get-tuple-element.69), channel_id=1, source_target_pairs={{0,1},{1,2},{2,3},{3,4},{4,5},{5,6},{6,7},{7,8},{8,9},{9,10},{10,1... | collective-permute-start | bytes 6152 | tf_op jit(solution)/shard_map/ppermute | solution.py:18
  5.8 4.9 %collective-permute-start.1 = (bf16[4,1,256]{2,1,0:T(2,128)(2,1)S(1)}, bf16[4,1,256]{2,1,0:T(2,128)(2,1)S(1)}, u32[]{:S(2)}, u32[]{:S(2)}) collective-permute-start(bf16[4,1,256]{2,1,0:T(2,128)(2,1)S(1)} %get-tuple-element.70), channel_id=1, source_target_pairs={{1,0},{2,1},{3,2},{4,3},{5,4},{6,5},{7,6},{8,7},{9,8},{10,9},{11,1... | collective-permute-start | bytes 6152 | tf_op jit(solution)/shard_map/ppermute | solution.py:19
  11.0 3.7 %copy-start.3 = (bf16[2048,128]{1,0:T(8,128)(2,1)S(1)}, bf16[2048,128]{1,0:T(8,128)(2,1)}, u32[]{:S(2)}) copy-start(bf16[2048,128]{1,0:T(8,128)(2,1)} %param.15) | copy-start | bytes 1572868
  16.0 2.4 %copy-start.2 = (f32[1024,128]{1,0:T(8,128)}, f32[1024,128]{1,0:T(8,128)S(1)}, u32[]{:S(2)}) copy-start(f32[1024,128]{1,0:T(8,128)S(1)} %get-tuple-element.74) | copy-start | bytes 1572868
  46.3 1.0 copy-start.1
  50.9 3.8 %collective-permute-start.2 = (f32[8,2176]{1,0:T(8,128)S(1)}, f32[8,2176]{1,0:T(8,128)S(1)}, u32[]{:S(2)}, u32[]{:S(2)}) collective-permute-start(f32[8,2176]{1,0:T(8,128)S(1)} %pad_maximum_fusion.2), channel_id=1, source_target_pairs={{0,16},{16,0},{32,48},{48,32},{64,80},{80,64},{96,112},{112,96},{1... | collective-permute-start | bytes 208904 | tf_op jit(solution)/shard_map/ppermute | solution.py:46
  54.8 7.3 %collective-permute-start.3 = (f32[8,2176]{1,0:T(8,128)S(1)}, f32[8,2176]{1,0:T(8,128)S(1)}, u32[]{:S(2)}, u32[]{:S(2)}) collective-permute-start(f32[8,2176]{1,0:T(8,128)S(1)} %add_select_fusion.3), channel_id=1, source_target_pairs={{0,32},{16,48},{32,0},{48,16},{64,96},{80,112},{96,64},{112,80},{1... | collective-permute-start | bytes 208904 | tf_op jit(solution)/shard_map/ppermute | solution.py:46
  62.3 7.2 %collective-permute-start.4 = (f32[8,2176]{1,0:T(8,128)S(1)}, f32[8,2176]{1,0:T(8,128)S(1)}, u32[]{:S(2)}, u32[]{:S(2)}) collective-permute-start(f32[8,2176]{1,0:T(8,128)S(1)} %add_select_fusion.2), channel_id=1, source_target_pairs={{0,64},{16,80},{32,96},{48,112},{64,0},{80,16},{96,32},{112,48},{1... | collective-permute-start | bytes 208904 | tf_op jit(solution)/shard_map/ppermute | solution.py:46
  69.8 4.8 %collective-permute-start.5 = (f32[8,2176]{1,0:T(8,128)S(1)}, f32[8,2176]{1,0:T(8,128)S(1)}, u32[]{:S(2)}, u32[]{:S(2)}) collective-permute-start(f32[8,2176]{1,0:T(8,128)S(1)} %add_select_fusion.1), channel_id=1, source_target_pairs={{0,128},{16,144},{32,160},{48,176},{64,192},{80,208},{96,224},{112... | collective-permute-start | bytes 208904 | tf_op jit(solution)/shard_map/ppermute | solution.py:46
  77.9 3.1 %collective-permute-start.6 = (f32[8,2048]{1,0:T(8,128)S(1)}, f32[8,2048]{1,0:T(8,128)S(1)}, u32[]{:S(2)}, u32[]{:S(2)}) collective-permute-start(f32[8,2048]{1,0:T(8,128)S(1)} %fusion), channel_id=1, source_target_pairs={{0,16},{16,0},{32,48},{48,32},{64,80},{80,64},{96,112},{112,96},{1... | collective-permute-start | bytes 196616 | tf_op jit(solution)/shard_map/ppermute | solution.py:29
  81.1 4.6 %collective-permute-start.7 = (f32[8,2048]{1,0:T(8,128)S(1)}, f32[8,2048]{1,0:T(8,128)S(1)}, u32[]{:S(2)}, u32[]{:S(2)}) collective-permute-start(f32[8,2048]{1,0:T(8,128)S(1)} %add.52), channel_id=1, source_target_pairs={{0,32},{16,48},{32,0},{48,16},{64,96},{80,112},{96,64},{112,80},{1... | collective-permute-start | bytes 196616 | tf_op jit(solution)/shard_map/ppermute | solution.py:29
  85.7 7.5 %collective-permute-start.8 = (f32[8,2048]{1,0:T(8,128)S(1)}, f32[8,2048]{1,0:T(8,128)S(1)}, u32[]{:S(2)}, u32[]{:S(2)}) collective-permute-start(f32[8,2048]{1,0:T(8,128)S(1)} %add.53), channel_id=1, source_target_pairs={{0,64},{16,80},{32,96},{48,112},{64,0},{80,16},{96,32},{112,48},{1... | collective-permute-start | bytes 196616 | tf_op jit(solution)/shard_map/ppermute | solution.py:29
  93.2 6.0 %collective-permute-start.9 = (f32[8,2048]{1,0:T(8,128)S(1)}, f32[8,2048]{1,0:T(8,128)S(1)}, u32[]{:S(2)}, u32[]{:S(2)}) collective-permute-start(f32[8,2048]{1,0:T(8,128)S(1)} %add.54), channel_id=1, source_target_pairs={{0,128},{16,144},{32,160},{48,176},{64,192},{80,208},{96,224},{112... | collective-permute-start | bytes 196616 | tf_op jit(solution)/shard_map/ppermute | solution.py:29

commit v11 on v9

--- a/solution.py
+++ b/solution.py
@@ -11,12 +11,13 @@
 def with_halo(array, sides, width):
     for axis, dim in sides:
         count, length = (lax.axis_size(axis), array.shape[dim])
-        up = [(i, (i + 1) % count) for i in range(count - 1)]
+        index = lax.axis_index(axis)
+        up = [(i, (i + 1) % count) for i in range(count)]
         down = [(j, i) for i, j in up]
         last = lax.slice_in_dim(array, length - width, length, axis=dim)
         initial = lax.slice_in_dim(array, 0, width, axis=dim)
-        before = lax.ppermute(last, axis, up)
-        after = lax.ppermute(initial, axis, down)
+        before = jnp.where(index == 0, 0, lax.ppermute(last, axis, up)).astype(array.dtype)
+        after = jnp.where(index == count - 1, 0, lax.ppermute(initial, axis, down)).astype(array.dtype)
         array = jnp.concatenate([before, array, after], axis=dim)
     return array
 

time: 131 us -> 130 us (level)
  starting transfers between devices: 30.9 us -> 23.7 us
  blocking collectives: 52.9 us -> 55.6 us
  other arithmetic: 9.84 us -> 11.3 us
    ppermute x2, starting transfers between devices: 6.42 us -> 3.37 us  [the longest x1 2.67 us: with_halo(): lax.ppermute(last, axis, up)]
    ppermute x4, starting transfers between devices: 13.3 us -> 10.7 us  [butterfly_softmax_sum(): value = merge(value, lax.ppermute(value, axis, pairs))]
    all_to_all x1, blocking collectives: 25 us -> 26.6 us  [per_device(): lax.all_to_all(packed, 'exp', 0, 0, tiled=True)]
    ppermute x4, starting transfers between devices: 11.1 us -> 9.62 us  [butterfly_sum(): value = value + lax.ppermute(value, axis, pairs)]
    concatenate x1, other arithmetic: 0.27 us -> 1.71 us  [per_device(): jnp.concatenate([padded[:, offset:offset + channels] for offset in range(...]
    unnamed x12 -> x14, local copies, waits for them, and re-layouts: 2.6 us -> 3.39 us
where the time goes in v11:
time: 130 us; the launch traced here: 129 us
  blocking collectives  55.6 us (43%)
  starting transfers between devices  23.7 us (18%)
  waiting for transfers between devices  19.7 us (15%)
  other arithmetic  11.3 us (9%)
  matrix products  9.69 us (7%)
  local copies, waits for them, and re-layouts  5.25 us (4%)
  Pallas kernels  3.85 us (3%)
    all_gather x1, blocking collectives, per_device(): slot_all = lax.all_gather(slot_out, 'exp', axis=0, tiled=True)  29 us
    all_to_all x1, blocking collectives, per_device(): lax.all_to_all(packed, 'exp', 0, 0, tiled=True)  26.6 us
    ppermute x4, starting transfers between devices, butterfly_softmax_sum(): value = merge(value, lax.ppermute(value, axis, pairs))  10.7 us
    ppermute x4, waiting for transfers between devices, butterfly_softmax_sum(): value = merge(value, lax.ppermute(value, axis, pairs))  10.7 us
    ppermute x4, starting transfers between devices, butterfly_sum(): value = value + lax.ppermute(value, axis, pairs)  9.62 us
    ppermute x4, waiting for transfers between devices, butterfly_sum(): value = value + lax.ppermute(value, axis, pairs)  8.08 us
    another operation x6, other arithmetic  3.89 us
    pallas_call x1, Pallas kernels, mix(): pl.pallas_call(mix_kernel, grid=(channels // block,), in_specs=[pl.BlockS...  3.85 us
  transfers between devices with their start and end apart: 10, of which 8 were waited for; matrix products, arithmetic and copies ran while one was open for 3% of the time, Pallas kernels for 0%

profile of v11, /device:TPU:1, one launch (start us, length us, event | category | flops | bytes accessed | tf_op | source)
XLA Modules:
  0.0 129.4 jit_solution(17578892404498138993)
XLA Ops:
  0.0 1.3 copy.38
  1.3 0.8 copy-done.3
  2.1 2.7 %collective-permute-start = (bf16[4,1,256]{2,1,0:T(2,128)(2,1)S(1)}, bf16[4,1,256]{2,1,0:T(2,128)(2,1)S(1)}, u32[]{:S(2)}, u32[]{:S(2)}) collective-permute-start(bf16[4,1,256]{2,1,0:T(2,128)(2,1)S(1)} %get-tuple-element.69), channel_id=1, source_target_pairs={{0,1},{1,2},{2,3},{3,4},{4,5},{5,6},{6,7},{7,8},{8,9},{9,10},{10,1... | collective-permute-start | bytes 6152 | tf_op jit(solution)/shard_map/ppermute | solution.py:19
  4.7 0.7 collective-permute-start.1
  5.4 0.7 compare_reduce_fusion.1
  6.2 0.6 compare_reduce_fusion
  6.8 1.0 collective-permute-done.1
  7.8 1.7 %fusion.4 = bf16[4,256,768]{2,1,0:T(8,128)(2,1)S(1)} fusion(bf16[4,1,256]{2,1,0:T(2,128)(2,1)S(1)} %broadcast_select_fusion, bf16[4,256,256]{2,1,0:T(8,128)(2,1)} %bitcast.56, bf16[4,1,256]{2,1,0:T(2,128)(2,1)S(1)} %broadcast_select_fusion.1), kind=kLoop, calls=%fused_computation.6 | loop fusion | flops 7864320 | bytes 2101248 | tf_op jit(solution)/shard_map/concatenate | solution.py:82
  9.5 3.6 %convolution_convert_fusion = bf16[1024,2048]{1,0:T(8,128)(2,1)S(1)} fusion(bf16[1024,768]{1,0:T(8,128)(2,1)S(1)} %bitcast.57, bf16[768,2048]{1,0:T(8,128)(2,1)S(1)} %bitcast.54), kind=kOutput, calls=%fused_computation | convolution fusion | flops 3223322624 | bytes 8912896 | tf_op jit(solution)/shard_map/dot_general | solution.py:85
  13.2 1.3 %fusion.55 = (f32[128]{0:T(128)S(1)}, f32[1024]{0:T(1024)S(1)}, f32[1024,128]{1,0:T(8,128)S(1)}) fusion(bf16[1024,2048]{1,0:T(8,128)(2,1)S(1)} %convolution_convert_fusion, bf16[2048,128]{1,0:T(8,128)(2,1)S(1)} %copy-done.4), kind=kOutput, calls=%fused_computation.84 | convolution fusion | flops 537131904 | bytes 5247488 | tf_op jit(solution)/shard_map/dot_general | solution.py:86
  14.5 1.7 %fusion.10 = f32[128,2048]{1,0:T(8,128)} fusion(bf16[1024,2048]{1,0:T(8,128)(2,1)S(1)} %convolution_convert_fusion, f32[1024,128]{1,0:T(8,128)S(1)} %get-tuple-element.74, f32[128]{0:T(128)S(1)} %get-tuple-element.55), kind=kOutput, calls=%fused_computation.19 | convolution fusion | flops 537133056 | bytes 5767680 | tf_op jit(solution)/shard_map/dot_general | solution.py:92
  16.2 0.7 fusion.44
  16.9 0.4 fusion.8
  17.3 0.6 fusion.45
  18.1 0.4 scatter.15
  18.5 1.3 %maximum_bitcast_fusion = f32[16,8,2176]{2,1,0:T(8,128)S(1)} fusion(f32[128,128]{1,0:T(8,128)S(1)} %scatter.15, f32[128,2048]{1,0:T(8,128)} %fusion.10), kind=kLoop, calls=%fused_computation.9 | loop fusion | flops 278528 | bytes 2228224 | tf_op jit(solution)/shard_map/all_to_all | solution.py:100
  19.8 26.6 %all_to_all.9 = f32[16,8,2176]{2,1,0:T(8,128)S(1)} all-to-all(f32[16,8,2176]{2,1,0:T(8,128)S(1)} %maximum_bitcast_fusion), channel_id=1, replica_groups=mesh['pos'=16,'exp'=16] {'exp'}, dimensions={0} | all-to-all | bytes 2228224 | tf_op jit(solution)/shard_map/all_to_all | solution.py:100
  46.4 1.0 copy-done.1
  47.4 0.1 fusion.56
  47.5 0.7 fusion.43
  48.4 0.1 copy.33
  48.6 0.2 fusion.42
  48.8 0.6 fusion.46
  49.5 1.4 %fusion.6 = f32[8,2048]{1,0:T(8,128)S(1)} fusion(f32[16,8,2176]{2,1,0:T(8,128)} %copy-done.1, f32[16,8]{1,0:T(8,128)S(1)} %copy.30), kind=kLoop, calls=%fused_computation.11 | loop fusion | flops 507904 | bytes 1114624 | tf_op jit(solution)/shard_map/reduce_sum | solution.py:104
  50.9 0.2 collective-permute-start.2
  51.1 3.1 %collective-permute-done.2 = f32[8,2176]{1,0:T(8,128)S(1)} collective-permute-done((f32[8,2176]{1,0:T(8,128)S(1)}, f32[8,2176]{1,0:T(8,128)S(1)}, u32[]{:S(2)}, u32[]{:S(2)}) %collective-permute-start.2) | collective-permute-done | bytes 69664 | tf_op jit(solution)/shard_map/ppermute | solution.py:47
  54.4 4.6 %collective-permute-start.3 = (f32[8,2176]{1,0:T(8,128)S(1)}, f32[8,2176]{1,0:T(8,128)S(1)}, u32[]{:S(2)}, u32[]{:S(2)}) collective-permute-start(f32[8,2176]{1,0:T(8,128)S(1)} %add_select_fusion.3), channel_id=1, source_target_pairs={{0,32},{16,48},{32,0},{48,16},{64,96},{80,112},{96,64},{112,80},{1... | collective-permute-start | bytes 208904 | tf_op jit(solution)/shard_map/ppermute | solution.py:47
  58.9 1.7 %collective-permute-done.3 = f32[8,2176]{1,0:T(8,128)S(1)} collective-permute-done((f32[8,2176]{1,0:T(8,128)S(1)}, f32[8,2176]{1,0:T(8,128)S(1)}, u32[]{:S(2)}, u32[]{:S(2)}) %collective-permute-start.3) | collective-permute-done | bytes 69664 | tf_op jit(solution)/shard_map/ppermute | solution.py:47
  60.6 0.1 fusion.52
  60.9 3.2 %collective-permute-start.4 = (f32[8,2176]{1,0:T(8,128)S(1)}, f32[8,2176]{1,0:T(8,128)S(1)}, u32[]{:S(2)}, u32[]{:S(2)}) collective-permute-start(f32[8,2176]{1,0:T(8,128)S(1)} %add_select_fusion.2), channel_id=1, source_target_pairs={{0,64},{16,80},{32,96},{48,112},{64,0},{80,16},{96,32},{112,48},{1... | collective-permute-start | bytes 208904 | tf_op jit(solution)/shard_map/ppermute | solution.py:47
  64.0 4.0 %collective-permute-done.4 = f32[8,2176]{1,0:T(8,128)S(1)} collective-permute-done((f32[8,2176]{1,0:T(8,128)S(1)}, f32[8,2176]{1,0:T(8,128)S(1)}, u32[]{:S(2)}, u32[]{:S(2)}) %collective-permute-start.4) | collective-permute-done | bytes 69664 | tf_op jit(solution)/shard_map/ppermute | solution.py:47
  68.0 0.1 fusion.53
  68.3 2.8 %collective-permute-start.5 = (f32[8,2176]{1,0:T(8,128)S(1)}, f32[8,2176]{1,0:T(8,128)S(1)}, u32[]{:S(2)}, u32[]{:S(2)}) collective-permute-start(f32[8,2176]{1,0:T(8,128)S(1)} %add_select_fusion.1), channel_id=1, source_target_pairs={{0,128},{16,144},{32,160},{48,176},{64,192},{80,208},{96,224},{112... | collective-permute-start | bytes 208904 | tf_op jit(solution)/shard_map/ppermute | solution.py:47
  71.1 1.9 %collective-permute-done.5 = f32[8,2176]{1,0:T(8,128)S(1)} collective-permute-done((f32[8,2176]{1,0:T(8,128)S(1)}, f32[8,2176]{1,0:T(8,128)S(1)}, u32[]{:S(2)}, u32[]{:S(2)}) %collective-permute-start.5) | collective-permute-done | bytes 69664 | tf_op jit(solution)/shard_map/ppermute | solution.py:47
  73.0 0.1 fusion.54
  73.3 0.2 slice_reduce_fusion
  73.5 3.0 %fusion = f32[8,2048]{1,0:T(8,128)S(1)} fusion(bf16[1,512,2048]{2,1,0:T(8,128)(2,1)} %param.17, bf16[1,2048,512]{2,1,0:T(8,128)(2,1)} %param.16, f32[8,2176]{1,0:T(8,128)S(1)} %add_select_fusion, f32[8]{0:T(128)S(1)} %slice_reduce_fusion), kind=kOutput, calls=%fused_computation.1 | convolution fusion | flops 33624064 | bytes 4325888 | tf_op jit(solution)/shard_map/dot_general | solution.py:114
  76.5 1.3 %collective-permute-start.6 = (f32[8,2048]{1,0:T(8,128)S(1)}, f32[8,2048]{1,0:T(8,128)S(1)}, u32[]{:S(2)}, u32[]{:S(2)}) collective-permute-start(f32[8,2048]{1,0:T(8,128)S(1)} %fusion), channel_id=1, source_target_pairs={{0,16},{16,0},{32,48},{48,32},{64,80},{80,64},{96,112},{112,96},{1... | collective-permute-start | bytes 196616 | tf_op jit(solution)/shard_map/ppermute | solution.py:30
  77.8 1.8 %collective-permute-done.6 = f32[8,2048]{1,0:T(8,128)S(1)} collective-permute-done((f32[8,2048]{1,0:T(8,128)S(1)}, f32[8,2048]{1,0:T(8,128)S(1)}, u32[]{:S(2)}, u32[]{:S(2)}) %collective-permute-start.6) | collective-permute-done | bytes 65568 | tf_op jit(solution)/shard_map/ppermute | solution.py:30
  79.6 2.9 %collective-permute-start.7 = (f32[8,2048]{1,0:T(8,128)S(1)}, f32[8,2048]{1,0:T(8,128)S(1)}, u32[]{:S(2)}, u32[]{:S(2)}) collective-permute-start(f32[8,2048]{1,0:T(8,128)S(1)} %add.56), channel_id=1, source_target_pairs={{0,32},{16,48},{32,0},{48,16},{64,96},{80,112},{96,64},{112,80},{1... | collective-permute-start | bytes 196616 | tf_op jit(solution)/shard_map/ppermute | solution.py:30
  82.5 1.7 %collective-permute-done.7 = f32[8,2048]{1,0:T(8,128)S(1)} collective-permute-done((f32[8,2048]{1,0:T(8,128)S(1)}, f32[8,2048]{1,0:T(8,128)S(1)}, u32[]{:S(2)}, u32[]{:S(2)}) %collective-permute-start.7) | collective-permute-done | bytes 65568 | tf_op jit(solution)/shard_map/ppermute | solution.py:30
  84.2 2.7 %collective-permute-start.8 = (f32[8,2048]{1,0:T(8,128)S(1)}, f32[8,2048]{1,0:T(8,128)S(1)}, u32[]{:S(2)}, u32[]{:S(2)}) collective-permute-start(f32[8,2048]{1,0:T(8,128)S(1)} %add.57), channel_id=1, source_target_pairs={{0,64},{16,80},{32,96},{48,112},{64,0},{80,16},{96,32},{112,48},{1... | collective-permute-start | bytes 196616 | tf_op jit(solution)/shard_map/ppermute | solution.py:30
  86.9 4.6 %collective-permute-done.8 = f32[8,2048]{1,0:T(8,128)S(1)} collective-permute-done((f32[8,2048]{1,0:T(8,128)S(1)}, f32[8,2048]{1,0:T(8,128)S(1)}, u32[]{:S(2)}, u32[]{:S(2)}) %collective-permute-start.8) | collective-permute-done | bytes 65568 | tf_op jit(solution)/shard_map/ppermute | solution.py:30
  91.5 2.7 %collective-permute-start.9 = (f32[8,2048]{1,0:T(8,128)S(1)}, f32[8,2048]{1,0:T(8,128)S(1)}, u32[]{:S(2)}, u32[]{:S(2)}) collective-permute-start(f32[8,2048]{1,0:T(8,128)S(1)} %add.58), channel_id=1, source_target_pairs={{0,128},{16,144},{32,160},{48,176},{64,192},{80,208},{96,224},{112... | collective-permute-start | bytes 196616 | tf_op jit(solution)/shard_map/ppermute | solution.py:30
  94.2 1.4 %divide_convert_fusion = bf16[1024,128]{1,0:T(8,128)(2,1)S(1)} fusion(f32[1024,128]{1,0:T(8,128)} %copy-done.2, f32[1024]{0:T(1024)S(1)} %get-tuple-element.54, f32[1024]{0:T(1024)S(1)} %get-tuple-element.56), kind=kLoop, calls=%fused_computation.14 | loop fusion | flops 393216 | bytes 794624 | tf_op jit(solution)/shard_map/convert_element_type | solution.py:118
  95.6 0.9 copy.25
  96.5 29.0 %all_gather.3.slots_ref = bf16[128,2048]{1,0:T(8,128)(2,1)} all-gather(bf16[8,2048]{1,0:T(8,128)(2,1)S(1)} %add_convert_fusion), channel_id=1, replica_groups=mesh['pos'=16,'exp'=16] {'exp'}, dimensions={0}, use_global_device_ids=true | all-gather | bytes 557056 | tf_op jit(solution)/shard_map/all_gather | solution.py:119
  125.6 3.9 %shard_map.55 = bf16[256,4,2048]{2,1,0:T(4,128)(2,1)} custom-call(bf16[1024,128]{1,0:T(8,128)(2,1)} %bitcast.58, bf16[128,2048]{1,0:T(8,128)(2,1)} %all_gather.3.slots_ref), custom_call_target="tpu_custom_call" | custom-call | flops 536870912 | bytes 4980736 | tf_op jit(solution)/shard_map/pallas_call | solution.py:61
  (35 shorter events, 1.1 us)
Async XLA Ops:
  0.0 9.5 %copy-start = (bf16[3,256,2048]{2,1,0:T(8,128)(2,1)S(1)}, bf16[3,256,2048]{2,1,0:T(8,128)(2,1)}, u32[]{:S(2)}) copy-start(bf16[3,256,2048]{2,1,0:T(8,128)(2,1)} %param.14) | copy-start | bytes 9437188
  1.3 0.8 copy-start.3
  2.1 4.7 %collective-permute-start = (bf16[4,1,256]{2,1,0:T(2,128)(2,1)S(1)}, bf16[4,1,256]{2,1,0:T(2,128)(2,1)S(1)}, u32[]{:S(2)}, u32[]{:S(2)}) collective-permute-start(bf16[4,1,256]{2,1,0:T(2,128)(2,1)S(1)} %get-tuple-element.69), channel_id=1, source_target_pairs={{0,1},{1,2},{2,3},{3,4},{4,5},{5,6},{6,7},{7,8},{8,9},{9,10},{10,1... | collective-permute-start | bytes 6152 | tf_op jit(solution)/shard_map/ppermute | solution.py:19
  4.7 3.0 %collective-permute-start.1 = (bf16[4,1,256]{2,1,0:T(2,128)(2,1)S(1)}, bf16[4,1,256]{2,1,0:T(2,128)(2,1)S(1)}, u32[]{:S(2)}, u32[]{:S(2)}) collective-permute-start(bf16[4,1,256]{2,1,0:T(2,128)(2,1)S(1)} %get-tuple-element.70), channel_id=1, source_target_pairs={{1,0},{2,1},{3,2},{4,3},{5,4},{6,5},{7,6},{8,7},{9,8},{10,9},{11,1... | collective-permute-start | bytes 6152 | tf_op jit(solution)/shard_map/ppermute | solution.py:20
  9.5 3.7 %copy-start.4 = (bf16[2048,128]{1,0:T(8,128)(2,1)S(1)}, bf16[2048,128]{1,0:T(8,128)(2,1)}, u32[]{:S(2)}) copy-start(bf16[2048,128]{1,0:T(8,128)(2,1)} %param.15) | copy-start | bytes 1572868
  14.5 2.4 %copy-start.2 = (f32[1024,128]{1,0:T(8,128)}, f32[1024,128]{1,0:T(8,128)S(1)}, u32[]{:S(2)}) copy-start(f32[1024,128]{1,0:T(8,128)S(1)} %get-tuple-element.74) | copy-start | bytes 1572868
  46.4 1.0 copy-start.1
  50.9 3.2 %collective-permute-start.2 = (f32[8,2176]{1,0:T(8,128)S(1)}, f32[8,2176]{1,0:T(8,128)S(1)}, u32[]{:S(2)}, u32[]{:S(2)}) collective-permute-start(f32[8,2176]{1,0:T(8,128)S(1)} %pad_maximum_fusion.2), channel_id=1, source_target_pairs={{0,16},{16,0},{32,48},{48,32},{64,80},{80,64},{96,112},{112,96},{1... | collective-permute-start | bytes 208904 | tf_op jit(solution)/shard_map/ppermute | solution.py:47
  54.4 6.3 %collective-permute-start.3 = (f32[8,2176]{1,0:T(8,128)S(1)}, f32[8,2176]{1,0:T(8,128)S(1)}, u32[]{:S(2)}, u32[]{:S(2)}) collective-permute-start(f32[8,2176]{1,0:T(8,128)S(1)} %add_select_fusion.3), channel_id=1, source_target_pairs={{0,32},{16,48},{32,0},{48,16},{64,96},{80,112},{96,64},{112,80},{1... | collective-permute-start | bytes 208904 | tf_op jit(solution)/shard_map/ppermute | solution.py:47
  60.9 7.2 %collective-permute-start.4 = (f32[8,2176]{1,0:T(8,128)S(1)}, f32[8,2176]{1,0:T(8,128)S(1)}, u32[]{:S(2)}, u32[]{:S(2)}) collective-permute-start(f32[8,2176]{1,0:T(8,128)S(1)} %add_select_fusion.2), channel_id=1, source_target_pairs={{0,64},{16,80},{32,96},{48,112},{64,0},{80,16},{96,32},{112,48},{1... | collective-permute-start | bytes 208904 | tf_op jit(solution)/shard_map/ppermute | solution.py:47
  68.3 4.8 %collective-permute-start.5 = (f32[8,2176]{1,0:T(8,128)S(1)}, f32[8,2176]{1,0:T(8,128)S(1)}, u32[]{:S(2)}, u32[]{:S(2)}) collective-permute-start(f32[8,2176]{1,0:T(8,128)S(1)} %add_select_fusion.1), channel_id=1, source_target_pairs={{0,128},{16,144},{32,160},{48,176},{64,192},{80,208},{96,224},{112... | collective-permute-start | bytes 208904 | tf_op jit(solution)/shard_map/ppermute | solution.py:47
  76.5 3.1 %collective-permute-start.6 = (f32[8,2048]{1,0:T(8,128)S(1)}, f32[8,2048]{1,0:T(8,128)S(1)}, u32[]{:S(2)}, u32[]{:S(2)}) collective-permute-start(f32[8,2048]{1,0:T(8,128)S(1)} %fusion), channel_id=1, source_target_pairs={{0,16},{16,0},{32,48},{48,32},{64,80},{80,64},{96,112},{112,96},{1... | collective-permute-start | bytes 196616 | tf_op jit(solution)/shard_map/ppermute | solution.py:30
  79.6 4.6 %collective-permute-start.7 = (f32[8,2048]{1,0:T(8,128)S(1)}, f32[8,2048]{1,0:T(8,128)S(1)}, u32[]{:S(2)}, u32[]{:S(2)}) collective-permute-start(f32[8,2048]{1,0:T(8,128)S(1)} %add.56), channel_id=1, source_target_pairs={{0,32},{16,48},{32,0},{48,16},{64,96},{80,112},{96,64},{112,80},{1... | collective-permute-start | bytes 196616 | tf_op jit(solution)/shard_map/ppermute | solution.py:30
  84.2 7.3 %collective-permute-start.8 = (f32[8,2048]{1,0:T(8,128)S(1)}, f32[8,2048]{1,0:T(8,128)S(1)}, u32[]{:S(2)}, u32[]{:S(2)}) collective-permute-start(f32[8,2048]{1,0:T(8,128)S(1)} %add.57), channel_id=1, source_target_pairs={{0,64},{16,80},{32,96},{48,112},{64,0},{80,16},{96,32},{112,48},{1... | collective-permute-start | bytes 196616 | tf_op jit(solution)/shard_map/ppermute | solution.py:30
  91.5 5.0 %collective-permute-start.9 = (f32[8,2048]{1,0:T(8,128)S(1)}, f32[8,2048]{1,0:T(8,128)S(1)}, u32[]{:S(2)}, u32[]{:S(2)}) collective-permute-start(f32[8,2048]{1,0:T(8,128)S(1)} %add.58), channel_id=1, source_target_pairs={{0,128},{16,144},{32,160},{48,176},{64,192},{80,208},{96,224},{112... | collective-permute-start | bytes 196616 | tf_op jit(solution)/shard_map/ppermute | solution.py:30

commit v12 on v11

--- a/solution.py
+++ b/solution.py
@@ -24,11 +24,11 @@
 
 def butterfly_sum(value, axis):
     count = lax.axis_size(axis)
-    step = 1
-    while step < count:
+    step = count // 2
+    while step >= 1:
         pairs = [(i, i ^ step) for i in range(count)]
         value = value + lax.ppermute(value, axis, pairs)
-        step *= 2
+        step //= 2
     return value
 
 
@@ -41,11 +41,11 @@
 
 def butterfly_softmax_sum(value, axis):
     count = lax.axis_size(axis)
-    step = 1
-    while step < count:
+    step = count // 2
+    while step >= 1:
         pairs = [(i, i ^ step) for i in range(count)]
         value = merge(value, lax.ppermute(value, axis, pairs))
-        step *= 2
+        step //= 2
     return value
 
 

time: 130 us -> 130 us (level)
  starting transfers between devices: 23.7 us -> 27.8 us
  waiting for transfers between devices: 19.7 us -> 17.4 us
    ppermute x4, starting transfers between devices: 9.62 us -> 12.7 us  [butterfly_sum(): value = value + lax.ppermute(value, axis, pairs)]
    ppermute x4, waiting for transfers between devices: 8.08 us -> 6.61 us  [butterfly_sum(): value = value + lax.ppermute(value, axis, pairs)]
where the time goes in v12:
time: 130 us
  blocking collectives  54.6 us (42%)
  starting transfers between devices  27.8 us (21%)
  waiting for transfers between devices  17.4 us (13%)
  other arithmetic  11.3 us (9%)
  matrix products  9.69 us (7%)
  local copies, waits for them, and re-layouts  5.25 us (4%)
  Pallas kernels  3.84 us (3%)
    all_gather x1, blocking collectives, per_device(): slot_all = lax.all_gather(slot_out, 'exp', axis=0, tiled=True)  28 us
    all_to_all x1, blocking collectives, per_device(): lax.all_to_all(packed, 'exp', 0, 0, tiled=True)  26.6 us
    ppermute x4, starting transfers between devices, butterfly_sum(): value = value + lax.ppermute(value, axis, pairs)  12.7 us
    ppermute x4, starting transfers between devices, butterfly_softmax_sum(): value = merge(value, lax.ppermute(value, axis, pairs))  11.7 us
    ppermute x4, waiting for transfers between devices, butterfly_softmax_sum(): value = merge(value, lax.ppermute(value, axis, pairs))  9.83 us
    ppermute x4, waiting for transfers between devices, butterfly_sum(): value = value + lax.ppermute(value, axis, pairs)  6.61 us
    another operation x6, other arithmetic  3.89 us
    pallas_call x1, Pallas kernels, mix(): pl.pallas_call(mix_kernel, grid=(channels // block,), in_specs=[pl.BlockS...  3.84 us
  transfers between devices with their start and end apart: 10, of which 8 were waited for; matrix products, arithmetic and copies ran while one was open for 3% of the time, Pallas kernels for 0%

profile of v12, /device:TPU:1, one launch (start us, length us, event | category | flops | bytes accessed | tf_op | source)
XLA Modules:
  0.0 130.1 jit_solution(6209549131379787009)
XLA Ops:
  0.0 1.3 copy.38
  1.3 0.8 copy-done.3
  2.1 2.7 %collective-permute-start = (bf16[4,1,256]{2,1,0:T(2,128)(2,1)S(1)}, bf16[4,1,256]{2,1,0:T(2,128)(2,1)S(1)}, u32[]{:S(2)}, u32[]{:S(2)}) collective-permute-start(bf16[4,1,256]{2,1,0:T(2,128)(2,1)S(1)} %get-tuple-element.69), channel_id=1, source_target_pairs={{0,1},{1,2},{2,3},{3,4},{4,5},{5,6},{6,7},{7,8},{8,9},{9,10},{10,1... | collective-permute-start | bytes 6152 | tf_op jit(solution)/shard_map/ppermute | solution.py:19
  4.7 0.7 collective-permute-start.1
  5.4 0.7 compare_reduce_fusion.1
  6.2 0.6 compare_reduce_fusion
  6.8 1.0 collective-permute-done.1
  7.8 1.7 %fusion.4 = bf16[4,256,768]{2,1,0:T(8,128)(2,1)S(1)} fusion(bf16[4,1,256]{2,1,0:T(2,128)(2,1)S(1)} %broadcast_select_fusion, bf16[4,256,256]{2,1,0:T(8,128)(2,1)} %bitcast.56, bf16[4,1,256]{2,1,0:T(2,128)(2,1)S(1)} %broadcast_select_fusion.1), kind=kLoop, calls=%fused_computation.6 | loop fusion | flops 7864320 | bytes 2101248 | tf_op jit(solution)/shard_map/concatenate | solution.py:82
  9.5 3.6 %convolution_convert_fusion = bf16[1024,2048]{1,0:T(8,128)(2,1)S(1)} fusion(bf16[1024,768]{1,0:T(8,128)(2,1)S(1)} %bitcast.57, bf16[768,2048]{1,0:T(8,128)(2,1)S(1)} %bitcast.54), kind=kOutput, calls=%fused_computation | convolution fusion | flops 3223322624 | bytes 8912896 | tf_op jit(solution)/shard_map/dot_general | solution.py:85
  13.2 1.3 %fusion.55 = (f32[128]{0:T(128)S(1)}, f32[1024]{0:T(1024)S(1)}, f32[1024,128]{1,0:T(8,128)S(1)}) fusion(bf16[1024,2048]{1,0:T(8,128)(2,1)S(1)} %convolution_convert_fusion, bf16[2048,128]{1,0:T(8,128)(2,1)S(1)} %copy-done.4), kind=kOutput, calls=%fused_computation.84 | convolution fusion | flops 537131904 | bytes 5247488 | tf_op jit(solution)/shard_map/dot_general | solution.py:86
  14.5 1.7 %fusion.10 = f32[128,2048]{1,0:T(8,128)} fusion(bf16[1024,2048]{1,0:T(8,128)(2,1)S(1)} %convolution_convert_fusion, f32[1024,128]{1,0:T(8,128)S(1)} %get-tuple-element.74, f32[128]{0:T(128)S(1)} %get-tuple-element.55), kind=kOutput, calls=%fused_computation.19 | convolution fusion | flops 537133056 | bytes 5767680 | tf_op jit(solution)/shard_map/dot_general | solution.py:92
  16.2 0.7 fusion.44
  16.9 0.4 fusion.8
  17.3 0.6 fusion.45
  18.1 0.4 scatter.15
  18.5 1.3 %maximum_bitcast_fusion = f32[16,8,2176]{2,1,0:T(8,128)S(1)} fusion(f32[128,128]{1,0:T(8,128)S(1)} %scatter.15, f32[128,2048]{1,0:T(8,128)} %fusion.10), kind=kLoop, calls=%fused_computation.9 | loop fusion | flops 278528 | bytes 2228224 | tf_op jit(solution)/shard_map/all_to_all | solution.py:100
  19.8 26.6 %all_to_all.9 = f32[16,8,2176]{2,1,0:T(8,128)S(1)} all-to-all(f32[16,8,2176]{2,1,0:T(8,128)S(1)} %maximum_bitcast_fusion), channel_id=1, replica_groups=mesh['pos'=16,'exp'=16] {'exp'}, dimensions={0} | all-to-all | bytes 2228224 | tf_op jit(solution)/shard_map/all_to_all | solution.py:100
  46.4 1.0 copy-done.1
  47.4 0.1 fusion.56
  47.5 0.7 fusion.43
  48.4 0.1 copy.33
  48.6 0.2 fusion.42
  48.8 0.6 fusion.46
  49.5 1.4 %fusion.6 = f32[8,2048]{1,0:T(8,128)S(1)} fusion(f32[16,8,2176]{2,1,0:T(8,128)} %copy-done.1, f32[16,8]{1,0:T(8,128)S(1)} %copy.30), kind=kLoop, calls=%fused_computation.11 | loop fusion | flops 507904 | bytes 1114624 | tf_op jit(solution)/shard_map/reduce_sum | solution.py:104
  50.9 1.3 collective-permute-start.2
  52.2 3.5 %collective-permute-done.2 = f32[8,2176]{1,0:T(8,128)S(1)} collective-permute-done((f32[8,2176]{1,0:T(8,128)S(1)}, f32[8,2176]{1,0:T(8,128)S(1)}, u32[]{:S(2)}, u32[]{:S(2)}) %collective-permute-start.2) | collective-permute-done | bytes 69664 | tf_op jit(solution)/shard_map/ppermute | solution.py:47
  55.9 4.6 %collective-permute-start.3 = (f32[8,2176]{1,0:T(8,128)S(1)}, f32[8,2176]{1,0:T(8,128)S(1)}, u32[]{:S(2)}, u32[]{:S(2)}) collective-permute-start(f32[8,2176]{1,0:T(8,128)S(1)} %add_select_fusion.3), channel_id=1, source_target_pairs={{0,64},{16,80},{32,96},{48,112},{64,0},{80,16},{96,32},{112,48},{1... | collective-permute-start | bytes 208904 | tf_op jit(solution)/shard_map/ppermute | solution.py:47
  60.4 2.7 %collective-permute-done.3 = f32[8,2176]{1,0:T(8,128)S(1)} collective-permute-done((f32[8,2176]{1,0:T(8,128)S(1)}, f32[8,2176]{1,0:T(8,128)S(1)}, u32[]{:S(2)}, u32[]{:S(2)}) %collective-permute-start.3) | collective-permute-done | bytes 69664 | tf_op jit(solution)/shard_map/ppermute | solution.py:47
  63.1 0.1 fusion.52
  63.4 2.2 %collective-permute-start.4 = (f32[8,2176]{1,0:T(8,128)S(1)}, f32[8,2176]{1,0:T(8,128)S(1)}, u32[]{:S(2)}, u32[]{:S(2)}) collective-permute-start(f32[8,2176]{1,0:T(8,128)S(1)} %add_select_fusion.2), channel_id=1, source_target_pairs={{0,32},{16,48},{32,0},{48,16},{64,96},{80,112},{96,64},{112,80},{1... | collective-permute-start | bytes 208904 | tf_op jit(solution)/shard_map/ppermute | solution.py:47
  65.5 2.0 %collective-permute-done.4 = f32[8,2176]{1,0:T(8,128)S(1)} collective-permute-done((f32[8,2176]{1,0:T(8,128)S(1)}, f32[8,2176]{1,0:T(8,128)S(1)}, u32[]{:S(2)}, u32[]{:S(2)}) %collective-permute-start.4) | collective-permute-done | bytes 69664 | tf_op jit(solution)/shard_map/ppermute | solution.py:47
  67.5 0.1 fusion.53
  67.7 3.6 %collective-permute-start.5 = (f32[8,2176]{1,0:T(8,128)S(1)}, f32[8,2176]{1,0:T(8,128)S(1)}, u32[]{:S(2)}, u32[]{:S(2)}) collective-permute-start(f32[8,2176]{1,0:T(8,128)S(1)} %add_select_fusion.1), channel_id=1, source_target_pairs={{0,16},{16,0},{32,48},{48,32},{64,80},{80,64},{96,112},{112,96},{1... | collective-permute-start | bytes 208904 | tf_op jit(solution)/shard_map/ppermute | solution.py:47
  71.4 1.7 %collective-permute-done.5 = f32[8,2176]{1,0:T(8,128)S(1)} collective-permute-done((f32[8,2176]{1,0:T(8,128)S(1)}, f32[8,2176]{1,0:T(8,128)S(1)}, u32[]{:S(2)}, u32[]{:S(2)}) %collective-permute-start.5) | collective-permute-done | bytes 69664 | tf_op jit(solution)/shard_map/ppermute | solution.py:47
  73.1 0.1 fusion.54
  73.3 0.2 slice_reduce_fusion
  73.5 3.0 %fusion = f32[8,2048]{1,0:T(8,128)S(1)} fusion(bf16[1,512,2048]{2,1,0:T(8,128)(2,1)} %param.17, bf16[1,2048,512]{2,1,0:T(8,128)(2,1)} %param.16, f32[8,2176]{1,0:T(8,128)S(1)} %add_select_fusion, f32[8]{0:T(128)S(1)} %slice_reduce_fusion), kind=kOutput, calls=%fused_computation.1 | convolution fusion | flops 33624064 | bytes 4325888 | tf_op jit(solution)/shard_map/dot_general | solution.py:114
  76.5 3.0 %collective-permute-start.6 = (f32[8,2048]{1,0:T(8,128)S(1)}, f32[8,2048]{1,0:T(8,128)S(1)}, u32[]{:S(2)}, u32[]{:S(2)}) collective-permute-start(f32[8,2048]{1,0:T(8,128)S(1)} %fusion), channel_id=1, source_target_pairs={{0,128},{16,144},{32,160},{48,176},{64,192},{80,208},{96,224},{112... | collective-permute-start | bytes 196616 | tf_op jit(solution)/shard_map/ppermute | solution.py:30
  79.5 1.7 %collective-permute-done.6 = f32[8,2048]{1,0:T(8,128)S(1)} collective-permute-done((f32[8,2048]{1,0:T(8,128)S(1)}, f32[8,2048]{1,0:T(8,128)S(1)}, u32[]{:S(2)}, u32[]{:S(2)}) %collective-permute-start.6) | collective-permute-done | bytes 65568 | tf_op jit(solution)/shard_map/ppermute | solution.py:30
  81.2 4.0 %collective-permute-start.7 = (f32[8,2048]{1,0:T(8,128)S(1)}, f32[8,2048]{1,0:T(8,128)S(1)}, u32[]{:S(2)}, u32[]{:S(2)}) collective-permute-start(f32[8,2048]{1,0:T(8,128)S(1)} %add.56), channel_id=1, source_target_pairs={{0,64},{16,80},{32,96},{48,112},{64,0},{80,16},{96,32},{112,48},{1... | collective-permute-start | bytes 196616 | tf_op jit(solution)/shard_map/ppermute | solution.py:30
  85.2 3.1 %collective-permute-done.7 = f32[8,2048]{1,0:T(8,128)S(1)} collective-permute-done((f32[8,2048]{1,0:T(8,128)S(1)}, f32[8,2048]{1,0:T(8,128)S(1)}, u32[]{:S(2)}, u32[]{:S(2)}) %collective-permute-start.7) | collective-permute-done | bytes 65568 | tf_op jit(solution)/shard_map/ppermute | solution.py:30
  88.3 3.1 %collective-permute-start.8 = (f32[8,2048]{1,0:T(8,128)S(1)}, f32[8,2048]{1,0:T(8,128)S(1)}, u32[]{:S(2)}, u32[]{:S(2)}) collective-permute-start(f32[8,2048]{1,0:T(8,128)S(1)} %add.57), channel_id=1, source_target_pairs={{0,32},{16,48},{32,0},{48,16},{64,96},{80,112},{96,64},{112,80},{1... | collective-permute-start | bytes 196616 | tf_op jit(solution)/shard_map/ppermute | solution.py:30
  91.4 1.9 %collective-permute-done.8 = f32[8,2048]{1,0:T(8,128)S(1)} collective-permute-done((f32[8,2048]{1,0:T(8,128)S(1)}, f32[8,2048]{1,0:T(8,128)S(1)}, u32[]{:S(2)}, u32[]{:S(2)}) %collective-permute-start.8) | collective-permute-done | bytes 65568 | tf_op jit(solution)/shard_map/ppermute | solution.py:30
  93.3 2.6 %collective-permute-start.9 = (f32[8,2048]{1,0:T(8,128)S(1)}, f32[8,2048]{1,0:T(8,128)S(1)}, u32[]{:S(2)}, u32[]{:S(2)}) collective-permute-start(f32[8,2048]{1,0:T(8,128)S(1)} %add.58), channel_id=1, source_target_pairs={{0,16},{16,0},{32,48},{48,32},{64,80},{80,64},{96,112},{112,96},{1... | collective-permute-start | bytes 196616 | tf_op jit(solution)/shard_map/ppermute | solution.py:30
  95.9 1.4 %divide_convert_fusion = bf16[1024,128]{1,0:T(8,128)(2,1)S(1)} fusion(f32[1024,128]{1,0:T(8,128)} %copy-done.2, f32[1024]{0:T(1024)S(1)} %get-tuple-element.54, f32[1024]{0:T(1024)S(1)} %get-tuple-element.56), kind=kLoop, calls=%fused_computation.14 | loop fusion | flops 393216 | bytes 794624 | tf_op jit(solution)/shard_map/convert_element_type | solution.py:118
  97.3 0.9 copy.25
  98.2 28.0 %all_gather.3.slots_ref = bf16[128,2048]{1,0:T(8,128)(2,1)} all-gather(bf16[8,2048]{1,0:T(8,128)(2,1)S(1)} %add_convert_fusion), channel_id=1, replica_groups=mesh['pos'=16,'exp'=16] {'exp'}, dimensions={0}, use_global_device_ids=true | all-gather | bytes 557056 | tf_op jit(solution)/shard_map/all_gather | solution.py:119
  126.3 3.8 %shard_map.55 = bf16[256,4,2048]{2,1,0:T(4,128)(2,1)} custom-call(bf16[1024,128]{1,0:T(8,128)(2,1)} %bitcast.58, bf16[128,2048]{1,0:T(8,128)(2,1)} %all_gather.3.slots_ref), custom_call_target="tpu_custom_call" | custom-call | flops 536870912 | bytes 4980736 | tf_op jit(solution)/shard_map/pallas_call | solution.py:61
  (35 shorter events, 1.1 us)
Async XLA Ops:
  0.0 9.5 %copy-start = (bf16[3,256,2048]{2,1,0:T(8,128)(2,1)S(1)}, bf16[3,256,2048]{2,1,0:T(8,128)(2,1)}, u32[]{:S(2)}) copy-start(bf16[3,256,2048]{2,1,0:T(8,128)(2,1)} %param.14) | copy-start | bytes 9437188
  1.3 0.8 copy-start.3
  2.1 4.7 %collective-permute-start = (bf16[4,1,256]{2,1,0:T(2,128)(2,1)S(1)}, bf16[4,1,256]{2,1,0:T(2,128)(2,1)S(1)}, u32[]{:S(2)}, u32[]{:S(2)}) collective-permute-start(bf16[4,1,256]{2,1,0:T(2,128)(2,1)S(1)} %get-tuple-element.69), channel_id=1, source_target_pairs={{0,1},{1,2},{2,3},{3,4},{4,5},{5,6},{6,7},{7,8},{8,9},{9,10},{10,1... | collective-permute-start | bytes 6152 | tf_op jit(solution)/shard_map/ppermute | solution.py:19
  4.7 3.0 %collective-permute-start.1 = (bf16[4,1,256]{2,1,0:T(2,128)(2,1)S(1)}, bf16[4,1,256]{2,1,0:T(2,128)(2,1)S(1)}, u32[]{:S(2)}, u32[]{:S(2)}) collective-permute-start(bf16[4,1,256]{2,1,0:T(2,128)(2,1)S(1)} %get-tuple-element.70), channel_id=1, source_target_pairs={{1,0},{2,1},{3,2},{4,3},{5,4},{6,5},{7,6},{8,7},{9,8},{10,9},{11,1... | collective-permute-start | bytes 6152 | tf_op jit(solution)/shard_map/ppermute | solution.py:20
  9.5 3.7 %copy-start.4 = (bf16[2048,128]{1,0:T(8,128)(2,1)S(1)}, bf16[2048,128]{1,0:T(8,128)(2,1)}, u32[]{:S(2)}) copy-start(bf16[2048,128]{1,0:T(8,128)(2,1)} %param.15) | copy-start | bytes 1572868
  14.5 2.4 %copy-start.2 = (f32[1024,128]{1,0:T(8,128)}, f32[1024,128]{1,0:T(8,128)S(1)}, u32[]{:S(2)}) copy-start(f32[1024,128]{1,0:T(8,128)S(1)} %get-tuple-element.74) | copy-start | bytes 1572868
  46.4 1.0 copy-start.1
  50.9 4.8 %collective-permute-start.2 = (f32[8,2176]{1,0:T(8,128)S(1)}, f32[8,2176]{1,0:T(8,128)S(1)}, u32[]{:S(2)}, u32[]{:S(2)}) collective-permute-start(f32[8,2176]{1,0:T(8,128)S(1)} %pad_maximum_fusion.2), channel_id=1, source_target_pairs={{0,128},{16,144},{32,160},{48,176},{64,192},{80,208},{96,224},{112... | collective-permute-start | bytes 208904 | tf_op jit(solution)/shard_map/ppermute | solution.py:47
  55.9 7.3 %collective-permute-start.3 = (f32[8,2176]{1,0:T(8,128)S(1)}, f32[8,2176]{1,0:T(8,128)S(1)}, u32[]{:S(2)}, u32[]{:S(2)}) collective-permute-start(f32[8,2176]{1,0:T(8,128)S(1)} %add_select_fusion.3), channel_id=1, source_target_pairs={{0,64},{16,80},{32,96},{48,112},{64,0},{80,16},{96,32},{112,48},{1... | collective-permute-start | bytes 208904 | tf_op jit(solution)/shard_map/ppermute | solution.py:47
  63.4 4.1 %collective-permute-start.4 = (f32[8,2176]{1,0:T(8,128)S(1)}, f32[8,2176]{1,0:T(8,128)S(1)}, u32[]{:S(2)}, u32[]{:S(2)}) collective-permute-start(f32[8,2176]{1,0:T(8,128)S(1)} %add_select_fusion.2), channel_id=1, source_target_pairs={{0,32},{16,48},{32,0},{48,16},{64,96},{80,112},{96,64},{112,80},{1... | collective-permute-start | bytes 208904 | tf_op jit(solution)/shard_map/ppermute | solution.py:47
  67.7 5.3 %collective-permute-start.5 = (f32[8,2176]{1,0:T(8,128)S(1)}, f32[8,2176]{1,0:T(8,128)S(1)}, u32[]{:S(2)}, u32[]{:S(2)}) collective-permute-start(f32[8,2176]{1,0:T(8,128)S(1)} %add_select_fusion.1), channel_id=1, source_target_pairs={{0,16},{16,0},{32,48},{48,32},{64,80},{80,64},{96,112},{112,96},{1... | collective-permute-start | bytes 208904 | tf_op jit(solution)/shard_map/ppermute | solution.py:47
  76.5 4.6 %collective-permute-start.6 = (f32[8,2048]{1,0:T(8,128)S(1)}, f32[8,2048]{1,0:T(8,128)S(1)}, u32[]{:S(2)}, u32[]{:S(2)}) collective-permute-start(f32[8,2048]{1,0:T(8,128)S(1)} %fusion), channel_id=1, source_target_pairs={{0,128},{16,144},{32,160},{48,176},{64,192},{80,208},{96,224},{112... | collective-permute-start | bytes 196616 | tf_op jit(solution)/shard_map/ppermute | solution.py:30
  81.2 7.1 %collective-permute-start.7 = (f32[8,2048]{1,0:T(8,128)S(1)}, f32[8,2048]{1,0:T(8,128)S(1)}, u32[]{:S(2)}, u32[]{:S(2)}) collective-permute-start(f32[8,2048]{1,0:T(8,128)S(1)} %add.56), channel_id=1, source_target_pairs={{0,64},{16,80},{32,96},{48,112},{64,0},{80,16},{96,32},{112,48},{1... | collective-permute-start | bytes 196616 | tf_op jit(solution)/shard_map/ppermute | solution.py:30
  88.3 5.0 %collective-permute-start.8 = (f32[8,2048]{1,0:T(8,128)S(1)}, f32[8,2048]{1,0:T(8,128)S(1)}, u32[]{:S(2)}, u32[]{:S(2)}) collective-permute-start(f32[8,2048]{1,0:T(8,128)S(1)} %add.57), channel_id=1, source_target_pairs={{0,32},{16,48},{32,0},{48,16},{64,96},{80,112},{96,64},{112,80},{1... | collective-permute-start | bytes 196616 | tf_op jit(solution)/shard_map/ppermute | solution.py:30
  93.3 4.9 %collective-permute-start.9 = (f32[8,2048]{1,0:T(8,128)S(1)}, f32[8,2048]{1,0:T(8,128)S(1)}, u32[]{:S(2)}, u32[]{:S(2)}) collective-permute-start(f32[8,2048]{1,0:T(8,128)S(1)} %add.58), channel_id=1, source_target_pairs={{0,16},{16,0},{32,48},{48,32},{64,80},{80,64},{96,112},{112,96},{1... | collective-permute-start | bytes 196616 | tf_op jit(solution)/shard_map/ppermute | solution.py:30

commit v13 on v11

--- a/solution.py
+++ b/solution.py
@@ -75,6 +75,13 @@
     )(combine, slot_all)
 
 
+def pack(sums, peak, total):
+    rows = sums.shape[0]
+    column = lax.broadcasted_iota(jnp.int32, (rows, 128), 1)
+    extra = jnp.where(column == 0, peak[:, None], jnp.where(column == 1, total[:, None], 0.0))
+    return jnp.concatenate([sums, extra], axis=1)
+
+
 def per_device(patches, conv_weight, phi, w_in, w_out):
     channels, periods, samples = patches.shape
     every = ("pos", "exp")
@@ -93,9 +100,7 @@
         raw_weights.astype(jnp.bfloat16), flat, (((0,), (0,)), ((), ())),
         preferred_element_type=jnp.float32,
     )
-    extra = jnp.zeros((slots, 128), jnp.float32)
-    extra = extra.at[:, 0].set(local_peak).at[:, 1].set(local_total)
-    packed = jnp.concatenate([every_slot, extra], axis=1)
+    packed = pack(every_slot, local_peak, local_total)
     groups = lax.axis_size("exp")
     mine = lax.all_to_all(packed, "exp", 0, 0, tiled=True).reshape(groups, SLOTS_PER, -1)
     peaks = mine[:, :, D]
@@ -103,9 +108,7 @@
     scale = jnp.exp(peaks - peak)
     sums = jnp.sum(mine[:, :, :D] * scale[:, :, None], axis=0)
     total = jnp.sum(mine[:, :, D + 1] * scale, axis=0)
-    owned = jnp.concatenate(
-        [sums, jnp.zeros((SLOTS_PER, 128), jnp.float32).at[:, 0].set(peak).at[:, 1].set(total)], axis=1
-    )
+    owned = pack(sums, peak, total)
     owned = butterfly_softmax_sum(owned, "pos")
     slot_in = (owned[:, :D] / owned[:, D + 1 : D + 2]).astype(jnp.bfloat16)
     hidden = jax.nn.gelu(

time: 130 us -> 124 us (0.954)
  other arithmetic: 11.3 us -> 6.48 us
  waiting for transfers between devices: 19.7 us -> 21 us
    another operation x6 -> x0, other arithmetic: 3.89 us -> none
    unnamed x14 -> x13, local copies, waits for them, and re-layouts: 3.39 us -> 3.34 us
  transfers between devices with their start and end apart: 10 -> 10, of which waited for: 8 -> 9; matrix products, arithmetic and copies ran while one was open for 3% -> 2% of each run, Pallas kernels for 0% -> 0%
where the time goes in v13:
time: 124 us
  blocking collectives  55.6 us (45%)
  starting transfers between devices  23.9 us (19%)
  waiting for transfers between devices  21 us (17%)
  matrix products  8.71 us (7%)
  other arithmetic  6.48 us (5%)
  local copies, waits for them, and re-layouts  4.51 us (4%)
  Pallas kernels  3.84 us (3%)
    all_gather x1, blocking collectives, per_device(): slot_all = lax.all_gather(slot_out, 'exp', axis=0, tiled=True)  29 us
    all_to_all x1, blocking collectives, per_device(): lax.all_to_all(packed, 'exp', 0, 0, tiled=True)  26.5 us
    ppermute x4, starting transfers between devices, butterfly_softmax_sum(): value = merge(value, lax.ppermute(value, axis, pairs))  10.8 us
    ppermute x4, waiting for transfers between devices, butterfly_softmax_sum(): value = merge(value, lax.ppermute(value, axis, pairs))  10.6 us
    ppermute x4, starting transfers between devices, butterfly_sum(): value = value + lax.ppermute(value, axis, pairs)  9.65 us
    ppermute x4, waiting for transfers between devices, butterfly_sum(): value = value + lax.ppermute(value, axis, pairs)  8.06 us
    pallas_call x1, Pallas kernels, mix(): pl.pallas_call(mix_kernel, grid=(channels // block,), in_specs=[pl.BlockS...  3.84 us
    dot_general x1, matrix products, per_device(): jnp.dot(window, taps, preferred_element_type=jnp.float32)  3.63 us
  transfers between devices with their start and end apart: 10, of which 9 were waited for; matrix products, arithmetic and copies ran while one was open for 2% of the time, Pallas kernels for 0%

profile of v13, /device:TPU:1, one launch (start us, length us, event | category | flops | bytes accessed | tf_op | source)
XLA Modules:
  0.0 124.2 jit_solution(16916755119168497314)
XLA Ops:
  0.0 1.3 %copy.25 = bf16[256,4,256]{2,0,1:T(8,128)(2,1)S(1)} copy(bf16[256,4,256]{2,1,0:T(4,128)(2,1)} %param.5) | data formatting | bytes 1048576 | tf_op args[0]
  1.3 0.8 copy-done.3
  2.1 2.7 %collective-permute-start = (bf16[4,1,256]{2,1,0:T(2,128)(2,1)S(1)}, bf16[4,1,256]{2,1,0:T(2,128)(2,1)S(1)}, u32[]{:S(2)}, u32[]{:S(2)}) collective-permute-start(bf16[4,1,256]{2,1,0:T(2,128)(2,1)S(1)} %get-tuple-element.24), channel_id=1, source_target_pairs={{0,1},{1,2},{2,3},{3,4},{4,5},{5,6},{6,7},{7,8},{8,9},{9,10},{10,1... | collective-permute-start | bytes 6152 | tf_op jit(solution)/shard_map/ppermute | solution.py:19
  4.7 0.7 collective-permute-start.1
  5.5 0.6 collective-permute-done
  6.0 1.7 %collective-permute-done.1 = bf16[4,1,256]{2,1,0:T(2,128)(2,1)S(1)} collective-permute-done((bf16[4,1,256]{2,1,0:T(2,128)(2,1)S(1)}, bf16[4,1,256]{2,1,0:T(2,128)(2,1)S(1)}, u32[]{:S(2)}, u32[]{:S(2)}) %collective-permute-start.1) | collective-permute-done | bytes 2080 | tf_op jit(solution)/shard_map/ppermute | solution.py:20
  7.8 1.7 %fusion.4 = bf16[4,256,768]{2,1,0:T(8,128)(2,1)S(1)} fusion(bf16[4,1,256]{2,1,0:T(2,128)(2,1)S(1)} %broadcast_select_fusion, bf16[4,256,256]{2,1,0:T(8,128)(2,1)} %bitcast.42, bf16[4,1,256]{2,1,0:T(2,128)(2,1)S(1)} %broadcast_select_fusion.1), kind=kLoop, calls=%fused_computation.6 | loop fusion | flops 7864320 | bytes 2101248 | tf_op jit(solution)/shard_map/concatenate | solution.py:89
  9.5 3.6 %convolution_convert_fusion = bf16[1024,2048]{1,0:T(8,128)(2,1)S(1)} fusion(bf16[1024,768]{1,0:T(8,128)(2,1)S(1)} %bitcast.43, bf16[768,2048]{1,0:T(8,128)(2,1)S(1)} %bitcast.40), kind=kOutput, calls=%fused_computation | convolution fusion | flops 3223322624 | bytes 8912896 | tf_op jit(solution)/shard_map/dot_general | solution.py:92
  13.2 1.3 %fusion.51 = (f32[128]{0:T(128)S(1)}, f32[1024]{0:T(1024)S(1)}, f32[1024,128]{1,0:T(8,128)S(1)}) fusion(bf16[1024,2048]{1,0:T(8,128)(2,1)S(1)} %convolution_convert_fusion, bf16[2048,128]{1,0:T(8,128)(2,1)S(1)} %copy-done.4), kind=kOutput, calls=%fused_computation.77 | convolution fusion | flops 537131904 | bytes 5247488 | tf_op jit(solution)/shard_map/dot_general | solution.py:93
  14.5 0.8 fusion.10
  15.3 0.4 fusion.8
  15.7 0.1 select_select_fusion
  15.8 26.5 %all_to_all.9 = f32[16,8,2176]{2,1,0:T(8,128)S(1)} all-to-all(f32[16,8,2176]{2,1,0:T(8,128)S(1)} %maximum_bitcast_fusion), channel_id=1, replica_groups=mesh['pos'=16,'exp'=16] {'exp'}, dimensions={0} | all-to-all | bytes 2228224 | tf_op jit(solution)/shard_map/all_to_all | solution.py:105
  42.4 1.0 copy-done.1
  43.4 0.1 slice_reduce_fusion.1
  43.5 0.1 copy.21
  43.8 0.1 copy.22
  43.9 0.2 fusion.42
  44.2 1.4 %fusion.6 = f32[8,2048]{1,0:T(8,128)S(1)} fusion(f32[16,8,2176]{2,1,0:T(8,128)} %copy-done.1, f32[16,8]{1,0:T(8,128)S(1)} %copy.20), kind=kLoop, calls=%fused_computation.11 | loop fusion | flops 507904 | bytes 1114624 | tf_op jit(solution)/shard_map/reduce_sum | solution.py:109
  45.6 0.2 collective-permute-start.2
  45.8 3.0 %collective-permute-done.2 = f32[8,2176]{1,0:T(8,128)S(1)} collective-permute-done((f32[8,2176]{1,0:T(8,128)S(1)}, f32[8,2176]{1,0:T(8,128)S(1)}, u32[]{:S(2)}, u32[]{:S(2)}) %collective-permute-start.2) | collective-permute-done | bytes 69664 | tf_op jit(solution)/shard_map/ppermute | solution.py:47
  48.8 0.1 fusion.47
  49.0 0.1 add_select_fusion.3
  49.1 4.6 %collective-permute-start.3 = (f32[8,2176]{1,0:T(8,128)S(1)}, f32[8,2176]{1,0:T(8,128)S(1)}, u32[]{:S(2)}, u32[]{:S(2)}) collective-permute-start(f32[8,2176]{1,0:T(8,128)S(1)} %add_select_fusion.3), channel_id=1, source_target_pairs={{0,32},{16,48},{32,0},{48,16},{64,96},{80,112},{96,64},{112,80},{1... | collective-permute-start | bytes 208904 | tf_op jit(solution)/shard_map/ppermute | solution.py:47
  53.7 1.7 %collective-permute-done.3 = f32[8,2176]{1,0:T(8,128)S(1)} collective-permute-done((f32[8,2176]{1,0:T(8,128)S(1)}, f32[8,2176]{1,0:T(8,128)S(1)}, u32[]{:S(2)}, u32[]{:S(2)}) %collective-permute-start.3) | collective-permute-done | bytes 69664 | tf_op jit(solution)/shard_map/ppermute | solution.py:47
  55.4 0.1 fusion.48
  55.5 0.1 add_select_fusion.2
  55.6 3.2 %collective-permute-start.4 = (f32[8,2176]{1,0:T(8,128)S(1)}, f32[8,2176]{1,0:T(8,128)S(1)}, u32[]{:S(2)}, u32[]{:S(2)}) collective-permute-start(f32[8,2176]{1,0:T(8,128)S(1)} %add_select_fusion.2), channel_id=1, source_target_pairs={{0,64},{16,80},{32,96},{48,112},{64,0},{80,16},{96,32},{112,48},{1... | collective-permute-start | bytes 208904 | tf_op jit(solution)/shard_map/ppermute | solution.py:47
  58.8 4.0 %collective-permute-done.4 = f32[8,2176]{1,0:T(8,128)S(1)} collective-permute-done((f32[8,2176]{1,0:T(8,128)S(1)}, f32[8,2176]{1,0:T(8,128)S(1)}, u32[]{:S(2)}, u32[]{:S(2)}) %collective-permute-start.4) | collective-permute-done | bytes 69664 | tf_op jit(solution)/shard_map/ppermute | solution.py:47
  62.8 0.1 fusion.49
  63.0 0.1 add_select_fusion.1
  63.1 2.8 %collective-permute-start.5 = (f32[8,2176]{1,0:T(8,128)S(1)}, f32[8,2176]{1,0:T(8,128)S(1)}, u32[]{:S(2)}, u32[]{:S(2)}) collective-permute-start(f32[8,2176]{1,0:T(8,128)S(1)} %add_select_fusion.1), channel_id=1, source_target_pairs={{0,128},{16,144},{32,160},{48,176},{64,192},{80,208},{96,224},{112... | collective-permute-start | bytes 208904 | tf_op jit(solution)/shard_map/ppermute | solution.py:47
  65.9 1.9 %collective-permute-done.5 = f32[8,2176]{1,0:T(8,128)S(1)} collective-permute-done((f32[8,2176]{1,0:T(8,128)S(1)}, f32[8,2176]{1,0:T(8,128)S(1)}, u32[]{:S(2)}, u32[]{:S(2)}) %collective-permute-start.5) | collective-permute-done | bytes 69664 | tf_op jit(solution)/shard_map/ppermute | solution.py:47
  67.8 0.1 fusion.50
  67.9 0.1 add_select_fusion
  68.0 0.2 slice_reduce_fusion
  68.2 3.0 %fusion = f32[8,2048]{1,0:T(8,128)S(1)} fusion(bf16[1,512,2048]{2,1,0:T(8,128)(2,1)} %param.9, bf16[1,2048,512]{2,1,0:T(8,128)(2,1)} %param.8, f32[8,2176]{1,0:T(8,128)S(1)} %add_select_fusion, f32[8]{0:T(128)S(1)} %slice_reduce_fusion), kind=kOutput, calls=%fused_computation.1 | convolution fusion | flops 33624064 | bytes 4325888 | tf_op jit(solution)/shard_map/dot_general | solution.py:117
  71.2 1.3 %collective-permute-start.6 = (f32[8,2048]{1,0:T(8,128)S(1)}, f32[8,2048]{1,0:T(8,128)S(1)}, u32[]{:S(2)}, u32[]{:S(2)}) collective-permute-start(f32[8,2048]{1,0:T(8,128)S(1)} %fusion), channel_id=1, source_target_pairs={{0,16},{16,0},{32,48},{48,32},{64,80},{80,64},{96,112},{112,96},{1... | collective-permute-start | bytes 196616 | tf_op jit(solution)/shard_map/ppermute | solution.py:30
  72.5 1.8 %collective-permute-done.6 = f32[8,2048]{1,0:T(8,128)S(1)} collective-permute-done((f32[8,2048]{1,0:T(8,128)S(1)}, f32[8,2048]{1,0:T(8,128)S(1)}, u32[]{:S(2)}, u32[]{:S(2)}) %collective-permute-start.6) | collective-permute-done | bytes 65568 | tf_op jit(solution)/shard_map/ppermute | solution.py:30
  74.4 2.9 %collective-permute-start.7 = (f32[8,2048]{1,0:T(8,128)S(1)}, f32[8,2048]{1,0:T(8,128)S(1)}, u32[]{:S(2)}, u32[]{:S(2)}) collective-permute-start(f32[8,2048]{1,0:T(8,128)S(1)} %add.44), channel_id=1, source_target_pairs={{0,32},{16,48},{32,0},{48,16},{64,96},{80,112},{96,64},{112,80},{1... | collective-permute-start | bytes 196616 | tf_op jit(solution)/shard_map/ppermute | solution.py:30
  77.3 1.7 %collective-permute-done.7 = f32[8,2048]{1,0:T(8,128)S(1)} collective-permute-done((f32[8,2048]{1,0:T(8,128)S(1)}, f32[8,2048]{1,0:T(8,128)S(1)}, u32[]{:S(2)}, u32[]{:S(2)}) %collective-permute-start.7) | collective-permute-done | bytes 65568 | tf_op jit(solution)/shard_map/ppermute | solution.py:30
  79.0 2.7 %collective-permute-start.8 = (f32[8,2048]{1,0:T(8,128)S(1)}, f32[8,2048]{1,0:T(8,128)S(1)}, u32[]{:S(2)}, u32[]{:S(2)}) collective-permute-start(f32[8,2048]{1,0:T(8,128)S(1)} %add.45), channel_id=1, source_target_pairs={{0,64},{16,80},{32,96},{48,112},{64,0},{80,16},{96,32},{112,48},{1... | collective-permute-start | bytes 196616 | tf_op jit(solution)/shard_map/ppermute | solution.py:30
  81.7 4.6 %collective-permute-done.8 = f32[8,2048]{1,0:T(8,128)S(1)} collective-permute-done((f32[8,2048]{1,0:T(8,128)S(1)}, f32[8,2048]{1,0:T(8,128)S(1)}, u32[]{:S(2)}, u32[]{:S(2)}) %collective-permute-start.8) | collective-permute-done | bytes 65568 | tf_op jit(solution)/shard_map/ppermute | solution.py:30
  86.3 2.7 %collective-permute-start.9 = (f32[8,2048]{1,0:T(8,128)S(1)}, f32[8,2048]{1,0:T(8,128)S(1)}, u32[]{:S(2)}, u32[]{:S(2)}) collective-permute-start(f32[8,2048]{1,0:T(8,128)S(1)} %add.46), channel_id=1, source_target_pairs={{0,128},{16,144},{32,160},{48,176},{64,192},{80,208},{96,224},{112... | collective-permute-start | bytes 196616 | tf_op jit(solution)/shard_map/ppermute | solution.py:30
  89.0 1.4 %divide_convert_fusion = bf16[1024,128]{1,0:T(8,128)(2,1)S(1)} fusion(f32[1024,128]{1,0:T(8,128)} %copy-done.2, f32[1024]{0:T(1024)S(1)} %get-tuple-element.6, f32[1024]{0:T(1024)S(1)} %get-tuple-element.8), kind=kLoop, calls=%fused_computation.14 | loop fusion | flops 393216 | bytes 794624 | tf_op jit(solution)/shard_map/convert_element_type | solution.py:121
  90.4 0.9 copy.17
  91.3 29.0 %all_gather.3.slots_ref = bf16[128,2048]{1,0:T(8,128)(2,1)} all-gather(bf16[8,2048]{1,0:T(8,128)(2,1)S(1)} %add_convert_fusion), channel_id=1, replica_groups=mesh['pos'=16,'exp'=16] {'exp'}, dimensions={0}, use_global_device_ids=true | all-gather | bytes 557056 | tf_op jit(solution)/shard_map/all_gather | solution.py:122
  120.3 3.8 %shard_map.55 = bf16[256,4,2048]{2,1,0:T(4,128)(2,1)} custom-call(bf16[1024,128]{1,0:T(8,128)(2,1)} %bitcast.44, bf16[128,2048]{1,0:T(8,128)(2,1)} %all_gather.3.slots_ref), custom_call_target="tpu_custom_call" | custom-call | flops 536870912 | bytes 4980736 | tf_op jit(solution)/shard_map/pallas_call | solution.py:61
  (23 shorter events, 0.4 us)
Async XLA Ops:
  0.0 9.5 %copy-start = (bf16[3,256,2048]{2,1,0:T(8,128)(2,1)S(1)}, bf16[3,256,2048]{2,1,0:T(8,128)(2,1)}, u32[]{:S(2)}) copy-start(bf16[3,256,2048]{2,1,0:T(8,128)(2,1)} %param.6) | copy-start | bytes 9437188
  1.3 0.8 copy-start.3
  2.1 3.9 %collective-permute-start = (bf16[4,1,256]{2,1,0:T(2,128)(2,1)S(1)}, bf16[4,1,256]{2,1,0:T(2,128)(2,1)S(1)}, u32[]{:S(2)}, u32[]{:S(2)}) collective-permute-start(bf16[4,1,256]{2,1,0:T(2,128)(2,1)S(1)} %get-tuple-element.24), channel_id=1, source_target_pairs={{0,1},{1,2},{2,3},{3,4},{4,5},{5,6},{6,7},{7,8},{8,9},{9,10},{10,1... | collective-permute-start | bytes 6152 | tf_op jit(solution)/shard_map/ppermute | solution.py:19
  4.7 3.0 %collective-permute-start.1 = (bf16[4,1,256]{2,1,0:T(2,128)(2,1)S(1)}, bf16[4,1,256]{2,1,0:T(2,128)(2,1)S(1)}, u32[]{:S(2)}, u32[]{:S(2)}) collective-permute-start(bf16[4,1,256]{2,1,0:T(2,128)(2,1)S(1)} %get-tuple-element.25), channel_id=1, source_target_pairs={{1,0},{2,1},{3,2},{4,3},{5,4},{6,5},{7,6},{8,7},{9,8},{10,9},{11,1... | collective-permute-start | bytes 6152 | tf_op jit(solution)/shard_map/ppermute | solution.py:20
  9.5 3.7 %copy-start.4 = (bf16[2048,128]{1,0:T(8,128)(2,1)S(1)}, bf16[2048,128]{1,0:T(8,128)(2,1)}, u32[]{:S(2)}) copy-start(bf16[2048,128]{1,0:T(8,128)(2,1)} %param.7) | copy-start | bytes 1572868
  14.5 0.8 copy-start.2
  42.4 1.0 copy-start.1
  45.6 3.2 %collective-permute-start.2 = (f32[8,2176]{1,0:T(8,128)S(1)}, f32[8,2176]{1,0:T(8,128)S(1)}, u32[]{:S(2)}, u32[]{:S(2)}) collective-permute-start(f32[8,2176]{1,0:T(8,128)S(1)} %pad_maximum_fusion.2), channel_id=1, source_target_pairs={{0,16},{16,0},{32,48},{48,32},{64,80},{80,64},{96,112},{112,96},{1... | collective-permute-start | bytes 208904 | tf_op jit(solution)/shard_map/ppermute | solution.py:47
  49.1 6.3 %collective-permute-start.3 = (f32[8,2176]{1,0:T(8,128)S(1)}, f32[8,2176]{1,0:T(8,128)S(1)}, u32[]{:S(2)}, u32[]{:S(2)}) collective-permute-start(f32[8,2176]{1,0:T(8,128)S(1)} %add_select_fusion.3), channel_id=1, source_target_pairs={{0,32},{16,48},{32,0},{48,16},{64,96},{80,112},{96,64},{112,80},{1... | collective-permute-start | bytes 208904 | tf_op jit(solution)/shard_map/ppermute | solution.py:47
  55.6 7.2 %collective-permute-start.4 = (f32[8,2176]{1,0:T(8,128)S(1)}, f32[8,2176]{1,0:T(8,128)S(1)}, u32[]{:S(2)}, u32[]{:S(2)}) collective-permute-start(f32[8,2176]{1,0:T(8,128)S(1)} %add_select_fusion.2), channel_id=1, source_target_pairs={{0,64},{16,80},{32,96},{48,112},{64,0},{80,16},{96,32},{112,48},{1... | collective-permute-start | bytes 208904 | tf_op jit(solution)/shard_map/ppermute | solution.py:47
  63.1 4.8 %collective-permute-start.5 = (f32[8,2176]{1,0:T(8,128)S(1)}, f32[8,2176]{1,0:T(8,128)S(1)}, u32[]{:S(2)}, u32[]{:S(2)}) collective-permute-start(f32[8,2176]{1,0:T(8,128)S(1)} %add_select_fusion.1), channel_id=1, source_target_pairs={{0,128},{16,144},{32,160},{48,176},{64,192},{80,208},{96,224},{112... | collective-permute-start | bytes 208904 | tf_op jit(solution)/shard_map/ppermute | solution.py:47
  71.2 3.1 %collective-permute-start.6 = (f32[8,2048]{1,0:T(8,128)S(1)}, f32[8,2048]{1,0:T(8,128)S(1)}, u32[]{:S(2)}, u32[]{:S(2)}) collective-permute-start(f32[8,2048]{1,0:T(8,128)S(1)} %fusion), channel_id=1, source_target_pairs={{0,16},{16,0},{32,48},{48,32},{64,80},{80,64},{96,112},{112,96},{1... | collective-permute-start | bytes 196616 | tf_op jit(solution)/shard_map/ppermute | solution.py:30
  74.4 4.6 %collective-permute-start.7 = (f32[8,2048]{1,0:T(8,128)S(1)}, f32[8,2048]{1,0:T(8,128)S(1)}, u32[]{:S(2)}, u32[]{:S(2)}) collective-permute-start(f32[8,2048]{1,0:T(8,128)S(1)} %add.44), channel_id=1, source_target_pairs={{0,32},{16,48},{32,0},{48,16},{64,96},{80,112},{96,64},{112,80},{1... | collective-permute-start | bytes 196616 | tf_op jit(solution)/shard_map/ppermute | solution.py:30
  79.0 7.3 %collective-permute-start.8 = (f32[8,2048]{1,0:T(8,128)S(1)}, f32[8,2048]{1,0:T(8,128)S(1)}, u32[]{:S(2)}, u32[]{:S(2)}) collective-permute-start(f32[8,2048]{1,0:T(8,128)S(1)} %add.45), channel_id=1, source_target_pairs={{0,64},{16,80},{32,96},{48,112},{64,0},{80,16},{96,32},{112,48},{1... | collective-permute-start | bytes 196616 | tf_op jit(solution)/shard_map/ppermute | solution.py:30
  86.3 5.0 %collective-permute-start.9 = (f32[8,2048]{1,0:T(8,128)S(1)}, f32[8,2048]{1,0:T(8,128)S(1)}, u32[]{:S(2)}, u32[]{:S(2)}) collective-permute-start(f32[8,2048]{1,0:T(8,128)S(1)} %add.46), channel_id=1, source_target_pairs={{0,128},{16,144},{32,160},{48,176},{64,192},{80,208},{96,224},{112... | collective-permute-start | bytes 196616 | tf_op jit(solution)/shard_map/ppermute | solution.py:30
